TPU v7x, 128 devices: a whole 4x4x4 slice. The times are simulated.
128 devices in a mesh: seq: 32 (over x, y, core), dp: 4 (over z).
Axes of the slice: x: 4, y: 4, z: 4, core: 2. Of those that a mesh axis runs over, the one named last changes fastest.
Arguments:
- inputs: bfloat16 [8, 8192, 1024], P('dp', 'seq'), may hold values from -6 to 6
- lengths: int32 [8, 64], P('dp'), may hold values from 1 to 256, 8192 in all within a row
- norm_gain: float32 [1024], replicated, may hold values from 0.5 to 1.5
- qkv_weight: bfloat16 [1024, 3072], replicated, may hold values from -4 to 4
- out_weight: bfloat16 [1024, 1024], replicated, may hold values from -0.75 to 0.75
- kernel: float32 [31, 1024], replicated, may hold values from -1 to 1
- cotangent: bfloat16 [8, 8192, 1024], P('dp', 'seq'), may hold values from -6 to 6
Outputs:
- output: bfloat16 [8, 8192, 1024], P('dp', 'seq')
- grad_inputs: bfloat16 [8, 8192, 1024], P('dp', 'seq')
- grad_qkv_weight: float32 [1024, 3072], P(('seq', 'dp'))
- grad_out_weight: float32 [1024, 1024], P(('seq', 'dp'))
- grad_kernel: float32 [31, 1024], replicated
- grad_gain: float32 [1024], replicated
Inputs may be any that keep to these rules, and one draw needn't show every extreme that they name: `lengths`: each row sums to 8192.
All inputs are finite; a program needn't handle non-finite values.
Results may differ from a plain program's by a relative error of at most 0.017.
Values may be sent and summed in bfloat16 or wider, within the bound.
No kernel may reach another device: no remote copies, remote signals or barrier semaphores. Data moves between devices by JAX's collectives and lax.ppermute only.
A program may use at most 192 MiB of HBM per device.

v0:
```python
import jax
import jax.numpy as jnp
from jax import lax
from jax.sharding import PartitionSpec as P

HEADS = 16
MOST = 256


EPSILON = 1e-05
NEGATIVE = -1e30


def with_halo(shard, sides, width):
    for axis, dim in sides:
        size, length = (lax.axis_size(axis), shard.shape[dim])
        up = [(i, (i + 1) % size) for i in range(size - 1)]
        down = [(j, i) for i, j in up]
        last = lax.slice_in_dim(shard, length - width, length, axis=dim)
        initial = lax.slice_in_dim(shard, 0, width, axis=dim)
        before = lax.ppermute(last, axis, up)
        after = lax.ppermute(initial, axis, down)
        shard = jnp.concatenate([before, shard, after], axis=dim)
    return shard


def segment_ids(positions, length_row, seq_length):
    ends = jnp.cumsum(length_row)
    inside = (positions >= 0) & (positions < seq_length)
    counted = jnp.sum((ends[None, :] <= positions[:, None]).astype(jnp.int32), axis=1)
    return jnp.where(inside, counted, -1)


def block_probs(queries, key_rows, allowed, score_scale):
    scores = (
        jnp.einsum("hqd,hkd->hqk", queries, key_rows, preferred_element_type=jnp.float32)
        * score_scale
    )
    scores = jnp.where(allowed[None], scores, NEGATIVE)
    row_max = jnp.max(scores, axis=-1, keepdims=True)
    exponent = jnp.where(allowed[None], jnp.exp(scores - row_max), 0.0)
    return exponent / jnp.sum(exponent, axis=-1, keepdims=True)


def block_forward(queries, key_rows, values, allowed, score_scale):
    attn_probs = block_probs(queries, key_rows, allowed, score_scale)
    return jnp.einsum(
        "hqk,hkd->hqd", attn_probs.astype(jnp.bfloat16), values, preferred_element_type=jnp.float32
    ).astype(jnp.bfloat16)


def block_backward(queries, key_rows, values, allowed, score_scale, output, grad_output):
    attn_probs = block_probs(queries, key_rows, allowed, score_scale)
    row_delta = jnp.sum(
        grad_output.astype(jnp.float32) * output.astype(jnp.float32), axis=-1, keepdims=True
    )
    value_part = jnp.einsum(
        "hqk,hqd->hkd",
        attn_probs.astype(jnp.bfloat16),
        grad_output,
        preferred_element_type=jnp.float32,
    )
    grad_probs = jnp.einsum("hqd,hkd->hqk", grad_output, values, preferred_element_type=jnp.float32)
    grad_scores = (attn_probs * (grad_probs - row_delta) * score_scale).astype(jnp.bfloat16)
    grad_query = jnp.einsum(
        "hqk,hkd->hqd", grad_scores, key_rows, preferred_element_type=jnp.float32
    ).astype(jnp.bfloat16)
    key_part = jnp.einsum("hqk,hqd->hkd", grad_scores, queries, preferred_element_type=jnp.float32)
    return (grad_query, key_part, value_part)


def windowed_forward(queries, key_rows, values, segment_all, segment_pad, score_scale):
    pair_count, seq_length, head_dim = queries.shape
    block_rows = min(512, seq_length)
    window = block_rows + 2 * MOST
    pad_keys = jnp.pad(key_rows, ((0, 0), (MOST, MOST), (0, 0)))
    pad_values = jnp.pad(values, ((0, 0), (MOST, MOST), (0, 0)))

    def one_block(step_index):
        offset = step_index * block_rows
        allowed = (
            lax.dynamic_slice_in_dim(segment_all, offset, block_rows, 0)[:, None]
            == lax.dynamic_slice_in_dim(segment_pad, offset, window, 0)[None, :]
        )
        return block_forward(
            lax.dynamic_slice_in_dim(queries, offset, block_rows, 1),
            lax.dynamic_slice_in_dim(pad_keys, offset, window, 1),
            lax.dynamic_slice_in_dim(pad_values, offset, window, 1),
            allowed,
            score_scale,
        )

    block_outs = lax.map(one_block, jnp.arange(seq_length // block_rows, dtype=jnp.int32))
    return block_outs.transpose(1, 0, 2, 3).reshape(pair_count, seq_length, head_dim)


def windowed_backward(
    queries, key_rows, values, segment_all, segment_pad, score_scale, output, grad_output
):
    pair_count, seq_length, head_dim = queries.shape
    block_rows = min(512, seq_length)
    window = block_rows + 2 * MOST
    pad_keys = jnp.pad(key_rows, ((0, 0), (MOST, MOST), (0, 0)))
    pad_values = jnp.pad(values, ((0, 0), (MOST, MOST), (0, 0)))

    def one_block(carried, step_index):
        key_grads, value_grads = carried
        offset = step_index * block_rows
        allowed = (
            lax.dynamic_slice_in_dim(segment_all, offset, block_rows, 0)[:, None]
            == lax.dynamic_slice_in_dim(segment_pad, offset, window, 0)[None, :]
        )
        grad_query, key_part, value_part = block_backward(
            lax.dynamic_slice_in_dim(queries, offset, block_rows, 1),
            lax.dynamic_slice_in_dim(pad_keys, offset, window, 1),
            lax.dynamic_slice_in_dim(pad_values, offset, window, 1),
            allowed,
            score_scale,
            lax.dynamic_slice_in_dim(output, offset, block_rows, 1),
            lax.dynamic_slice_in_dim(grad_output, offset, block_rows, 1),
        )
        key_grads = lax.dynamic_update_slice_in_dim(
            key_grads, lax.dynamic_slice_in_dim(key_grads, offset, window, 1) + key_part, offset, 1
        )
        value_grads = lax.dynamic_update_slice_in_dim(
            value_grads,
            lax.dynamic_slice_in_dim(value_grads, offset, window, 1) + value_part,
            offset,
            1,
        )
        return ((key_grads, value_grads), grad_query)

    empty_grads = jnp.zeros((pair_count, seq_length + 2 * MOST, head_dim), jnp.float32)
    (key_grads, value_grads), query_grads = lax.scan(
        one_block, (empty_grads, empty_grads), jnp.arange(seq_length // block_rows, dtype=jnp.int32)
    )
    query_grads = query_grads.transpose(1, 0, 2, 3).reshape(pair_count, seq_length, head_dim)
    return (
        query_grads,
        key_grads[:, MOST : MOST + seq_length].astype(jnp.bfloat16),
        value_grads[:, MOST : MOST + seq_length].astype(jnp.bfloat16),
    )


def local(inputs, lengths, norm_gain, qkv_weight, out_weight, kernel, cotangent):
    batches, frames, model_width = inputs.shape
    shards = lax.axis_size("seq")
    position = lax.axis_index("seq")
    seq_length = frames * shards
    head_dim = model_width // HEADS
    score_scale = head_dim ** (-0.5)
    conv_reach = kernel.shape[0] // 2
    factor = (batches * seq_length * lax.axis_size("dp")) ** (-0.5)
    first_frame = position * frames
    local_pos = first_frame + jnp.arange(frames, dtype=jnp.int32)
    segment_local = jnp.stack(
        [segment_ids(local_pos, lengths[batch_index], seq_length) for batch_index in range(batches)]
    )
    widened = inputs.astype(jnp.float32)
    average = jnp.mean(widened, axis=-1, keepdims=True)
    centred = widened - average
    inverse = lax.rsqrt(jnp.mean(centred * centred, axis=-1, keepdims=True) + EPSILON)
    unit_rows = centred * inverse
    normed = (unit_rows * norm_gain).astype(jnp.bfloat16)
    flat_normed = normed.reshape(-1, model_width)
    projected = jnp.dot(flat_normed, qkv_weight, preferred_element_type=jnp.float32).astype(
        jnp.bfloat16
    )
    projected = projected.reshape(batches, frames, 3 * model_width)
    pair_count = batches * HEADS // shards
    packed = projected.reshape(batches, frames, 3, HEADS, head_dim).transpose(0, 3, 1, 2, 4)
    packed = packed.reshape(batches * HEADS, frames // 2, 6 * head_dim)
    gathered = lax.all_to_all(packed, "seq", split_axis=0, concat_axis=1, tiled=True).reshape(
        pair_count, seq_length, 3, head_dim
    )
    head_queries = gathered[:, :, 0]
    head_keys = gathered[:, :, 1]
    head_values = gathered[:, :, 2]
    local_batch = position * pair_count // HEADS
    length_row = lax.dynamic_index_in_dim(lengths, local_batch, 0, keepdims=False)
    segment_all = segment_ids(jnp.arange(seq_length, dtype=jnp.int32), length_row, seq_length)
    segment_pad = segment_ids(
        jnp.arange(-MOST, seq_length + MOST, dtype=jnp.int32), length_row, seq_length
    )
    head_out = windowed_forward(
        head_queries, head_keys, head_values, segment_all, segment_pad, score_scale
    )
    returned = lax.all_to_all(
        head_out.reshape(pair_count, seq_length // 2, 2 * head_dim),
        "seq",
        split_axis=1,
        concat_axis=0,
        tiled=True,
    )
    attended = returned.reshape(batches, HEADS, frames, head_dim).transpose(0, 2, 1, 3)
    attended = attended.reshape(batches, frames, model_width)
    flat_attended = attended.reshape(-1, model_width)
    attn_rows = jnp.dot(flat_attended, out_weight, preferred_element_type=jnp.float32)
    hidden = (widened + attn_rows.reshape(batches, frames, model_width)).astype(jnp.bfloat16)
    padded = with_halo(hidden, (("seq", 1),), conv_reach).astype(jnp.float32)
    ext_pos = first_frame - conv_reach + jnp.arange(frames + 2 * conv_reach, dtype=jnp.int32)
    segment_ext = jnp.stack(
        [segment_ids(ext_pos, lengths[batch_index], seq_length) for batch_index in range(batches)]
    )
    conv_sum = jnp.zeros((batches, frames, model_width), jnp.float32)
    for tap_index in range(kernel.shape[0]):
        same_seg = (segment_ext[:, tap_index : tap_index + frames] == segment_local)[..., None]
        conv_sum = conv_sum + jnp.where(
            same_seg, kernel[tap_index] * padded[:, tap_index : tap_index + frames], 0.0
        )
    gated = jax.nn.sigmoid(conv_sum)
    output = (hidden.astype(jnp.float32) + conv_sum * gated).astype(jnp.bfloat16)
    incoming = cotangent.astype(jnp.float32)
    grad_conv = incoming * gated * (1.0 + conv_sum * (1.0 - gated))
    grad_pad = with_halo(grad_conv.astype(jnp.bfloat16), (("seq", 1),), conv_reach).astype(
        grad_conv.dtype
    )
    grad_hidden = incoming
    kernel_rows = []
    for tap_index in range(kernel.shape[0]):
        back_index = 2 * conv_reach - tap_index
        same_back = (segment_ext[:, back_index : back_index + frames] == segment_local)[..., None]
        grad_hidden = grad_hidden + jnp.where(
            same_back, kernel[tap_index] * grad_pad[:, back_index : back_index + frames], 0.0
        )
        same_seg = (segment_ext[:, tap_index : tap_index + frames] == segment_local)[..., None]
        kernel_rows.append(
            jnp.sum(
                jnp.where(same_seg, grad_conv * padded[:, tap_index : tap_index + frames], 0.0),
                axis=(0, 1),
            )
        )
    grad_hidden_b = grad_hidden.astype(jnp.bfloat16)
    flat_grad_hidden = grad_hidden_b.reshape(-1, model_width)
    grad_attended = jnp.dot(
        flat_grad_hidden, out_weight.T, preferred_element_type=jnp.float32
    ).astype(jnp.bfloat16)
    grad_packed = grad_attended.reshape(batches, frames, HEADS, head_dim).transpose(0, 2, 1, 3)
    grad_packed = grad_packed.reshape(batches * HEADS, frames // 2, 2 * head_dim)
    grad_heads = lax.all_to_all(
        grad_packed, "seq", split_axis=0, concat_axis=1, tiled=True
    ).reshape(pair_count, seq_length, head_dim)
    query_grads, key_grads, value_grads = windowed_backward(
        head_queries,
        head_keys,
        head_values,
        segment_all,
        segment_pad,
        score_scale,
        head_out,
        grad_heads,
    )
    stacked = jnp.stack([query_grads, key_grads, value_grads], axis=2).reshape(
        pair_count, seq_length // 2, 6 * head_dim
    )
    sent_back = lax.all_to_all(stacked, "seq", split_axis=1, concat_axis=0, tiled=True)
    grad_qkv = sent_back.reshape(batches, HEADS, frames, 3, head_dim).transpose(0, 2, 3, 1, 4)
    grad_qkv = grad_qkv.reshape(batches, frames, 3 * model_width)
    flat_grad_qkv = grad_qkv.reshape(-1, 3 * model_width)
    grad_normed = jnp.dot(flat_grad_qkv, qkv_weight.T, preferred_element_type=jnp.float32)
    grad_normed = grad_normed.reshape(batches, frames, model_width)
    scaled = grad_normed * norm_gain
    grad_inputs = grad_hidden + inverse * (
        scaled
        - jnp.mean(scaled, axis=-1, keepdims=True)
        - unit_rows * jnp.mean(scaled * unit_rows, axis=-1, keepdims=True)
    )
    gain_sum = jnp.sum(grad_normed * unit_rows, axis=(0, 1))
    contract_rows = (((0,), (0,)), ((), ()))
    summed = lax.psum_scatter(
        jnp.concatenate(
            [
                lax.dot_general(
                    flat_normed, flat_grad_qkv, contract_rows, preferred_element_type=jnp.float32
                ),
                lax.dot_general(
                    flat_attended,
                    flat_grad_hidden,
                    contract_rows,
                    preferred_element_type=jnp.float32,
                ),
            ],
            axis=1,
        ),
        ("seq", "dp"),
        scatter_dimension=0,
        tiled=True,
    )
    small_sums = lax.psum((jnp.stack(kernel_rows), gain_sum), ("seq", "dp"))
    return (
        output,
        grad_inputs.astype(jnp.bfloat16),
        summed[:, : 3 * model_width] * factor,
        summed[:, 3 * model_width :] * factor,
        small_sums[0] * factor,
        small_sums[1] * factor,
    )


def solution(mesh):
    in_specs = (P("dp", "seq", None), P("dp", None), P(), P(), P(), P(), P("dp", "seq", None))
    out_specs = (
        P("dp", "seq", None),
        P("dp", "seq", None),
        P(("seq", "dp"), None),
        P(("seq", "dp"), None),
        P(),
        P(),
    )
    return jax.shard_map(local, mesh=mesh, in_specs=in_specs, out_specs=out_specs, check_vma=False)
```

profile of v0, /device:TPU:0, one launch (start us, length us, event | category | flops | bytes accessed | tf_op | source)
XLA Modules:
  0.0 1635.9 jit_solution(17612072159544728397)
XLA Ops:
  12.0 7.6 convolution_convert_fusion.2
  19.6 4.7 copy.93
  24.3 5.5 reshape_reshape.9
  29.8 21.3 %copy.94 = bf16[2,16,256,3,64]{4,3,2,1,0:T(4,128)(2,1)} copy(bf16[2,16,256,3,64]{2,0,4,1,3:T(2,128)(2,1)} %bitcast.236) | data formatting | bytes 6291456 | tf_op jit(solution)/shard_map/transpose | solution.py:171
  51.1 15.4 reshape.390
  66.4 8.2 all-to-all-start
  77.3 37.5 %all-to-all-done = bf16[32,128,384]{2,1,0:T(8,128)(2,1)} async-done(((bf16[32,128,384]{2,1,0:T(8,128)(2,1)}), bf16[32,128,384]{2,1,0:T(8,128)(2,1)}, u32[]{:S(2)}, u32[]{:S(2)}) %all-to-all-start) | async-done | bytes 3145760 | tf_op jit(solution)/shard_map/all_to_all | solution.py:173
  114.8 16.0 reshape.391
  130.9 20.1 %fusion.197 = (bf16[1,8192,1,64]{3,2,1,0:T(2,128)(2,1)}, bf16[1,8192,1,64]{3,2,1,0:T(2,128)(2,1)}, bf16[1,8192,1,64]{3,2,1,0:T(2,128)(2,1)}) fusion(bf16[1,8192,3,64]{3,2,1,0:T(4,128)(2,1)} %reshape.391), kind=kLoop, calls=%fused_computation.373 | loop fusion | bytes 6291456 | tf_op jit(solution)/shard_map/slice | solution.py:178
  151.0 8.9 copy.97
  162.6 8.9 copy.96
  174.2 8.9 copy.95
  183.0 2.8 copy.98
  185.8 3.0 pad.10.clone
  191.6 98.0 %while.24 = (s32[]{:T(128)}, bf16[16,1,512,64]{2,3,1,0:T(8,128)(2,1)}, s32[16]{0:T(128)S(1)}, s32[8192]{0:T(1024)S(1)}, s32[8704]{0:T(1024)S(1)}, /*index=5*/bf1...) while((s32[]{:T(128)}, ...), condition=%wide.region_8.9_spmd, body=%wide.region_5.8_spmd.sunk | while | flops 143162368 | bytes 7053552 | solution.py:93
  292.4 8.0 reshape_reshape_transpose.4
  301.0 24.6 %reduce.16 = bf16[4096,128]{1,0:T(8,128)(2,1)} reduce(bf16[4096,1,128]{2,1,0:T(2,128)(2,1)} %bitcast.239, bf16[]{:T(256)} %broadcast.278), dimensions={1}, to_apply=%bitcast.167.reduce_sub_computation | reduce | bytes 2097154
  327.7 4.9 all-to-all-start.1
  336.8 12.6 all-to-all-done.1
  349.4 5.8 reshape.412
  355.2 19.5 %bitcast_reduce_fusion.1 = bf16[4096,128]{1,0:T(8,128)(2,1)} fusion(bf16[4096,1,128]{2,1,0:T(2,128)(2,1)} %reshape.412), kind=kLoop, calls=%fused_computation.379 | loop fusion | bytes 2097152 | tf_op jit(solution)/shard_map/all_to_all | solution.py:188
  374.7 3.8 reshape.392
  390.4 21.8 %select_reduce_fusion = (f32[1024]{0:T(1024)}, f32[1024]{0:T(1024)}, f32[1024]{0:T(1024)}, f32[1024]{0:T(1024)}, f32[1024]{0:T(1024)}, /*index=5*/f32[1024]{0:T(...) fusion(f32[2,286,1024]{2,1,0:T(8,128)S(1)} %maximum_convert_fus, ...), kind=kLoop, calls=%fused_computation.180 | loop fusion | flops 67099648 | bytes 70434304 | tf_op jit(solution)/shard_map/reduce_sum | solution.py:228
  412.2 4.5 select_reduce_fusion.9
  416.8 4.7 collective-permute-start.2
  425.1 12.5 fusion.195
  443.8 12.9 all-to-all-start.2
  456.7 16.8 %all-to-all-done.2 = bf16[32,128,128]{2,1,0:T(8,128)(2,1)S(1)} async-done(((bf16[32,128,128]{2,1,0:T(8,128)(2,1)}), bf16[32,128,128]{2,1,0:T(8,128)(2,1)S(1)}, u32[]{:S(2)}, u32[]{:S(2)}) %all-to-all-start.2) | async-done | bytes 1048608 | tf_op jit(solution)/shard_map/all_to_all | solution.py:240
  477.2 192.3 %while.25 = (s32[]{:T(128)}, f32[1,8704,64]{1,2,0:T(8,128)S(1)}, f32[1,8704,64]{1,2,0:T(8,128)}, bf16[16,1,512,64]{2,3,1,0:T(8,128)(2,1)S(1)}, s32[16]{0:T(128)S...) while((s32[]{:T(128)}, f32[1,8704,64]{1,2,0:T(8,128)S(1)}, ...), condition=%wide.region_19.20_spmd, body=%wide.region_15.19_spmd.sunk | while | flops 349993472 | bytes 14145836 | solution.py:134
  675.6 8.4 copy.114
  684.0 27.3 %reshape.405 = bf16[1,4096,384]{2,0,1:T(2,128)(2,1)} reshape(bf16[1,8192,3,64]{3,2,1,0:T(4,128)(2,1)} %copy.114) | data formatting | bytes 6291456 | tf_op jit(solution)/shard_map/reshape | solution.py:253
  711.3 67.1 %reduce.17 = bf16[4096,384]{1,0:T(8,128)(2,1)S(1)} reduce(bf16[4096,1,384]{2,1,0:T(2,128)(2,1)} %bitcast.233, bf16[]{:T(256)} %broadcast.278), dimensions={1}, to_apply=%bitcast.169.reduce_sub_computation | reduce | bytes 6291458
  780.9 4.8 all-to-all-start.3
  785.8 3.0 copy.119
  792.6 3.7 select_reduce_fusion.18
  799.3 4.5 fusion.203
  803.8 22.1 %all-to-all-done.3 = bf16[32,2,24576]{2,1,0:T(2,128)(2,1)} async-done(((bf16[32,2,24576]{2,1,0:T(2,128)(2,1)}), bf16[32,2,24576]{2,1,0:T(2,128)(2,1)}, u32[]{:S(2)}, u32[]{:S(2)}) %all-to-all-start.3) | async-done | bytes 3145760 | tf_op jit(solution)/shard_map/all_to_all | solution.py:256
  826.0 19.1 %reshape.414 = bf16[4096,1,384]{2,1,0:T(2,128)(2,1)} reshape(bf16[32,2,24576]{2,1,0:T(2,128)(2,1)} %all-to-all-done.3) | data formatting | bytes 6291456
  845.0 66.4 %bitcast_reduce_fusion = bf16[4096,384]{1,0:T(8,128)(2,1)S(1)} fusion(bf16[4096,1,384]{2,1,0:T(2,128)(2,1)} %reshape.414), kind=kLoop, calls=%fused_computation.378 | loop fusion | bytes 6291456 | tf_op jit(solution)/shard_map/all_to_all | solution.py:256
  911.4 9.2 reshape.402
  920.6 19.3 %copy.118 = bf16[2,256,3,16,64]{1,0,4,3,2:T(2,128)(2,1)S(1)} copy(bf16[2,256,3,16,64]{4,2,1,3,0:T(4,128)(2,1)} %bitcast.231) | data formatting | bytes 6291456 | tf_op jit(solution)/shard_map/transpose | solution.py:257
  941.1 3.5 fusion.202
  944.6 6.3 pad_maximum_fusion
  956.0 12.3 copy.116
  968.4 9.1 fusion.61
  977.5 66.8 %psum.15 = f32[1024]{0:T(1024)S(1)} all-reduce(f32[1024]{0:T(1024)S(1)} %get-tuple-element.207), channel_id=1, replica_groups=mesh['seq'=32,'dp'=4] {'seq','dp'}, use_global_device_ids=true, to_apply=%region_56.57 | all-reduce | flops 1024 | bytes 8192 | tf_op jit(solution)/shard_map/psum | solution.py:289
  1044.9 4.1 fusion.60
  1049.0 576.8 %reduce-scatter.2.cloned.1.call-done = f32[8,4096]{1,0:T(8,128)} async-done(((f32[1024,4096]{1,0:T(8,128)}), f32[8,4096]{1,0:T(8,128)}) %reduce-scatter.2.cloned.1.call-update) | async-done | bytes 131088 | tf_op jit(solution)/shard_map/reduce_scatter | solution.py:270
  (565 shorter events, 343.1 us)
Async XLA Ops:
  7.2 374.0 %copy-start = (bf16[1024,1024]{1,0:T(8,128)(2,1)S(1)}, bf16[1024,1024]{1,0:T(8,128)(2,1)}, u32[]{:S(2)}) copy-start(bf16[1024,1024]{1,0:T(8,128)(2,1)} %param.15) | copy-start | bytes 6291460
  66.4 8.2 copy-start.109
  66.4 48.4 %all-to-all-start = ((bf16[32,128,384]{2,1,0:T(8,128)(2,1)}), bf16[32,128,384]{2,1,0:T(8,128)(2,1)}, u32[]{:S(2)}, u32[]{:S(2)}) async-start(bf16[32,128,384]{2,1,0:T(8,128)(2,1)} %reshape.390), calls=%async_computation | async-start | bytes 6291456 | tf_op jit(solution)/shard_map/all_to_all | solution.py:173
  325.5 11.1 copy-start.19
  327.7 21.7 %all-to-all-start.1 = ((bf16[32,2,8192]{2,1,0:T(2,128)(2,1)}), bf16[32,2,8192]{2,1,0:T(2,128)(2,1)}, u32[]{:S(2)}, u32[]{:S(2)}) async-start(bf16[32,2,8192]{2,1,0:T(2,128)(2,1)} %reshape.411), calls=%async_computation.1 | async-start | bytes 2097152 | tf_op jit(solution)/shard_map/all_to_all | solution.py:188
  336.7 53.3 %copy-start.20 = (f32[1,1024]{1,0:T(1,128)}, f32[1,1024]{1,0:T(1,128)S(1)}, u32[]{:S(2)}) copy-start(f32[1,1024]{1,0:T(1,128)S(1)} %get-tuple-element.277) | copy-start | bytes 12292
  336.7 53.3 %copy-start.22 = (f32[1,1024]{1,0:T(1,128)}, f32[1,1024]{1,0:T(1,128)S(1)}, u32[]{:S(2)}) copy-start(f32[1,1024]{1,0:T(1,128)S(1)} %get-tuple-element.278) | copy-start | bytes 12292
  336.7 53.3 %copy-start.24 = (f32[1,1024]{1,0:T(1,128)}, f32[1,1024]{1,0:T(1,128)S(1)}, u32[]{:S(2)}) copy-start(f32[1,1024]{1,0:T(1,128)S(1)} %get-tuple-element.279) | copy-start | bytes 12292
  336.7 53.3 %copy-start.26 = (f32[1,1024]{1,0:T(1,128)}, f32[1,1024]{1,0:T(1,128)S(1)}, u32[]{:S(2)}) copy-start(f32[1,1024]{1,0:T(1,128)S(1)} %get-tuple-element.280) | copy-start | bytes 12292
  336.7 53.3 %copy-start.28 = (f32[1,1024]{1,0:T(1,128)}, f32[1,1024]{1,0:T(1,128)S(1)}, u32[]{:S(2)}) copy-start(f32[1,1024]{1,0:T(1,128)S(1)} %get-tuple-element.281) | copy-start | bytes 12292
  336.7 53.3 %copy-start.30 = (f32[1,1024]{1,0:T(1,128)}, f32[1,1024]{1,0:T(1,128)S(1)}, u32[]{:S(2)}) copy-start(f32[1,1024]{1,0:T(1,128)S(1)} %get-tuple-element.282) | copy-start | bytes 12292
  336.8 53.3 %copy-start.32 = (f32[1,1024]{1,0:T(1,128)}, f32[1,1024]{1,0:T(1,128)S(1)}, u32[]{:S(2)}) copy-start(f32[1,1024]{1,0:T(1,128)S(1)} %get-tuple-element.283) | copy-start | bytes 12292
  336.8 53.3 %copy-start.34 = (f32[1,1024]{1,0:T(1,128)}, f32[1,1024]{1,0:T(1,128)S(1)}, u32[]{:S(2)}) copy-start(f32[1,1024]{1,0:T(1,128)S(1)} %get-tuple-element.284) | copy-start | bytes 12292
  336.8 53.3 %copy-start.36 = (f32[1,1024]{1,0:T(1,128)}, f32[1,1024]{1,0:T(1,128)S(1)}, u32[]{:S(2)}) copy-start(f32[1,1024]{1,0:T(1,128)S(1)} %get-tuple-element.285) | copy-start | bytes 12292
  336.8 53.3 %copy-start.38 = (f32[1,1024]{1,0:T(1,128)}, f32[1,1024]{1,0:T(1,128)S(1)}, u32[]{:S(2)}) copy-start(f32[1,1024]{1,0:T(1,128)S(1)} %get-tuple-element.286) | copy-start | bytes 12292
  336.8 53.3 %copy-start.40 = (f32[1,1024]{1,0:T(1,128)}, f32[1,1024]{1,0:T(1,128)S(1)}, u32[]{:S(2)}) copy-start(f32[1,1024]{1,0:T(1,128)S(1)} %get-tuple-element.287) | copy-start | bytes 12292
  336.8 53.3 %copy-start.42 = (f32[1,1024]{1,0:T(1,128)}, f32[1,1024]{1,0:T(1,128)S(1)}, u32[]{:S(2)}) copy-start(f32[1,1024]{1,0:T(1,128)S(1)} %get-tuple-element.288) | copy-start | bytes 12292
  383.7 6.4 copy-start.12
  383.7 6.4 copy-start.57
  383.7 6.4 copy-start.59
  383.7 6.4 copy-start.61
  384.0 3.8 collective-permute-start
  386.4 3.1 collective-permute-start.1
  389.9 22.3 %copy-start.2 = (f32[2,286,1024]{2,1,0:T(8,128)}, f32[2,286,1024]{2,1,0:T(8,128)S(1)}, u32[]{:S(2)}) copy-start(f32[2,286,1024]{2,1,0:T(8,128)S(1)} %maximum_convert_fusion) | copy-start | bytes 7028740
  416.7 8.3 copy-start.21
  416.7 8.3 copy-start.23
  416.7 8.3 copy-start.25
  416.7 8.3 copy-start.27
  416.7 8.3 copy-start.29
  416.7 8.3 copy-start.31
  416.8 8.3 copy-start.33
  416.8 8.3 copy-start.35
  416.8 8.3 copy-start.37
  416.8 8.3 copy-start.39
  416.8 8.3 copy-start.41
  416.8 8.3 copy-start.43
  416.8 6.0 collective-permute-start.2
  421.5 3.1 collective-permute-start.3
  443.8 29.7 %all-to-all-start.2 = ((bf16[32,128,128]{2,1,0:T(8,128)(2,1)}), bf16[32,128,128]{2,1,0:T(8,128)(2,1)S(1)}, u32[]{:S(2)}, u32[]{:S(2)}) async-start(bf16[32,128,128]{2,1,0:T(8,128)(2,1)} %reshape.399), calls=%async_computation.2 | async-start | bytes 2097152 | tf_op jit(solution)/shard_map/all_to_all | solution.py:240
  780.9 45.0 %all-to-all-start.3 = ((bf16[32,2,24576]{2,1,0:T(2,128)(2,1)}), bf16[32,2,24576]{2,1,0:T(2,128)(2,1)}, u32[]{:S(2)}, u32[]{:S(2)}) async-start(bf16[32,2,24576]{2,1,0:T(2,128)(2,1)} %reshape.413), calls=%async_computation.3 | async-start | bytes 6291456 | tf_op jit(solution)/shard_map/all_to_all | solution.py:256
  785.8 168.7 %all-reduce.4.cloned.1.call-start = ((), (), s32[]{:S(2)}) async-start(), calls=%async_computation.6 | async-start | bytes 262144 | tf_op jit(solution)/shard_map/psum | solution.py:289
  792.6 6.7 copy-start.16
  799.3 826.6 %reduce-scatter.2.cloned.1.call-start = ((), (), s32[]{:S(2)}) async-start(), calls=%async_computation.5 | async-start | bytes 16908288 | tf_op jit(solution)/shard_map/reduce_scatter | solution.py:270
  956.0 12.3 copy-start.7
  956.0 12.3 copy-start.45
  956.0 12.3 copy-start.47
  956.0 12.4 copy-start.93
  1044.9 583.8 %copy-start.1 = (bf16[1024,1024]{1,0:T(8,128)(2,1)S(1)}, bf16[1024,1024]{1,0:T(8,128)(2,1)}, u32[]{:S(2)}) copy-start(bf16[1024,1024]{1,0:T(8,128)(2,1)} %param.15) | copy-start | bytes 6291460
  (72 other events, 302.8 us)
Sparse Core Ops, SparseCore 0:
  799.4 152.5 all-reduce.3
  954.4 671.3 reduce-scatter.1
where the time goes:
time: 1650 us; the launch traced here: 1640 us
  waiting for transfers between devices  669 us (41%)
  local copies, waits for them, and re-layouts  384 us (23%)
  matrix products  233 us (14%)
  other arithmetic  204 us (12%)
  blocking collectives  66.8 us (4%)
  starting transfers between devices  40.5 us (2%)
  loops' own time  21.7 us (1%)
    reduce_scatter x1, waiting for transfers between devices, local(): lax.psum_scatter(jnp.concatenate([lax.dot_general(flat_normed, flat_grad_...  577 us
    unnamed x2, other arithmetic  91.7 us
    psum x1, blocking collectives, local(): small_sums = lax.psum((jnp.stack(kernel_rows), gain_sum), ('seq', 'dp'))  66.8 us
    all_to_all x1, local copies, waits for them, and re-layouts, local(): lax.all_to_all(stacked, 'seq', split_axis=1, concat_axis=0, tiled=True)  66.4 us
    dot_general x32, matrix products, block_probs(): jnp.einsum('hqd,hkd->hqk', queries, key_rows, preferred_element_type=jnp....  50.1 us
    unnamed x229, local copies, waits for them, and re-layouts  43.1 us
    dot_general x16, matrix products, block_backward(): jnp.einsum('hqk,hqd->hkd', attn_probs.astype(jnp.bfloat16), grad_output,...  41.5 us
    dot_general x16, matrix products, block_forward(): jnp.einsum('hqk,hkd->hqd', attn_probs.astype(jnp.bfloat16), values, prefe...  39.5 us
  transfers between devices with their start and end apart: 10, of which 7 were waited for; matrix products, arithmetic and copies ran while one was open for 11% of the time, Pallas kernels for 0%

commit v1 on v0

--- a/solution.py
+++ b/solution.py
@@ -22,6 +22,11 @@
         after = lax.ppermute(initial, axis, down)
         shard = jnp.concatenate([before, shard, after], axis=dim)
     return shard
+
+
+def staged_scatter(partial):
+    partial = lax.psum_scatter(partial, "seq", scatter_dimension=0, tiled=True)
+    return lax.psum_scatter(partial, "dp", scatter_dimension=0, tiled=True)
 
 
 def segment_ids(positions, length_row, seq_length):
@@ -267,31 +272,20 @@
     )
     gain_sum = jnp.sum(grad_normed * unit_rows, axis=(0, 1))
     contract_rows = (((0,), (0,)), ((), ()))
-    summed = lax.psum_scatter(
-        jnp.concatenate(
-            [
-                lax.dot_general(
-                    flat_normed, flat_grad_qkv, contract_rows, preferred_element_type=jnp.float32
-                ),
-                lax.dot_general(
-                    flat_attended,
-                    flat_grad_hidden,
-                    contract_rows,
-                    preferred_element_type=jnp.float32,
-                ),
-            ],
-            axis=1,
-        ),
-        ("seq", "dp"),
-        scatter_dimension=0,
-        tiled=True,
+    out_sum = staged_scatter(
+        lax.dot_general(
+            flat_attended, flat_grad_hidden, contract_rows, preferred_element_type=jnp.float32
+        )
+    )
+    qkv_sum = staged_scatter(
+        lax.dot_general(flat_normed, flat_grad_qkv, contract_rows, preferred_element_type=jnp.float32)
     )
     small_sums = lax.psum((jnp.stack(kernel_rows), gain_sum), ("seq", "dp"))
     return (
         output,
         grad_inputs.astype(jnp.bfloat16),
-        summed[:, : 3 * model_width] * factor,
-        summed[:, 3 * model_width :] * factor,
+        qkv_sum * factor,
+        out_sum * factor,
         small_sums[0] * factor,
         small_sums[1] * factor,
     )

time: 1650 us -> 1140 us (0.69)
  waiting for transfers between devices: 669 us -> 99.1 us
  blocking collectives: 66.8 us -> 115 us
    reduce_scatter x1 -> x4, waiting for transfers between devices: 577 us -> 47.3 us  [the longest x2 40.3 us: staged_scatter(): return lax.psum_scatter(partial, 'dp', scatter_dimension=0, tiled=True)]
    all_to_all x0 -> x1, blocking collectives: none -> 46.9 us  [local(): lax.all_to_all(stacked, 'seq', split_axis=1, concat_axis=0, tiled=True)]
    all_to_all x1 -> x0, waiting for transfers between devices: 22.1 us -> none  [local(): lax.all_to_all(stacked, 'seq', split_axis=1, concat_axis=0, tiled=True)]
    all_to_all x1, waiting for transfers between devices: 16.8 us -> 0.01 us  [local(): lax.all_to_all(grad_packed, 'seq', split_axis=0, concat_axis=1, tiled=True)]
    unnamed x229 -> x271, local copies, waits for them, and re-layouts: 43.1 us -> 47.8 us
  transfers between devices with their start and end apart: 10 -> 12, of which waited for: 7 -> 6; matrix products, arithmetic and copies ran while one was open for 11% -> 43% of each run, Pallas kernels for 0% -> 0%
where the time goes in v1:
time: 1140 us; the launch traced here: 1120 us
  local copies, waits for them, and re-layouts  396 us (35%)
  matrix products  237 us (21%)
  other arithmetic  204 us (18%)
  blocking collectives  115 us (10%)
  waiting for transfers between devices  99.1 us (9%)
  starting transfers between devices  31.7 us (3%)
  loops' own time  21.7 us (2%)
  between operations  18.3 us (2%)
    unnamed x2, other arithmetic  93.2 us
    psum x1, blocking collectives, local(): small_sums = lax.psum((jnp.stack(kernel_rows), gain_sum), ('seq', 'dp'))  68.1 us
    all_to_all x1, local copies, waits for them, and re-layouts, local(): lax.all_to_all(stacked, 'seq', split_axis=1, concat_axis=0, tiled=True)  66.4 us
    dot_general x32, matrix products, block_probs(): jnp.einsum('hqd,hkd->hqk', queries, key_rows, preferred_element_type=jnp....  50.1 us
    unnamed x271, local copies, waits for them, and re-layouts  47.8 us
    all_to_all x1, blocking collectives, local(): lax.all_to_all(stacked, 'seq', split_axis=1, concat_axis=0, tiled=True)  46.9 us
    dot_general x16, matrix products, block_backward(): jnp.einsum('hqk,hqd->hkd', attn_probs.astype(jnp.bfloat16), grad_output,...  41.4 us
    reduce_scatter x2, waiting for transfers between devices, staged_scatter(): return lax.psum_scatter(partial, 'dp', scatter_dimension=0, tiled=True)  40.3 us
  transfers between devices with their start and end apart: 12, of which 6 were waited for; matrix products, arithmetic and copies ran while one was open for 43% of the time, Pallas kernels for 0%

profile of v1, /device:TPU:0, one launch (start us, length us, event | category | flops | bytes accessed | tf_op | source)
XLA Modules:
  0.0 1122.8 jit_solution(8214030998194642378)
XLA Ops:
  12.9 7.6 convolution_convert_fusion.2
  20.4 4.7 copy.89
  25.1 5.5 reshape_reshape.9
  30.6 21.3 %copy.90 = bf16[2,16,256,3,64]{4,3,2,1,0:T(4,128)(2,1)} copy(bf16[2,16,256,3,64]{2,0,4,1,3:T(2,128)(2,1)} %bitcast.236) | data formatting | bytes 6291456 | tf_op jit(solution)/shard_map/transpose | solution.py:176
  51.9 15.4 %reshape.390 = bf16[32,128,384]{2,1,0:T(8,128)(2,1)} reshape(bf16[2,16,256,3,64]{4,3,2,1,0:T(4,128)(2,1)} %copy.90) | data formatting | bytes 6291456 | tf_op jit(solution)/shard_map/reshape | solution.py:177
  67.3 7.8 all-to-all-start
  77.8 37.5 %all-to-all-done = bf16[32,128,384]{2,1,0:T(8,128)(2,1)} async-done(((bf16[32,128,384]{2,1,0:T(8,128)(2,1)}), bf16[32,128,384]{2,1,0:T(8,128)(2,1)}, u32[]{:S(2)}, u32[]{:S(2)}) %all-to-all-start) | async-done | bytes 3145760 | tf_op jit(solution)/shard_map/all_to_all | solution.py:178
  115.3 16.0 %reshape.391 = bf16[1,8192,3,64]{3,2,1,0:T(4,128)(2,1)} reshape(bf16[32,128,384]{2,1,0:T(8,128)(2,1)} %all-to-all-done) | data formatting | bytes 6291456 | tf_op jit(solution)/shard_map/reshape | solution.py:178
  131.3 20.1 %fusion.197 = (bf16[1,8192,1,64]{3,2,1,0:T(2,128)(2,1)}, bf16[1,8192,1,64]{3,2,1,0:T(2,128)(2,1)}, bf16[1,8192,1,64]{3,2,1,0:T(2,128)(2,1)}) fusion(bf16[1,8192,3,64]{3,2,1,0:T(4,128)(2,1)} %reshape.391), kind=kLoop, calls=%fused_computation.372 | loop fusion | bytes 6291456 | tf_op jit(solution)/shard_map/slice | solution.py:183
  151.5 8.9 copy.93
  163.0 8.9 copy.92
  174.7 8.9 copy.91
  192.1 98.0 %while.24 = (s32[]{:T(128)}, bf16[16,1,512,64]{2,3,1,0:T(8,128)(2,1)}, s32[16]{0:T(128)S(1)}, s32[8192]{0:T(1024)S(1)}, s32[8704]{0:T(1024)S(1)}, /*index=5*/bf1...) while((s32[]{:T(128)}, ...), condition=%wide.region_8.9_spmd, body=%wide.region_5.8_spmd.sunk | while | flops 143162368 | bytes 7053552 | solution.py:98
  292.9 8.0 reshape_reshape_transpose.4
  301.4 24.5 %reduce.16 = bf16[4096,128]{1,0:T(8,128)(2,1)} reduce(bf16[4096,1,128]{2,1,0:T(2,128)(2,1)} %bitcast.239, bf16[]{:T(256)} %broadcast.278), dimensions={1}, to_apply=%bitcast.167.reduce_sub_computation | reduce | bytes 2097154
  328.1 4.9 all-to-all-start.1
  337.4 12.5 %all-to-all-done.1 = bf16[32,2,8192]{2,1,0:T(2,128)(2,1)} async-done(((bf16[32,2,8192]{2,1,0:T(2,128)(2,1)}), bf16[32,2,8192]{2,1,0:T(2,128)(2,1)}, u32[]{:S(2)}, u32[]{:S(2)}) %all-to-all-start.1) | async-done | bytes 1048608 | tf_op jit(solution)/shard_map/all_to_all | solution.py:193
  349.8 5.8 reshape.412
  355.6 19.5 %bitcast_reduce_fusion.1 = bf16[4096,128]{1,0:T(8,128)(2,1)} fusion(bf16[4096,1,128]{2,1,0:T(2,128)(2,1)} %reshape.412), kind=kLoop, calls=%fused_computation.378 | loop fusion | bytes 2097152 | tf_op jit(solution)/shard_map/all_to_all | solution.py:193
  375.1 3.9 reshape.392
  390.8 22.0 %select_reduce_fusion = (f32[1024]{0:T(1024)}, f32[1024]{0:T(1024)}, f32[1024]{0:T(1024)}, f32[1024]{0:T(1024)}, f32[1024]{0:T(1024)}, /*index=5*/f32[1024]{0:T(...) fusion(f32[2,286,1024]{2,1,0:T(8,128)S(1)} %maximum_convert_fus, ...), kind=kLoop, calls=%fused_computation.179 | loop fusion | flops 67099648 | bytes 70434304 | tf_op jit(solution)/shard_map/reduce_sum | solution.py:233
  412.9 4.5 select_reduce_fusion.9
  417.4 4.7 collective-permute-start.2
  423.4 4.0 copy.115
  431.4 13.5 %fusion.195 = (bf16[2,256,1024]{2,1,0:T(8,128)(2,1)S(1)}, f32[2,256,1024]{2,1,0:T(8,128)}) fusion(f32[2,286,1024]{2,1,0:T(8,128)S(1)} %maximum_convert_fusion.1, f32[1024]{0:T(1024)S(1)} %bitcast.274, pred[2,256]{1,0:T(4,128)(4,1)S(1)} %copy-done.65, f32[1024]{0:T(1024)S(1)} %bitcast.276, pred[2,256]{1,0:T(4,128)(4,1)S(1)} %copy-done.68, ...), kind=kLoop, calls=%fused_computation.371 | loop fusion | flops 49807360 | bytes 69348864 | tf_op jit(solution)/shard_map/convert_element_type | solution.py:238
  450.5 4.0 reshape.399
  454.5 9.0 all-to-all-start.2
  463.7 5.7 select_reduce_fusion.18
  471.1 4.8 stack.151
  475.9 4.8 fusion.203
  484.5 192.3 %while.25 = (s32[]{:T(128)}, f32[1,8704,64]{1,2,0:T(8,128)S(1)}, f32[1,8704,64]{1,2,0:T(8,128)}, bf16[16,1,512,64]{2,3,1,0:T(8,128)(2,1)S(1)}, s32[16]{0:T(128)S...) while((s32[]{:T(128)}, f32[1,8704,64]{1,2,0:T(8,128)S(1)}, ...), condition=%wide.region_19.20_spmd, body=%wide.region_15.19_spmd.sunk | while | flops 349993472 | bytes 14145836 | solution.py:139
  684.7 8.4 copy.110
  693.1 27.3 %reshape.405 = bf16[1,4096,384]{2,0,1:T(2,128)(2,1)} reshape(bf16[1,8192,3,64]{3,2,1,0:T(4,128)(2,1)} %copy.110) | data formatting | bytes 6291456 | tf_op jit(solution)/shard_map/reshape | solution.py:258
  720.4 68.7 %reduce.17 = bf16[4096,384]{1,0:T(8,128)(2,1)} reduce(bf16[4096,1,384]{2,1,0:T(2,128)(2,1)} %bitcast.233, bf16[]{:T(256)} %broadcast.278), dimensions={1}, to_apply=%bitcast.169.reduce_sub_computation | reduce | bytes 6291458
  789.1 6.3 reshape.413
  795.5 46.9 %all_to_all.16 = bf16[32,2,24576]{2,1,0:T(2,128)(2,1)} all-to-all(bf16[32,2,24576]{2,1,0:T(2,128)(2,1)S(1)} %reshape.413), channel_id=1, replica_groups=mesh['seq'=32,'dp'=4] {'seq'}, dimensions={0} | all-to-all | bytes 6291456 | tf_op jit(solution)/shard_map/all_to_all | solution.py:261
  842.4 18.9 %reshape.414 = bf16[4096,1,384]{2,1,0:T(2,128)(2,1)} reshape(bf16[32,2,24576]{2,1,0:T(2,128)(2,1)} %all_to_all.16) | data formatting | bytes 6291456
  861.2 66.4 %bitcast_reduce_fusion = bf16[4096,384]{1,0:T(8,128)(2,1)S(1)} fusion(bf16[4096,1,384]{2,1,0:T(2,128)(2,1)} %reshape.414), kind=kLoop, calls=%fused_computation.377 | loop fusion | bytes 6291456 | tf_op jit(solution)/shard_map/all_to_all | solution.py:261
  927.6 9.2 reshape.402
  936.8 19.3 %copy.114 = bf16[2,256,3,16,64]{1,0,4,3,2:T(2,128)(2,1)S(1)} copy(bf16[2,256,3,16,64]{4,2,1,3,0:T(4,128)(2,1)} %bitcast.231) | data formatting | bytes 6291456 | tf_op jit(solution)/shard_map/transpose | solution.py:262
  957.3 6.4 fusion.202
  968.8 12.9 %copy.112 = bf16[2,256,3,16,64]{1,4,3,2,0:T(8,128)(2,1)} copy(bf16[2,256,3,16,64]{4,2,1,3,0:T(4,128)(2,1)} %bitcast.232) | data formatting | bytes 6291456 | tf_op jit(solution)/shard_map/transpose | solution.py:262
  981.8 9.7 fusion.61
  991.6 68.1 %psum.15 = f32[1024]{0:T(1024)S(1)} all-reduce(f32[1024]{0:T(1024)S(1)} %get-tuple-element.207), channel_id=1, replica_groups=mesh['seq'=32,'dp'=4] {'seq','dp'}, use_global_device_ids=true, to_apply=%region_59.60 | all-reduce | flops 1024 | bytes 8192 | tf_op jit(solution)/shard_map/psum | solution.py:283
  1060.3 7.0 reduce-scatter.5.cloned.1.call-done
  1067.3 4.1 fusion.60
  1071.4 18.3 %reduce-scatter.11.cloned.1.call-done = f32[8,1024]{1,0:T(8,128)} async-done(((f32[32,1024]{1,0:T(8,128)}), f32[8,1024]{1,0:T(8,128)}) %reduce-scatter.11.cloned.1.call-update) | async-done | bytes 32784 | tf_op jit(solution)/shard_map/reduce_scatter | solution.py:29
  1091.1 22.1 %reduce-scatter.7.cloned.1.call-done = f32[8,3072]{1,0:T(8,128)} async-done(((f32[32,3072]{1,0:T(8,128)}), f32[8,3072]{1,0:T(8,128)}) %reduce-scatter.7.cloned.1.call-update) | async-done | bytes 98320 | tf_op jit(solution)/shard_map/reduce_scatter | solution.py:29
  (614 shorter events, 344.4 us)
Async XLA Ops:
  8.0 373.7 %copy-start = (bf16[1024,1024]{1,0:T(8,128)(2,1)S(1)}, bf16[1024,1024]{1,0:T(8,128)(2,1)}, u32[]{:S(2)}) copy-start(bf16[1024,1024]{1,0:T(8,128)(2,1)} %param.15) | copy-start | bytes 6291460
  67.3 7.9 copy-start.130
  67.3 48.0 %all-to-all-start = ((bf16[32,128,384]{2,1,0:T(8,128)(2,1)}), bf16[32,128,384]{2,1,0:T(8,128)(2,1)}, u32[]{:S(2)}, u32[]{:S(2)}) async-start(bf16[32,128,384]{2,1,0:T(8,128)(2,1)} %reshape.390), calls=%async_computation | async-start | bytes 6291456 | tf_op jit(solution)/shard_map/all_to_all | solution.py:178
  326.0 11.2 copy-start.17
  328.1 21.7 %all-to-all-start.1 = ((bf16[32,2,8192]{2,1,0:T(2,128)(2,1)}), bf16[32,2,8192]{2,1,0:T(2,128)(2,1)}, u32[]{:S(2)}, u32[]{:S(2)}) async-start(bf16[32,2,8192]{2,1,0:T(2,128)(2,1)} %reshape.411), calls=%async_computation.1 | async-start | bytes 2097152 | tf_op jit(solution)/shard_map/all_to_all | solution.py:193
  337.2 53.2 %copy-start.18 = (f32[1,1024]{1,0:T(1,128)}, f32[1,1024]{1,0:T(1,128)S(1)}, u32[]{:S(2)}) copy-start(f32[1,1024]{1,0:T(1,128)S(1)} %get-tuple-element.277) | copy-start | bytes 12292
  337.3 53.2 %copy-start.20 = (f32[1,1024]{1,0:T(1,128)}, f32[1,1024]{1,0:T(1,128)S(1)}, u32[]{:S(2)}) copy-start(f32[1,1024]{1,0:T(1,128)S(1)} %get-tuple-element.278) | copy-start | bytes 12292
  337.3 53.2 %copy-start.22 = (f32[1,1024]{1,0:T(1,128)}, f32[1,1024]{1,0:T(1,128)S(1)}, u32[]{:S(2)}) copy-start(f32[1,1024]{1,0:T(1,128)S(1)} %get-tuple-element.279) | copy-start | bytes 12292
  337.3 53.2 %copy-start.24 = (f32[1,1024]{1,0:T(1,128)}, f32[1,1024]{1,0:T(1,128)S(1)}, u32[]{:S(2)}) copy-start(f32[1,1024]{1,0:T(1,128)S(1)} %get-tuple-element.280) | copy-start | bytes 12292
  337.3 53.2 %copy-start.26 = (f32[1,1024]{1,0:T(1,128)}, f32[1,1024]{1,0:T(1,128)S(1)}, u32[]{:S(2)}) copy-start(f32[1,1024]{1,0:T(1,128)S(1)} %get-tuple-element.281) | copy-start | bytes 12292
  337.3 53.2 %copy-start.28 = (f32[1,1024]{1,0:T(1,128)}, f32[1,1024]{1,0:T(1,128)S(1)}, u32[]{:S(2)}) copy-start(f32[1,1024]{1,0:T(1,128)S(1)} %get-tuple-element.282) | copy-start | bytes 12292
  337.3 53.2 %copy-start.30 = (f32[1,1024]{1,0:T(1,128)}, f32[1,1024]{1,0:T(1,128)S(1)}, u32[]{:S(2)}) copy-start(f32[1,1024]{1,0:T(1,128)S(1)} %get-tuple-element.283) | copy-start | bytes 12292
  337.3 53.2 %copy-start.32 = (f32[1,1024]{1,0:T(1,128)}, f32[1,1024]{1,0:T(1,128)S(1)}, u32[]{:S(2)}) copy-start(f32[1,1024]{1,0:T(1,128)S(1)} %get-tuple-element.284) | copy-start | bytes 12292
  337.3 53.2 %copy-start.34 = (f32[1,1024]{1,0:T(1,128)}, f32[1,1024]{1,0:T(1,128)S(1)}, u32[]{:S(2)}) copy-start(f32[1,1024]{1,0:T(1,128)S(1)} %get-tuple-element.285) | copy-start | bytes 12292
  337.3 53.2 %copy-start.36 = (f32[1,1024]{1,0:T(1,128)}, f32[1,1024]{1,0:T(1,128)S(1)}, u32[]{:S(2)}) copy-start(f32[1,1024]{1,0:T(1,128)S(1)} %get-tuple-element.286) | copy-start | bytes 12292
  337.3 53.2 %copy-start.38 = (f32[1,1024]{1,0:T(1,128)}, f32[1,1024]{1,0:T(1,128)S(1)}, u32[]{:S(2)}) copy-start(f32[1,1024]{1,0:T(1,128)S(1)} %get-tuple-element.287) | copy-start | bytes 12292
  337.4 53.2 %copy-start.40 = (f32[1,1024]{1,0:T(1,128)}, f32[1,1024]{1,0:T(1,128)S(1)}, u32[]{:S(2)}) copy-start(f32[1,1024]{1,0:T(1,128)S(1)} %get-tuple-element.288) | copy-start | bytes 12292
  384.2 6.4 copy-start.12
  384.2 6.4 copy-start.55
  384.5 3.8 collective-permute-start
  386.9 3.1 collective-permute-start.1
  388.3 24.6 %copy-start.127 = (pred[2,256]{1,0:T(4,128)(4,1)}, pred[2,256]{1,0:T(4,128)(4,1)S(1)}, u32[]{:S(2)}) copy-start(pred[2,256]{1,0:T(4,128)(4,1)S(1)} %get-tuple-element.329) | copy-start | bytes 1540
  388.3 24.6 %copy-start.128 = (pred[2,256]{1,0:T(4,128)(4,1)}, pred[2,256]{1,0:T(4,128)(4,1)S(1)}, u32[]{:S(2)}) copy-start(pred[2,256]{1,0:T(4,128)(4,1)S(1)} %get-tuple-element.330) | copy-start | bytes 1540
  388.3 24.6 %copy-start.129 = (pred[2,256]{1,0:T(4,128)(4,1)}, pred[2,256]{1,0:T(4,128)(4,1)S(1)}, u32[]{:S(2)}) copy-start(pred[2,256]{1,0:T(4,128)(4,1)S(1)} %get-tuple-element.331) | copy-start | bytes 1540
  390.4 22.5 %copy-start.2 = (f32[2,286,1024]{2,1,0:T(8,128)}, f32[2,286,1024]{2,1,0:T(8,128)S(1)}, u32[]{:S(2)}) copy-start(f32[2,286,1024]{2,1,0:T(8,128)S(1)} %maximum_convert_fusion) | copy-start | bytes 7028740
  417.4 12.8 %collective-permute-start.2 = (bf16[2,15,1024]{2,1,0:T(8,128)(2,1)S(1)}, bf16[2,15,1024]{2,1,0:T(8,128)(2,1)S(1)}, u32[]{:S(2)}, u32[]{:S(2)}) collective-permute-start(bf16[2,15,1024]{2,1,0:T(8,128)(2,1)S(1)} %get-tuple-element.266), channel_id=1, source_target_pairs={{0,4},{4,8},{8,12},{12,16},{16,20},{20,24},{24,28},{28,32},{32,36}... | collective-permute-start | bytes 184328 | tf_op jit(solution)/shard_map/ppermute | solution.py:21
  422.1 8.1 collective-permute-start.3
  450.4 13.2 %copy-start.3 = (f32[2,286,1024]{2,1,0:T(8,128)S(1)}, f32[2,286,1024]{2,1,0:T(8,128)}, u32[]{:S(2)}) copy-start(f32[2,286,1024]{2,1,0:T(8,128)} %copy-done.2) | copy-start | bytes 7028740
  450.4 13.2 %copy-start.57 = (pred[2,256]{1,0:T(4,128)(4,1)S(1)}, pred[2,256]{1,0:T(4,128)(4,1)}, u32[]{:S(2)}) copy-start(pred[2,256]{1,0:T(4,128)(4,1)} %get-tuple-element.313) | copy-start | bytes 1540
  450.4 13.2 %copy-start.78 = (pred[2,256]{1,0:T(4,128)(4,1)S(1)}, pred[2,256]{1,0:T(4,128)(4,1)}, u32[]{:S(2)}) copy-start(pred[2,256]{1,0:T(4,128)(4,1)} %get-tuple-element.305) | copy-start | bytes 1540
  450.4 13.3 %copy-start.81 = (pred[2,256]{1,0:T(4,128)(4,1)S(1)}, pred[2,256]{1,0:T(4,128)(4,1)}, u32[]{:S(2)}) copy-start(pred[2,256]{1,0:T(4,128)(4,1)} %get-tuple-element.306) | copy-start | bytes 1540
  450.4 13.3 %copy-start.84 = (pred[2,256]{1,0:T(4,128)(4,1)S(1)}, pred[2,256]{1,0:T(4,128)(4,1)}, u32[]{:S(2)}) copy-start(pred[2,256]{1,0:T(4,128)(4,1)} %get-tuple-element.307) | copy-start | bytes 1540
  450.4 13.3 %copy-start.87 = (pred[2,256]{1,0:T(4,128)(4,1)S(1)}, pred[2,256]{1,0:T(4,128)(4,1)}, u32[]{:S(2)}) copy-start(pred[2,256]{1,0:T(4,128)(4,1)} %get-tuple-element.308) | copy-start | bytes 1540
  450.4 13.3 %copy-start.90 = (pred[2,256]{1,0:T(4,128)(4,1)S(1)}, pred[2,256]{1,0:T(4,128)(4,1)}, u32[]{:S(2)}) copy-start(pred[2,256]{1,0:T(4,128)(4,1)} %get-tuple-element.309) | copy-start | bytes 1540
  450.4 13.3 %copy-start.93 = (pred[2,256]{1,0:T(4,128)(4,1)S(1)}, pred[2,256]{1,0:T(4,128)(4,1)}, u32[]{:S(2)}) copy-start(pred[2,256]{1,0:T(4,128)(4,1)} %get-tuple-element.310) | copy-start | bytes 1540
  450.4 13.3 %copy-start.96 = (pred[2,256]{1,0:T(4,128)(4,1)S(1)}, pred[2,256]{1,0:T(4,128)(4,1)}, u32[]{:S(2)}) copy-start(pred[2,256]{1,0:T(4,128)(4,1)} %get-tuple-element.311) | copy-start | bytes 1540
  450.5 13.3 %copy-start.99 = (pred[2,256]{1,0:T(4,128)(4,1)S(1)}, pred[2,256]{1,0:T(4,128)(4,1)}, u32[]{:S(2)}) copy-start(pred[2,256]{1,0:T(4,128)(4,1)} %get-tuple-element.312) | copy-start | bytes 1540
  454.5 26.3 %all-to-all-start.2 = ((bf16[32,128,128]{2,1,0:T(8,128)(2,1)}), bf16[32,128,128]{2,1,0:T(8,128)(2,1)S(1)}, u32[]{:S(2)}, u32[]{:S(2)}) async-start(bf16[32,128,128]{2,1,0:T(8,128)(2,1)} %reshape.399), calls=%async_computation.2 | async-start | bytes 2097152 | tf_op jit(solution)/shard_map/all_to_all | solution.py:245
  463.6 503.7 %all-reduce.4.cloned.1.call-start = ((), (), s32[]{:S(2)}) async-start(), calls=%async_computation.12 | async-start | bytes 262144 | tf_op jit(solution)/shard_map/psum | solution.py:283
  475.9 515.6 %reduce-scatter.9.cloned.1.call-start = ((), (), s32[]{:S(2)}) async-start(), calls=%async_computation.10 | async-start | bytes 4325376 | tf_op jit(solution)/shard_map/reduce_scatter | solution.py:28
  480.7 586.5 %reduce-scatter.5.cloned.1.call-start = ((), (), s32[]{:S(2)}) async-start(), calls=%async_computation.8 | async-start | bytes 12976128 | tf_op jit(solution)/shard_map/reduce_scatter | solution.py:28
  963.7 126.0 %reduce-scatter.11.cloned.1.call-start = ((), (), s32[]{:S(2)}) async-start(), calls=%async_computation.11 | async-start | bytes 163840 | tf_op jit(solution)/shard_map/reduce_scatter | solution.py:29
  968.8 12.9 %copy-start.7 = (bf16[2,256,1024]{2,1,0:T(8,128)(2,1)S(1)}, bf16[2,256,1024]{2,1,0:T(8,128)(2,1)}, u32[]{:S(2)}) copy-start(bf16[2,256,1024]{2,1,0:T(8,128)(2,1)} %param.11) | copy-start | bytes 3145732
  968.8 12.9 %copy-start.43 = (f32[2,256]{1,0:T(2,128)S(1)}, f32[2,256]{1,0:T(2,128)}, u32[]{:S(2)}) copy-start(f32[2,256]{1,0:T(2,128)} %copy-done.42) | copy-start | bytes 6148
  968.8 12.9 %copy-start.45 = (f32[2,256]{1,0:T(2,128)S(1)}, f32[2,256]{1,0:T(2,128)}, u32[]{:S(2)}) copy-start(f32[2,256]{1,0:T(2,128)} %copy-done.44) | copy-start | bytes 6148
  968.8 13.0 %copy-start.113 = (f32[1024]{0:T(1024)S(1)}, f32[1024]{0:T(1024)}, u32[]{:S(2)}) copy-start(f32[1024]{0:T(1024)} %param.13) | copy-start | bytes 12292
  991.6 121.6 %reduce-scatter.7.cloned.1.call-start = ((), (), s32[]{:S(2)}) async-start(), calls=%async_computation.9 | async-start | bytes 491520 | tf_op jit(solution)/shard_map/reduce_scatter | solution.py:29
  1067.3 47.3 %copy-start.1 = (bf16[1024,1024]{1,0:T(8,128)(2,1)S(1)}, bf16[1024,1024]{1,0:T(8,128)(2,1)}, u32[]{:S(2)}) copy-start(bf16[1024,1024]{1,0:T(8,128)(2,1)} %param.15) | copy-start | bytes 6291460
  (95 other events, 296.7 us)
Sparse Core Ops, SparseCore 0:
  476.0 144.9 all-reduce.3
Sparse Core Ops, SparseCore 1:
  480.8 84.6 reduce-scatter.8
  963.8 103.4 reduce-scatter.4
  1069.5 20.1 reduce-scatter.10
  1092.1 21.0 reduce-scatter.6

commit v2 on v1

v2 whole, which is shorter than its diff:
```python
import jax
import jax.numpy as jnp
from jax import lax
from jax.sharding import PartitionSpec as P

HEADS = 16
MOST = 256


EPSILON = 1e-05
NEGATIVE = -1e30


def with_halo(shard, sides, width):
    for axis, dim in sides:
        size, length = (lax.axis_size(axis), shard.shape[dim])
        up = [(i, (i + 1) % size) for i in range(size - 1)]
        down = [(j, i) for i, j in up]
        last = lax.slice_in_dim(shard, length - width, length, axis=dim)
        initial = lax.slice_in_dim(shard, 0, width, axis=dim)
        before = lax.ppermute(last, axis, up)
        after = lax.ppermute(initial, axis, down)
        shard = jnp.concatenate([before, shard, after], axis=dim)
    return shard


def staged_scatter(partial):
    partial = lax.psum_scatter(partial, "seq", scatter_dimension=0, tiled=True)
    return lax.psum_scatter(partial, "dp", scatter_dimension=0, tiled=True)


def segment_ids(positions, length_row, seq_length):
    ends = jnp.cumsum(length_row)
    inside = (positions >= 0) & (positions < seq_length)
    counted = jnp.sum((ends[None, :] <= positions[:, None]).astype(jnp.int32), axis=1)
    return jnp.where(inside, counted, -1)


def from_neighbour(shard, axis, step):
    size = lax.axis_size(axis)
    if step > 0:
        pairs = [(i, i + step) for i in range(size - step)]
    else:
        pairs = [(i - step, i) for i in range(size + step)]
    return lax.ppermute(shard, axis, pairs)


def local(inputs, lengths, norm_gain, qkv_weight, out_weight, kernel, cotangent):
    batches, frames, model_width = inputs.shape
    shards = lax.axis_size("seq")
    position = lax.axis_index("seq")
    seq_length = frames * shards
    head_dim = model_width // HEADS
    score_scale = head_dim ** (-0.5)
    conv_reach = kernel.shape[0] // 2
    factor = (batches * seq_length * lax.axis_size("dp")) ** (-0.5)
    first_frame = position * frames
    local_pos = first_frame + jnp.arange(frames, dtype=jnp.int32)
    segment_local = jnp.stack(
        [segment_ids(local_pos, lengths[batch_index], seq_length) for batch_index in range(batches)]
    )
    widened = inputs.astype(jnp.float32)
    average = jnp.mean(widened, axis=-1, keepdims=True)
    centred = widened - average
    inverse = lax.rsqrt(jnp.mean(centred * centred, axis=-1, keepdims=True) + EPSILON)
    unit_rows = centred * inverse
    normed = (unit_rows * norm_gain).astype(jnp.bfloat16)
    flat_normed = normed.reshape(-1, model_width)
    projected = jnp.dot(flat_normed, qkv_weight, preferred_element_type=jnp.float32).astype(
        jnp.bfloat16
    )
    projected = projected.reshape(batches, frames, 3 * model_width)
    proj5 = projected.reshape(batches, frames, 3, HEADS, head_dim)
    head_queries = proj5[:, :, 0]
    own_kv = proj5[:, :, 1:]
    kv_window = jnp.concatenate(
        [from_neighbour(own_kv, "seq", 1), own_kv, from_neighbour(own_kv, "seq", -1)], axis=1
    )
    head_keys = kv_window[:, :, 0]
    head_values = kv_window[:, :, 1]
    window_pos = first_frame - frames + jnp.arange(3 * frames, dtype=jnp.int32)
    segment_window = jnp.stack(
        [segment_ids(window_pos, lengths[batch_index], seq_length) for batch_index in range(batches)]
    )
    allowed = (segment_local[:, :, None] == segment_window[:, None, :])[:, None]
    scores = (
        jnp.einsum("bqhd,bkhd->bhqk", head_queries, head_keys, preferred_element_type=jnp.float32)
        * score_scale
    )
    scores = jnp.where(allowed, scores, NEGATIVE)
    row_max = jnp.max(scores, axis=-1, keepdims=True)
    exponent = jnp.where(allowed, jnp.exp(scores - row_max), 0.0)
    attn_probs = exponent / jnp.sum(exponent, axis=-1, keepdims=True)
    weights = attn_probs.astype(jnp.bfloat16)
    head_out = jnp.einsum(
        "bhqk,bkhd->bqhd", weights, head_values, preferred_element_type=jnp.float32
    ).astype(jnp.bfloat16)
    attended = head_out.reshape(batches, frames, model_width)
    flat_attended = attended.reshape(-1, model_width)
    attn_rows = jnp.dot(flat_attended, out_weight, preferred_element_type=jnp.float32)
    hidden = (widened + attn_rows.reshape(batches, frames, model_width)).astype(jnp.bfloat16)
    padded = with_halo(hidden, (("seq", 1),), conv_reach).astype(jnp.float32)
    ext_pos = first_frame - conv_reach + jnp.arange(frames + 2 * conv_reach, dtype=jnp.int32)
    segment_ext = jnp.stack(
        [segment_ids(ext_pos, lengths[batch_index], seq_length) for batch_index in range(batches)]
    )
    conv_sum = jnp.zeros((batches, frames, model_width), jnp.float32)
    for tap_index in range(kernel.shape[0]):
        same_seg = (segment_ext[:, tap_index : tap_index + frames] == segment_local)[..., None]
        conv_sum = conv_sum + jnp.where(
            same_seg, kernel[tap_index] * padded[:, tap_index : tap_index + frames], 0.0
        )
    gated = jax.nn.sigmoid(conv_sum)
    output = (hidden.astype(jnp.float32) + conv_sum * gated).astype(jnp.bfloat16)
    incoming = cotangent.astype(jnp.float32)
    grad_conv = incoming * gated * (1.0 + conv_sum * (1.0 - gated))
    grad_pad = with_halo(grad_conv.astype(jnp.bfloat16), (("seq", 1),), conv_reach).astype(
        grad_conv.dtype
    )
    grad_hidden = incoming
    kernel_rows = []
    for tap_index in range(kernel.shape[0]):
        back_index = 2 * conv_reach - tap_index
        same_back = (segment_ext[:, back_index : back_index + frames] == segment_local)[..., None]
        grad_hidden = grad_hidden + jnp.where(
            same_back, kernel[tap_index] * grad_pad[:, back_index : back_index + frames], 0.0
        )
        same_seg = (segment_ext[:, tap_index : tap_index + frames] == segment_local)[..., None]
        kernel_rows.append(
            jnp.sum(
                jnp.where(same_seg, grad_conv * padded[:, tap_index : tap_index + frames], 0.0),
                axis=(0, 1),
            )
        )
    grad_hidden_b = grad_hidden.astype(jnp.bfloat16)
    flat_grad_hidden = grad_hidden_b.reshape(-1, model_width)
    grad_attended = jnp.dot(
        flat_grad_hidden, out_weight.T, preferred_element_type=jnp.float32
    ).astype(jnp.bfloat16)
    grad_heads = grad_attended.reshape(batches, frames, HEADS, head_dim)
    row_delta = jnp.sum(
        grad_heads.astype(jnp.float32) * head_out.astype(jnp.float32), axis=-1
    ).transpose(0, 2, 1)[..., None]
    value_window = jnp.einsum(
        "bhqk,bqhd->bkhd", weights, grad_heads, preferred_element_type=jnp.float32
    )
    grad_probs = jnp.einsum(
        "bqhd,bkhd->bhqk", grad_heads, head_values, preferred_element_type=jnp.float32
    )
    grad_scores = (attn_probs * (grad_probs - row_delta) * score_scale).astype(jnp.bfloat16)
    query_grads = jnp.einsum(
        "bhqk,bkhd->bqhd", grad_scores, head_keys, preferred_element_type=jnp.float32
    ).astype(jnp.bfloat16)
    key_window = jnp.einsum(
        "bhqk,bqhd->bkhd", grad_scores, head_queries, preferred_element_type=jnp.float32
    )
    kv_grad_window = jnp.stack([key_window, value_window], axis=2)
    kv_grads = (
        kv_grad_window[:, frames : 2 * frames]
        + from_neighbour(kv_grad_window[:, :frames].astype(jnp.bfloat16), "seq", -1).astype(
            jnp.float32
        )
        + from_neighbour(kv_grad_window[:, 2 * frames :].astype(jnp.bfloat16), "seq", 1).astype(
            jnp.float32
        )
    ).astype(jnp.bfloat16)
    grad_qkv = jnp.concatenate([query_grads[:, :, None], kv_grads], axis=2)
    grad_qkv = grad_qkv.reshape(batches, frames, 3 * model_width)
    flat_grad_qkv = grad_qkv.reshape(-1, 3 * model_width)
    grad_normed = jnp.dot(flat_grad_qkv, qkv_weight.T, preferred_element_type=jnp.float32)
    grad_normed = grad_normed.reshape(batches, frames, model_width)
    scaled = grad_normed * norm_gain
    grad_inputs = grad_hidden + inverse * (
        scaled
        - jnp.mean(scaled, axis=-1, keepdims=True)
        - unit_rows * jnp.mean(scaled * unit_rows, axis=-1, keepdims=True)
    )
    gain_sum = jnp.sum(grad_normed * unit_rows, axis=(0, 1))
    contract_rows = (((0,), (0,)), ((), ()))
    out_sum = staged_scatter(
        lax.dot_general(
            flat_attended, flat_grad_hidden, contract_rows, preferred_element_type=jnp.float32
        )
    )
    qkv_sum = staged_scatter(
        lax.dot_general(flat_normed, flat_grad_qkv, contract_rows, preferred_element_type=jnp.float32)
    )
    small_sums = lax.psum((jnp.stack(kernel_rows), gain_sum), ("seq", "dp"))
    return (
        output,
        grad_inputs.astype(jnp.bfloat16),
        qkv_sum * factor,
        out_sum * factor,
        small_sums[0] * factor,
        small_sums[1] * factor,
    )


def solution(mesh):
    in_specs = (P("dp", "seq", None), P("dp", None), P(), P(), P(), P(), P("dp", "seq", None))
    out_specs = (
        P("dp", "seq", None),
        P("dp", "seq", None),
        P(("seq", "dp"), None),
        P(("seq", "dp"), None),
        P(),
        P(),
    )
    return jax.shard_map(local, mesh=mesh, in_specs=in_specs, out_specs=out_specs, check_vma=False)
```

time: 1140 us -> 482 us (0.42); the launches traced: 1120 us -> 477 us
  local copies, waits for them, and re-layouts: 396 us -> 58.9 us
  matrix products: 237 us -> 97.8 us
  other arithmetic: 204 us -> 104 us
  blocking collectives: 115 us -> 65 us
  loops' own time: 21.7 us -> 0 us
    dot_general x112 -> x5, matrix products: 205 us -> 49.5 us  [the longest x1 15.1 us: local(): jnp.einsum('bqhd,bkhd->bhqk', grad_heads, head_values, preferred_element_...]
    unnamed x2 -> x0, other arithmetic: 93.2 us -> none
    all_to_all x2 -> x0, local copies, waits for them, and re-layouts: 85.9 us -> none  [the longest x1 66.4 us: local(): lax.all_to_all(stacked, 'seq', split_axis=1, concat_axis=0, tiled=True)]
    reshape x8 -> x2, local copies, waits for them, and re-layouts: 77.9 us -> 6.82 us  [local(): grad_heads = grad_attended.reshape(batches, frames, HEADS, head_dim)]
    transpose x6 -> x0, local copies, waits for them, and re-layouts: 62.6 us -> none  [the longest x2 32.2 us: local(): sent_back.reshape(batches, HEADS, frames, 3, head_dim)]
    all_to_all x3 -> x0, waiting for transfers between devices: 50 us -> none  [the longest x1 37.5 us: local(): lax.all_to_all(packed, 'seq', split_axis=0, concat_axis=1, tiled=True)]
    psum x1, waiting for transfers between devices: 0.01 us -> 48.1 us  [local(): small_sums = lax.psum((jnp.stack(kernel_rows), gain_sum), ('seq', 'dp'))]
    all_to_all x1 -> x0, blocking collectives: 46.9 us -> none  [local(): lax.all_to_all(stacked, 'seq', split_axis=1, concat_axis=0, tiled=True)]
  transfers between devices with their start and end apart: 12 -> 13, of which waited for: 6 -> 5; matrix products, arithmetic and copies ran while one was open for 43% -> 30% of each run, Pallas kernels for 0% -> 0%
where the time goes in v2:
time: 482 us; the launch traced here: 477 us
  other arithmetic  104 us (22%)
  waiting for transfers between devices  101 us (21%)
  matrix products  97.8 us (20%)
  blocking collectives  65 us (13%)
  local copies, waits for them, and re-layouts  58.9 us (12%)
  starting transfers between devices  32.8 us (7%)
  between operations  17.5 us (4%)
    psum x1, blocking collectives, local(): small_sums = lax.psum((jnp.stack(kernel_rows), gain_sum), ('seq', 'dp'))  65 us
    psum x1, waiting for transfers between devices, local(): small_sums = lax.psum((jnp.stack(kernel_rows), gain_sum), ('seq', 'dp'))  48.1 us
    reduce_scatter x2, waiting for transfers between devices, staged_scatter(): return lax.psum_scatter(partial, 'dp', scatter_dimension=0, tiled=True)  40.4 us
    reduce_sum x4, other arithmetic, local(): jnp.sum(jnp.where(same_seg, grad_conv * padded[:, tap_index:tap_index + f...  34.6 us
    sub x1, matrix products, local(): exponent = jnp.where(allowed, jnp.exp(scores - row_max), 0.0)  17.3 us
    unnamed x214, local copies, waits for them, and re-layouts  17.1 us
    ppermute x2, starting transfers between devices, with_halo(): before = lax.ppermute(last, axis, up)  15.1 us
    dot_general x1, matrix products, local(): jnp.einsum('bqhd,bkhd->bhqk', grad_heads, head_values, preferred_element_...  15.1 us
  transfers between devices with their start and end apart: 13, of which 5 were waited for; matrix products, arithmetic and copies ran while one was open for 30% of the time, Pallas kernels for 0%

profile of v2, /device:TPU:0, one launch (start us, length us, event | category | flops | bytes accessed | tf_op | source)
XLA Modules:
  0.0 476.8 jit_solution(15893773074737785022)
XLA Ops:
  8.1 1.6 convert_reduce_fusion
  9.7 1.6 fusion.31
  12.9 7.6 %convolution_convert_fusion = bf16[512,3072]{1,0:T(8,128)(2,1)} fusion(bf16[512,1024]{1,0:T(8,128)(2,1)S(1)} %bitcast.168, bf16[1024,3072]{1,0:T(8,128)(2,1)} %param.10), kind=kOutput, calls=%fused_computation.17 | convolution fusion | flops 3222798336 | bytes 10485760 | tf_op jit(solution)/shard_map/dot_general | solution.py:69
  20.5 8.6 %reshape.278 = bf16[2,256,3,16,64]{4,3,2,1,0:T(8,128)(2,1)} reshape(bf16[512,3072]{1,0:T(8,128)(2,1)} %convolution_convert_fusion) | data formatting | bytes 6291456 | tf_op jit(solution)/shard_map/reshape;reshape | solution.py:73
  29.1 4.9 %slice.678 = bf16[2,256,2,16,64]{4,3,2,1,0:T(8,128)(2,1)} slice(bf16[2,256,3,16,64]{4,3,2,1,0:T(8,128)(2,1)} %reshape.278), slice={[0:2], [0:256], [1:3], [0:16], [0:64]} | slice | bytes 4194304 | tf_op jit(solution)/shard_map/slice | solution.py:75
  34.1 5.8 %copy.52 = bf16[2,256,2,16,64]{1,4,3,0,2:T(8,128)(2,1)} copy(bf16[2,256,2,16,64]{4,3,2,1,0:T(8,128)(2,1)} %slice.678) | data formatting | bytes 4194304
  41.2 4.9 %collective-permute-start = (bf16[2,256,2,16,64]{1,4,3,0,2:T(8,128)(2,1)}, bf16[2,256,2,16,64]{1,4,3,0,2:T(8,128)(2,1)}, u32[]{:S(2)}, u32[]{:S(2)}) collective-permute-start(bf16[2,256,2,16,64]{1,4,3,0,2:T(8,128)(2,1)} %copy.52), channel_id=1, source_target_pairs={{0,4},{4,8},{8,12},{12,16},{16,20},{20,24},{24,28},{28,32},{32,36}... | collective-permute-start | bytes 6291464 | tf_op jit(solution)/shard_map/ppermute | solution.py:45
  46.1 3.4 slice.680
  50.4 3.6 copy.53
  60.6 5.9 %pad_maximum_fusion.1 = bf16[2,768,2,16,64]{1,4,3,0,2:T(8,128)(2,1)} fusion(bf16[2,256,2,16,64]{1,4,3,0,2:T(8,128)(2,1)} %collective-permute-done.1, bf16[2,256,2,16,64]{1,4,3,0,2:T(8,128)(2,1)} %copy.52, bf16[2,256,2,16,64]{1,4,3,0,2:T(8,128)(2,1)} %collective-permute-done), kind=kLoop, calls=%fused_computation.14 | loop fusion | flops 18874368 | bytes 12582912 | tf_op jit(solution)/shard_map/concatenate | solution.py:76
  66.4 17.3 %fusion.178 = (f32[2,16,256]{2,1,0:T(8,128)}, f32[2,16,256,768]{3,2,1,0:T(8,128)}) fusion(pred[2,256,768]{2,1,0:T(8,128)(4,1)S(1)} %broadcast_compare_fusion, bf16[2,768,2,16,64]{1,4,3,0,2:T(8,128)(2,1)} %pad_maximum_fusion.1, bf16[2,256,1,16,64]{1,4,3,0,2:T(8,128)(2,1)} %copy.53), kind=kOutput, calls=%fused_computation.352 | convolution fusion | flops 836764416 | bytes 30179328 | tf_op jit(solution)/shard_map/sub | solution.py:92
  83.8 13.3 %fusion.6 = bf16[2,16,256,768]{3,2,1,0:T(8,128)(2,1)} fusion(f32[2,16,256,768]{3,2,1,0:T(8,128)} %get-tuple-element.122, f32[2,16,256]{2,1,0:T(8,128)} %get-tuple-element.121), kind=kLoop, calls=%fused_computation.13 | loop fusion | flops 12582912 | bytes 37781504 | tf_op jit(solution)/shard_map/convert_element_type | solution.py:94
  97.1 9.4 %fusion.98 = bf16[2,16,64,256]{3,2,1,0:T(8,128)(2,1)S(1)} fusion(bf16[2,16,256,768]{3,2,1,0:T(8,128)(2,1)} %fusion.6, bf16[2,768,2,16,64]{1,4,3,0,2:T(8,128)(2,1)} %pad_maximum_fusion.1), kind=kOutput, calls=%fused_computation.184 | convolution fusion | flops 805830656 | bytes 16777216 | tf_op jit(solution)/shard_map/bhqk,bkhd->bqhd/dot_general | solution.py:95
  107.9 10.1 %collective-permute-start.2 = (bf16[2,15,1024]{2,1,0:T(8,128)(2,1)S(1)}, bf16[2,15,1024]{2,1,0:T(8,128)(2,1)S(1)}, u32[]{:S(2)}, u32[]{:S(2)}) collective-permute-start(bf16[2,15,1024]{2,1,0:T(8,128)(2,1)S(1)} %get-tuple-element.55), channel_id=1, source_target_pairs={{0,4},{4,8},{8,12},{12,16},{16,20},{20,24},{24,28},{28,32},{32,36}... | collective-permute-start | bytes 184328 | tf_op jit(solution)/shard_map/ppermute | solution.py:21
  118.0 1.5 collective-permute-start.3
  124.0 22.8 %select_reduce_fusion = (f32[1024]{0:T(1024)S(1)}, f32[1024]{0:T(1024)S(1)}, f32[1024]{0:T(1024)S(1)}, f32[1024]{0:T(1024)S(1)}, f32[1024]{0:T(1024)S(1)}, /*ind...) fusion(f32[2,286,1024]{2,1,0:T(8,128)S(1)} %maximum_convert_fus, ...), kind=kLoop, calls=%fused_computation.146 | loop fusion | flops 67099648 | bytes 70434304 | tf_op jit(solution)/shard_map/reduce_sum | solution.py:130
  146.8 5.2 %select_reduce_fusion.18 = (f32[1024]{0:T(1024)}, f32[1024]{0:T(1024)}, f32[1024]{0:T(1024)}, f32[1024]{0:T(1024)}, f32[1024]{0:T(1024)}, /*index=5*/f32[1024]{0...) fusion(f32[2,256,1024]{2,1,0:T(8,128)S(1)} %get-tuple-element.46, f32[2,286,1024]{2,1,0:T(8,128)S(1)} %maximum_convert_fusion, ...), kind=kLoop, calls=%fused_computation.164 | loop fusion | flops 14146560 | bytes 21012992 | tf_op jit(solution)/shard_map/reduce_sum | solution.py:130
  152.2 4.5 select_reduce_fusion.9
  156.7 5.0 %collective-permute-start.4 = (bf16[2,15,1024]{2,1,0:T(8,128)(2,1)S(1)}, bf16[2,15,1024]{2,1,0:T(8,128)(2,1)S(1)}, u32[]{:S(2)}, u32[]{:S(2)}) collective-permute-start(bf16[2,15,1024]{2,1,0:T(8,128)(2,1)S(1)} %get-tuple-element.53), channel_id=1, source_target_pairs={{0,4},{4,8},{8,12},{12,16},{16,20},{20,24},{24,28},{28,32},{32,36}... | collective-permute-start | bytes 184328 | tf_op jit(solution)/shard_map/ppermute | solution.py:21
  163.1 2.0 select_reduce_fusion.27
  165.1 5.5 %stack.157 = f32[31,1024]{1,0:T(8,128)} concatenate(f32[1,1024]{1,0:T(1,128)} %bitcast.246, f32[1,1024]{1,0:T(1,128)} %bitcast.245, f32[1,1024]{1,0:T(1,128)} %bitcast.244, f32[1,1024]{1,0:T(1,128)} %bitcast.243, f32[1,1024]{1,0:T(1,128)} %bitcast.255, f32[1,1024]{1,0:T(1,128)} %bitcast.254, f32[1,1024]{1,0:T(1,128)} %bitcast.253, f32[1,1024]{1,0:T(1,128)} %bitcast.252, ...), dimensions={0} | concatenate | bytes 253952 | tf_op jit(solution)/shard_map/stack | solution.py:188
  171.2 1.7 maximum_convert_fusion.1
  173.2 12.5 %fusion.171 = (bf16[2,256,1024]{2,1,0:T(8,128)(2,1)S(1)}, f32[2,256,1024]{2,1,0:T(8,128)}) fusion(f32[2,286,1024]{2,1,0:T(8,128)S(1)} %maximum_convert_fusion.1, f32[1024]{0:T(1024)S(1)} %bitcast.192, pred[2,256]{1,0:T(4,128)(4,1)S(1)} %copy-done.70, f32[1024]{0:T(1024)S(1)} %bitcast.194, pred[2,256]{1,0:T(4,128)(4,1)S(1)} %copy-done.72, ...), kind=kLoop, calls=%fused_computation.346 | loop fusion | flops 49807360 | bytes 69348864 | tf_op jit(solution)/shard_map/convert_element_type | solution.py:135
  186.7 2.3 convolution_convert_fusion.1
  189.0 4.0 reshape.279
  193.0 2.8 copy.39
  195.8 4.9 %fusion.184 = f32[1024,1024]{1,0:T(8,128)} fusion(bf16[512,1024]{0,1:T(8,128)(2,1)} %bitcast.170, bf16[512,1024]{1,0:T(8,128)(2,1)} %bitcast.167), kind=kOutput, calls=%fused_computation.354 | convolution fusion | flops 1073741824 | bytes 6291456 | tf_op jit(solution)/shard_map/dot_general | solution.py:181
  201.9 15.1 %multiply_convert_fusion = bf16[2,16,256,768]{3,2,1,0:T(8,128)(2,1)} fusion(f32[2,16,256]{2,1,0:T(8,128)S(1)} %bitcast.233, f32[2,16,256,768]{3,2,1,0:T(8,128)} %get-tuple-element.122, f32[2,16,256]{2,1,0:T(8,128)S(1)} %copy-done.50, bf16[2,256,16,64]{1,3,2,0:T(8,128)(2,1)S(1)} %copy.39, bf16[2,768,2,16,64]{1,4,3,0,2:T(8,128)(2,1)} %pad_maximum_fusion.1), kind=kOutput, calls=%fused_computation.1 | convolution fusion | flops 836763648 | bytes 42008576 | tf_op jit(solution)/shard_map/bqhd,bkhd->bhqk/dot_general | solution.py:147
  217.0 10.2 %convolution_bitcast_fusion = f32[2,768,1,16,64]{1,4,3,0,2:T(8,128)} fusion(bf16[2,256,16,64]{1,3,2,0:T(8,128)(2,1)S(1)} %copy.39, bf16[2,16,256,768]{3,2,1,0:T(8,128)(2,1)} %fusion.6), kind=kOutput, calls=%fused_computation.30 | convolution fusion | flops 805306368 | bytes 19922944 | tf_op jit(solution)/shard_map/bhqk,bqhd->bkhd/dot_general | solution.py:144
  227.7 5.0 %convolution_bitcast_fusion.1 = f32[2,768,1,16,64]{1,4,3,0,2:T(8,128)} fusion(bf16[2,16,256,768]{3,2,1,0:T(8,128)(2,1)S(1)} %copy-done.2, bf16[2,256,1,16,64]{1,4,3,0,2:T(8,128)(2,1)S(1)} %copy-done.8), kind=kOutput, calls=%fused_computation.31 | convolution fusion | flops 805306368 | bytes 19922944 | tf_op jit(solution)/shard_map/bhqk,bqhd->bkhd/dot_general | solution.py:154
  232.6 8.5 %fusion.2 = bf16[2,768,2,16,64]{1,4,3,0,2:T(8,128)(2,1)} fusion(f32[2,768,1,16,64]{1,4,3,0,2:T(8,128)} %convolution_bitcast_fusion, f32[2,768,1,16,64]{1,4,3,0,2:T(8,128)} %convolution_bitcast_fusion.1), kind=kLoop, calls=%fused_computation.8 | loop fusion | flops 3145728 | bytes 18874368 | tf_op jit(solution)/shard_map/convert.1
  241.1 4.2 fusion.173
  246.7 6.8 %collective-permute-start.7 = (bf16[2,256,2,16,64]{1,4,3,0,2:T(8,128)(2,1)S(1)}, bf16[2,256,2,16,64]{1,4,3,0,2:T(8,128)(2,1)}, u32[]{:S(2)}, u32[]{:S(2)}) collective-permute-start(bf16[2,256,2,16,64]{1,4,3,0,2:T(8,128)(2,1)S(1)} %get-tuple-element.51), channel_id=1, source_target_pairs={{0,4},{4,8},{8,12},{12,16},{16,20},{20,24},{24,28},{28,32},{32,36}... | collective-permute-start | bytes 6291464 | tf_op jit(solution)/shard_map/ppermute | solution.py:45
  253.5 9.8 %fusion.101 = bf16[2,256,1,16,64]{1,4,3,0,2:T(8,128)(2,1)S(1)} fusion(bf16[2,16,256,768]{3,2,1,0:T(8,128)(2,1)} %multiply_convert_fusion, bf16[2,768,2,16,64]{1,4,3,0,2:T(8,128)(2,1)} %pad_maximum_fusion.1), kind=kOutput, calls=%fused_computation.185 | convolution fusion | flops 805830656 | bytes 16777216 | tf_op jit(solution)/shard_map/bhqk,bkhd->bqhd/dot_general | solution.py:151
  263.2 4.2 fusion.12
  267.7 3.3 copy.44
  272.3 6.4 %fusion.183 = f32[1024,3072]{1,0:T(8,128)} fusion(bf16[512,1024]{1,0:T(8,128)(2,1)S(1)} %bitcast.169, bf16[512,3072]{0,1:T(8,128)(2,1)S(1)} %bitcast.165), kind=kOutput, calls=%fused_computation.353 | convolution fusion | flops 3221225472 | bytes 16777216 | tf_op jit(solution)/shard_map/dot_general | solution.py:186
  280.2 3.0 add_convert_fusion
  283.2 48.1 %all-reduce.2.cloned.1.call-done = f32[31,1024]{1,0:T(8,128)} async-done(((f32[31,1024]{1,0:T(8,128)}), f32[31,1024]{1,0:T(8,128)}) %all-reduce.2.cloned.1.call-update) | async-done | bytes 126992 | tf_op jit(solution)/shard_map/psum | solution.py:188
  331.3 1.6 broadcast_multiply_fusion
  332.9 2.4 copy.42
  335.3 8.6 %fusion.30 = (f32[1024]{0:T(1024)S(1)}, f32[2,256]{1,0:T(2,128)S(1)}, f32[2,256]{1,0:T(2,128)S(1)}, f32[2,256,1024]{2,1,0:T(8,128)}) fusion(bf16[2,256,1024]{2,1,0:T(8,128)(2,1)S(1)} %copy-done.4, f32[2,256]{1,0:T(2,128)S(1)} %copy-done.52, f32[2,256]{1,0:T(2,128)S(1)} %copy-done.49, f32[1024]{0:T(1024)S(1)} %copy-done.94, ...), kind=kOutput, calls=%fused_computation.48 | convolution fusion | flops 3225942016 | bytes 12599296 | tf_op jit(solution)/shard_map/dot_general | solution.py:170
  344.0 65.0 %psum.15 = f32[1024]{0:T(1024)S(1)} all-reduce(f32[1024]{0:T(1024)S(1)} %get-tuple-element.37), channel_id=1, replica_groups=mesh['seq'=32,'dp'=4] {'seq','dp'}, use_global_device_ids=true, to_apply=%region_52.53 | all-reduce | flops 1024 | bytes 8192 | tf_op jit(solution)/shard_map/psum | solution.py:188
  409.6 11.9 %reduce-scatter.5.cloned.1.call-done = f32[32,3072]{1,0:T(8,128)} async-done(((f32[1024,3072]{1,0:T(8,128)}), f32[32,3072]{1,0:T(8,128)}) %reduce-scatter.5.cloned.1.call-update) | async-done | bytes 393232 | tf_op jit(solution)/shard_map/reduce_scatter | solution.py:28
  421.6 4.1 fusion.29
  425.7 18.4 %reduce-scatter.11.cloned.1.call-done = f32[8,1024]{1,0:T(8,128)} async-done(((f32[32,1024]{1,0:T(8,128)}), f32[8,1024]{1,0:T(8,128)}) %reduce-scatter.11.cloned.1.call-update) | async-done | bytes 32784 | tf_op jit(solution)/shard_map/reduce_scatter | solution.py:29
  445.5 22.1 %reduce-scatter.7.cloned.1.call-done = f32[8,3072]{1,0:T(8,128)} async-done(((f32[32,3072]{1,0:T(8,128)}), f32[8,3072]{1,0:T(8,128)}) %reduce-scatter.7.cloned.1.call-update) | async-done | bytes 98320 | tf_op jit(solution)/shard_map/reduce_scatter | solution.py:29
  467.5 1.5 broadcast_multiply_fusion.1
  (277 shorter events, 26.5 us)
Async XLA Ops:
  8.0 98.5 %copy-start = (bf16[1024,1024]{1,0:T(8,128)(2,1)S(1)}, bf16[1024,1024]{1,0:T(8,128)(2,1)}, u32[]{:S(2)}) copy-start(bf16[1024,1024]{1,0:T(8,128)(2,1)} %param.11) | copy-start | bytes 6291460
  8.0 3.3 copy-start.4
  8.0 3.3 copy-start.93
  8.0 323.3 %all-reduce.2.cloned.1.call-start = ((), (), s32[]{:S(2)}) async-start(), calls=%async_computation.8 | async-start | bytes 262144 | tf_op jit(solution)/shard_map/psum | solution.py:188
  39.9 20.7 %collective-permute-start.1 = (bf16[2,256,2,16,64]{1,4,3,0,2:T(8,128)(2,1)}, bf16[2,256,2,16,64]{1,4,3,0,2:T(8,128)(2,1)}, u32[]{:S(2)}, u32[]{:S(2)}) collective-permute-start(bf16[2,256,2,16,64]{1,4,3,0,2:T(8,128)(2,1)} %copy.52), channel_id=1, source_target_pairs={{4,0},{8,4},{12,8},{16,12},{20,16},{24,20},{28,24},{32,28},{36,32}... | collective-permute-start | bytes 6291464 | tf_op jit(solution)/shard_map/ppermute | solution.py:45
  41.2 19.4 %collective-permute-start = (bf16[2,256,2,16,64]{1,4,3,0,2:T(8,128)(2,1)}, bf16[2,256,2,16,64]{1,4,3,0,2:T(8,128)(2,1)}, u32[]{:S(2)}, u32[]{:S(2)}) collective-permute-start(bf16[2,256,2,16,64]{1,4,3,0,2:T(8,128)(2,1)} %copy.52), channel_id=1, source_target_pairs={{0,4},{4,8},{8,12},{12,16},{16,20},{20,24},{24,28},{28,32},{32,36}... | collective-permute-start | bytes 6291464 | tf_op jit(solution)/shard_map/ppermute | solution.py:45
  46.1 3.4 copy-start.104
  49.5 9.4 %copy-start.16 = (f32[31,1024]{1,0:T(8,128)S(1)}, f32[31,1024]{1,0:T(8,128)}, u32[]{:S(2)}) copy-start(f32[31,1024]{1,0:T(8,128)} %param.12) | copy-start | bytes 380932
  106.5 13.6 %copy-start.5 = (bf16[2,16,64,256]{3,2,1,0:T(8,128)(2,1)}, bf16[2,16,64,256]{3,2,1,0:T(8,128)(2,1)S(1)}, u32[]{:S(2)}) copy-start(bf16[2,16,64,256]{3,2,1,0:T(8,128)(2,1)S(1)} %fusion.98) | copy-start | bytes 3145732
  107.8 15.3 %copy-start.10 = (bf16[2,256,1024]{2,1,0:T(8,128)(2,1)}, bf16[2,256,1024]{2,1,0:T(8,128)(2,1)S(1)}, u32[]{:S(2)}) copy-start(bf16[2,256,1024]{2,1,0:T(8,128)(2,1)S(1)} %fusion.58) | copy-start | bytes 3145732
  107.9 14.9 %collective-permute-start.2 = (bf16[2,15,1024]{2,1,0:T(8,128)(2,1)S(1)}, bf16[2,15,1024]{2,1,0:T(8,128)(2,1)S(1)}, u32[]{:S(2)}, u32[]{:S(2)}) collective-permute-start(bf16[2,15,1024]{2,1,0:T(8,128)(2,1)S(1)} %get-tuple-element.55), channel_id=1, source_target_pairs={{0,4},{4,8},{8,12},{12,16},{16,20},{20,24},{24,28},{28,32},{32,36}... | collective-permute-start | bytes 184328 | tf_op jit(solution)/shard_map/ppermute | solution.py:21
  118.0 5.1 %collective-permute-start.3 = (bf16[2,15,1024]{2,1,0:T(8,128)(2,1)S(1)}, bf16[2,15,1024]{2,1,0:T(8,128)(2,1)S(1)}, u32[]{:S(2)}, u32[]{:S(2)}) collective-permute-start(bf16[2,15,1024]{2,1,0:T(8,128)(2,1)S(1)} %get-tuple-element.56), channel_id=1, source_target_pairs={{4,0},{8,4},{12,8},{16,12},{20,16},{24,20},{28,24},{32,28},{36,32}... | collective-permute-start | bytes 184328 | tf_op jit(solution)/shard_map/ppermute | solution.py:22
  146.8 5.3 %copy-start.77 = (pred[2,256]{1,0:T(4,128)(4,1)S(1)}, pred[2,256]{1,0:T(4,128)(4,1)}, u32[]{:S(2)}) copy-start(pred[2,256]{1,0:T(4,128)(4,1)} %get-tuple-element.108) | copy-start | bytes 1540
  146.8 5.3 %copy-start.79 = (pred[2,256]{1,0:T(4,128)(4,1)S(1)}, pred[2,256]{1,0:T(4,128)(4,1)}, u32[]{:S(2)}) copy-start(pred[2,256]{1,0:T(4,128)(4,1)} %get-tuple-element.109) | copy-start | bytes 1540
  146.8 5.3 %copy-start.85 = (pred[2,256]{1,0:T(4,128)(4,1)S(1)}, pred[2,256]{1,0:T(4,128)(4,1)}, u32[]{:S(2)}) copy-start(pred[2,256]{1,0:T(4,128)(4,1)} %get-tuple-element.104) | copy-start | bytes 1540
  146.8 5.3 %copy-start.87 = (pred[2,256]{1,0:T(4,128)(4,1)S(1)}, pred[2,256]{1,0:T(4,128)(4,1)}, u32[]{:S(2)}) copy-start(pred[2,256]{1,0:T(4,128)(4,1)} %get-tuple-element.105) | copy-start | bytes 1540
  146.8 5.3 %copy-start.89 = (pred[2,256]{1,0:T(4,128)(4,1)S(1)}, pred[2,256]{1,0:T(4,128)(4,1)}, u32[]{:S(2)}) copy-start(pred[2,256]{1,0:T(4,128)(4,1)} %get-tuple-element.106) | copy-start | bytes 1540
  146.8 5.3 %copy-start.91 = (pred[2,256]{1,0:T(4,128)(4,1)S(1)}, pred[2,256]{1,0:T(4,128)(4,1)}, u32[]{:S(2)}) copy-start(pred[2,256]{1,0:T(4,128)(4,1)} %get-tuple-element.107) | copy-start | bytes 1540
  152.1 10.9 %copy-start.69 = (pred[2,256]{1,0:T(4,128)(4,1)S(1)}, pred[2,256]{1,0:T(4,128)(4,1)}, u32[]{:S(2)}) copy-start(pred[2,256]{1,0:T(4,128)(4,1)} %get-tuple-element.88) | copy-start | bytes 1540
  152.1 10.9 %copy-start.71 = (pred[2,256]{1,0:T(4,128)(4,1)S(1)}, pred[2,256]{1,0:T(4,128)(4,1)}, u32[]{:S(2)}) copy-start(pred[2,256]{1,0:T(4,128)(4,1)} %get-tuple-element.89) | copy-start | bytes 1540
  152.1 10.9 %copy-start.73 = (pred[2,256]{1,0:T(4,128)(4,1)S(1)}, pred[2,256]{1,0:T(4,128)(4,1)}, u32[]{:S(2)}) copy-start(pred[2,256]{1,0:T(4,128)(4,1)} %get-tuple-element.90) | copy-start | bytes 1540
  152.1 10.9 %copy-start.75 = (pred[2,256]{1,0:T(4,128)(4,1)S(1)}, pred[2,256]{1,0:T(4,128)(4,1)}, u32[]{:S(2)}) copy-start(pred[2,256]{1,0:T(4,128)(4,1)} %get-tuple-element.91) | copy-start | bytes 1540
  156.7 8.4 %copy-start.9 = (bf16[2,256,1024]{2,1,0:T(8,128)(2,1)}, bf16[2,256,1024]{2,1,0:T(8,128)(2,1)S(1)}, u32[]{:S(2)}) copy-start(bf16[2,256,1024]{2,1,0:T(8,128)(2,1)S(1)} %get-tuple-element.52) | copy-start | bytes 3145732
  156.7 14.4 %collective-permute-start.4 = (bf16[2,15,1024]{2,1,0:T(8,128)(2,1)S(1)}, bf16[2,15,1024]{2,1,0:T(8,128)(2,1)S(1)}, u32[]{:S(2)}, u32[]{:S(2)}) collective-permute-start(bf16[2,15,1024]{2,1,0:T(8,128)(2,1)S(1)} %get-tuple-element.53), channel_id=1, source_target_pairs={{0,4},{4,8},{8,12},{12,16},{16,20},{20,24},{24,28},{28,32},{32,36}... | collective-permute-start | bytes 184328 | tf_op jit(solution)/shard_map/ppermute | solution.py:21
  161.7 9.4 %collective-permute-start.5 = (bf16[2,15,1024]{2,1,0:T(8,128)(2,1)S(1)}, bf16[2,15,1024]{2,1,0:T(8,128)(2,1)S(1)}, u32[]{:S(2)}, u32[]{:S(2)}) collective-permute-start(bf16[2,15,1024]{2,1,0:T(8,128)(2,1)S(1)} %get-tuple-element.54), channel_id=1, source_target_pairs={{4,0},{8,4},{12,8},{16,12},{20,16},{24,20},{28,24},{32,28},{36,32}... | collective-permute-start | bytes 184328 | tf_op jit(solution)/shard_map/ppermute | solution.py:22
  170.6 2.3 copy-start.54
  170.6 2.3 copy-start.56
  170.6 2.3 copy-start.58
  170.6 2.3 copy-start.60
  170.6 2.3 copy-start.62
  170.6 173.3 %reduce-scatter.9.cloned.1.call-start = ((), (), s32[]{:S(2)}) async-start(), calls=%async_computation.6 | async-start | bytes 4325376 | tf_op jit(solution)/shard_map/reduce_scatter | solution.py:28
  170.9 2.0 copy-start.12
  170.9 2.0 copy-start.64
  170.9 2.0 copy-start.66
  170.9 2.0 copy-start.68
  195.8 4.9 %copy-start.6 = (bf16[2,16,64,256]{3,2,1,0:T(8,128)(2,1)S(1)}, bf16[2,16,64,256]{3,2,1,0:T(8,128)(2,1)}, u32[]{:S(2)}) copy-start(bf16[2,16,64,256]{3,2,1,0:T(8,128)(2,1)} %copy-done.5) | copy-start | bytes 3145732
  201.1 220.4 %reduce-scatter.5.cloned.1.call-start = ((), (), s32[]{:S(2)}) async-start(), calls=%async_computation.4 | async-start | bytes 12976128 | tf_op jit(solution)/shard_map/reduce_scatter | solution.py:28
  217.0 10.2 %copy-start.2 = (bf16[2,16,256,768]{3,2,1,0:T(8,128)(2,1)S(1)}, bf16[2,16,256,768]{3,2,1,0:T(8,128)(2,1)}, u32[]{:S(2)}) copy-start(bf16[2,16,256,768]{3,2,1,0:T(8,128)(2,1)} %multiply_convert_fusion) | copy-start | bytes 37748740
  217.0 10.7 %copy-start.8 = (bf16[2,256,1,16,64]{1,4,3,0,2:T(8,128)(2,1)S(1)}, bf16[2,256,1,16,64]{1,4,3,0,2:T(8,128)(2,1)}, u32[]{:S(2)}) copy-start(bf16[2,256,1,16,64]{1,4,3,0,2:T(8,128)(2,1)} %copy.53) | copy-start | bytes 3145732
  245.4 17.9 %collective-permute-start.6 = (bf16[2,256,2,16,64]{1,4,3,0,2:T(8,128)(2,1)}, bf16[2,256,2,16,64]{1,4,3,0,2:T(8,128)(2,1)S(1)}, u32[]{:S(2)}, u32[]{:S(2)}) collective-permute-start(bf16[2,256,2,16,64]{1,4,3,0,2:T(8,128)(2,1)} %get-tuple-element.50), channel_id=1, source_target_pairs={{4,0},{8,4},{12,8},{16,12},{20,16},{24,20},{28,24},{32,28},{36,32}... | collective-permute-start | bytes 6291464 | tf_op jit(solution)/shard_map/ppermute | solution.py:45
  246.7 16.6 %collective-permute-start.7 = (bf16[2,256,2,16,64]{1,4,3,0,2:T(8,128)(2,1)S(1)}, bf16[2,256,2,16,64]{1,4,3,0,2:T(8,128)(2,1)}, u32[]{:S(2)}, u32[]{:S(2)}) collective-permute-start(bf16[2,256,2,16,64]{1,4,3,0,2:T(8,128)(2,1)S(1)} %get-tuple-element.51), channel_id=1, source_target_pairs={{0,4},{4,8},{8,12},{12,16},{16,20},{20,24},{24,28},{28,32},{32,36}... | collective-permute-start | bytes 6291464 | tf_op jit(solution)/shard_map/ppermute | solution.py:45
  267.7 3.3 copy-start.3
  278.7 165.4 %reduce-scatter.11.cloned.1.call-start = ((), (), s32[]{:S(2)}) async-start(), calls=%async_computation.7 | async-start | bytes 163840 | tf_op jit(solution)/shard_map/reduce_scatter | solution.py:29
  332.9 2.4 copy-start.49
  332.9 2.4 copy-start.52
  332.9 2.4 copy-start.94
  343.9 123.6 %reduce-scatter.7.cloned.1.call-start = ((), (), s32[]{:S(2)}) async-start(), calls=%async_computation.5 | async-start | bytes 491520 | tf_op jit(solution)/shard_map/reduce_scatter | solution.py:29
  421.6 47.5 %copy-start.1 = (bf16[1024,1024]{1,0:T(8,128)(2,1)S(1)}, bf16[1024,1024]{1,0:T(8,128)(2,1)}, u32[]{:S(2)}) copy-start(bf16[1024,1024]{1,0:T(8,128)(2,1)} %param.11) | copy-start | bytes 6291460
  (70 other events, 103.4 us)
Sparse Core Ops, SparseCore 0:
  170.7 160.5 all-reduce.1
Sparse Core Ops, SparseCore 1:
  201.2 112.8 reduce-scatter.8
  317.8 103.7 reduce-scatter.4
  423.8 20.2 reduce-scatter.10
  446.5 21.0 reduce-scatter.6

commit v3 on v2

--- a/solution.py
+++ b/solution.py
@@ -177,20 +177,28 @@
     )
     gain_sum = jnp.sum(grad_normed * unit_rows, axis=(0, 1))
     contract_rows = (((0,), (0,)), ((), ()))
-    out_sum = staged_scatter(
-        lax.dot_general(
-            flat_attended, flat_grad_hidden, contract_rows, preferred_element_type=jnp.float32
-        )
-    )
-    qkv_sum = staged_scatter(
-        lax.dot_general(flat_normed, flat_grad_qkv, contract_rows, preferred_element_type=jnp.float32)
+    summed = staged_scatter(
+        jnp.concatenate(
+            [
+                lax.dot_general(
+                    flat_normed, flat_grad_qkv, contract_rows, preferred_element_type=jnp.float32
+                ),
+                lax.dot_general(
+                    flat_attended,
+                    flat_grad_hidden,
+                    contract_rows,
+                    preferred_element_type=jnp.float32,
+                ),
+            ],
+            axis=1,
+        )
     )
     small_sums = lax.psum((jnp.stack(kernel_rows), gain_sum), ("seq", "dp"))
     return (
         output,
         grad_inputs.astype(jnp.bfloat16),
-        qkv_sum * factor,
-        out_sum * factor,
+        summed[:, : 3 * model_width] * factor,
+        summed[:, 3 * model_width :] * factor,
         small_sums[0] * factor,
         small_sums[1] * factor,
     )

time: 482 us -> 518 us (1.075)
  waiting for transfers between devices: 101 us -> 142 us
    psum x1, waiting for transfers between devices: 48.1 us -> 125 us  [local(): small_sums = lax.psum((jnp.stack(kernel_rows), gain_sum), ('seq', 'dp'))]
    reduce_scatter x2 -> x1, waiting for transfers between devices: 40.4 us -> 14.5 us  [staged_scatter(): return lax.psum_scatter(partial, 'dp', scatter_dimension=0, tiled=True)]
    reduce_scatter x2 -> x1, waiting for transfers between devices: 12 us -> 0.03 us  [staged_scatter(): partial = lax.psum_scatter(partial, 'seq', scatter_dimension=0, tiled=True)]
    concatenate x0 -> x1, other arithmetic: none -> 6.04 us  [local(): jnp.concatenate([lax.dot_general(flat_normed, flat_grad_qkv, contract_row...]
    unnamed x214 -> x178, local copies, waits for them, and re-layouts: 17.1 us -> 15.3 us
  transfers between devices with their start and end apart: 13 -> 11, of which waited for: 5 -> 4; matrix products, arithmetic and copies ran while one was open for 30% -> 15% of each run, Pallas kernels for 0% -> 0%
where the time goes in v3:
time: 518 us; the launch traced here: 513 us
  waiting for transfers between devices  142 us (27%)
  other arithmetic  105 us (20%)
  matrix products  97.7 us (19%)
  blocking collectives  63.2 us (12%)
  local copies, waits for them, and re-layouts  54.8 us (11%)
  starting transfers between devices  33.1 us (6%)
  between operations  17.4 us (3%)
    psum x1, waiting for transfers between devices, local(): small_sums = lax.psum((jnp.stack(kernel_rows), gain_sum), ('seq', 'dp'))  125 us
    psum x1, blocking collectives, local(): small_sums = lax.psum((jnp.stack(kernel_rows), gain_sum), ('seq', 'dp'))  63.2 us
    reduce_sum x4, other arithmetic, local(): jnp.sum(jnp.where(same_seg, grad_conv * padded[:, tap_index:tap_index + f...  32.5 us
    sub x1, matrix products, local(): exponent = jnp.where(allowed, jnp.exp(scores - row_max), 0.0)  17.3 us
    ppermute x2, starting transfers between devices, with_halo(): before = lax.ppermute(last, axis, up)  15.4 us
    unnamed x178, local copies, waits for them, and re-layouts  15.3 us
    dot_general x1, matrix products, local(): jnp.einsum('bqhd,bkhd->bhqk', grad_heads, head_values, preferred_element_...  15.1 us
    reduce_scatter x1, waiting for transfers between devices, staged_scatter(): return lax.psum_scatter(partial, 'dp', scatter_dimension=0, tiled=True)  14.5 us
  transfers between devices with their start and end apart: 11, of which 4 were waited for; matrix products, arithmetic and copies ran while one was open for 15% of the time, Pallas kernels for 0%

profile of v3, /device:TPU:0, one launch (start us, length us, event | category | flops | bytes accessed | tf_op | source)
XLA Modules:
  0.0 512.8 jit_solution(2896854392377700394)
XLA Ops:
  8.1 1.6 convert_reduce_fusion
  9.7 1.6 fusion.31
  12.9 7.6 %convolution_convert_fusion = bf16[512,3072]{1,0:T(8,128)(2,1)} fusion(bf16[512,1024]{1,0:T(8,128)(2,1)S(1)} %bitcast.168, bf16[1024,3072]{1,0:T(8,128)(2,1)} %param.10), kind=kOutput, calls=%fused_computation.18 | convolution fusion | flops 3222798336 | bytes 10485760 | tf_op jit(solution)/shard_map/dot_general | solution.py:69
  20.5 8.6 %reshape.278 = bf16[2,256,3,16,64]{4,3,2,1,0:T(8,128)(2,1)} reshape(bf16[512,3072]{1,0:T(8,128)(2,1)} %convolution_convert_fusion) | data formatting | bytes 6291456 | tf_op jit(solution)/shard_map/reshape;reshape | solution.py:73
  29.1 4.9 slice.686
  34.1 5.8 %copy.56 = bf16[2,256,2,16,64]{1,4,3,0,2:T(8,128)(2,1)} copy(bf16[2,256,2,16,64]{4,3,2,1,0:T(8,128)(2,1)} %slice.686) | data formatting | bytes 4194304
  41.2 4.6 collective-permute-start
  45.8 3.4 slice.688
  50.0 3.6 copy.57
  60.2 5.9 %pad_maximum_fusion.2 = bf16[2,768,2,16,64]{1,4,3,0,2:T(8,128)(2,1)} fusion(bf16[2,256,2,16,64]{1,4,3,0,2:T(8,128)(2,1)} %collective-permute-done.1, bf16[2,256,2,16,64]{1,4,3,0,2:T(8,128)(2,1)} %copy.56, bf16[2,256,2,16,64]{1,4,3,0,2:T(8,128)(2,1)} %collective-permute-done), kind=kLoop, calls=%fused_computation.15 | loop fusion | flops 18874368 | bytes 12582912 | tf_op jit(solution)/shard_map/concatenate | solution.py:76
  66.1 17.3 %fusion.178 = (f32[2,16,256]{2,1,0:T(8,128)}, f32[2,16,256,768]{3,2,1,0:T(8,128)}) fusion(pred[2,256,768]{2,1,0:T(8,128)(4,1)S(1)} %broadcast_compare_fusion, bf16[2,768,2,16,64]{1,4,3,0,2:T(8,128)(2,1)} %pad_maximum_fusion.2, bf16[2,256,1,16,64]{1,4,3,0,2:T(8,128)(2,1)} %copy.57), kind=kOutput, calls=%fused_computation.353 | convolution fusion | flops 836764416 | bytes 30179328 | tf_op jit(solution)/shard_map/sub | solution.py:92
  83.4 13.3 %fusion.6 = bf16[2,16,256,768]{3,2,1,0:T(8,128)(2,1)} fusion(f32[2,16,256,768]{3,2,1,0:T(8,128)} %get-tuple-element.122, f32[2,16,256]{2,1,0:T(8,128)} %get-tuple-element.121), kind=kLoop, calls=%fused_computation.14 | loop fusion | flops 12582912 | bytes 37781504 | tf_op jit(solution)/shard_map/convert_element_type | solution.py:94
  96.7 9.4 %fusion.98 = bf16[2,16,64,256]{3,2,1,0:T(8,128)(2,1)S(1)} fusion(bf16[2,16,256,768]{3,2,1,0:T(8,128)(2,1)} %fusion.6, bf16[2,768,2,16,64]{1,4,3,0,2:T(8,128)(2,1)} %pad_maximum_fusion.2), kind=kOutput, calls=%fused_computation.185 | convolution fusion | flops 805830656 | bytes 16777216 | tf_op jit(solution)/shard_map/bhqk,bkhd->bqhd/dot_general | solution.py:95
  107.5 10.5 %collective-permute-start.2 = (bf16[2,15,1024]{2,1,0:T(8,128)(2,1)S(1)}, bf16[2,15,1024]{2,1,0:T(8,128)(2,1)S(1)}, u32[]{:S(2)}, u32[]{:S(2)}) collective-permute-start(bf16[2,15,1024]{2,1,0:T(8,128)(2,1)S(1)} %get-tuple-element.55), channel_id=1, source_target_pairs={{0,4},{4,8},{8,12},{12,16},{16,20},{20,24},{24,28},{28,32},{32,36}... | collective-permute-start | bytes 184328 | tf_op jit(solution)/shard_map/ppermute | solution.py:21
  118.0 1.7 collective-permute-start.3
  123.9 22.4 %select_reduce_fusion = (f32[1024]{0:T(1024)S(1)}, f32[1024]{0:T(1024)S(1)}, f32[1024]{0:T(1024)S(1)}, f32[1024]{0:T(1024)S(1)}, f32[1024]{0:T(1024)S(1)}, /*ind...) fusion(f32[2,286,1024]{2,1,0:T(8,128)S(1)} %maximum_convert_fus, ...), kind=kLoop, calls=%fused_computation.147 | loop fusion | flops 67099648 | bytes 70434304 | tf_op jit(solution)/shard_map/reduce_sum | solution.py:130
  146.4 4.9 select_reduce_fusion.9
  151.3 4.9 collective-permute-start.4
  156.2 1.5 collective-permute-start.5
  157.7 1.4 select_reduce_fusion.27
  160.9 12.5 %fusion.171 = (bf16[2,256,1024]{2,1,0:T(8,128)(2,1)S(1)}, f32[2,256,1024]{2,1,0:T(8,128)}) fusion(f32[2,286,1024]{2,1,0:T(8,128)S(1)} %maximum_convert_fusion.1, f32[1024]{0:T(1024)S(1)} %bitcast.192, pred[2,256]{1,0:T(4,128)(4,1)S(1)} %copy-done.68, f32[1024]{0:T(1024)S(1)} %bitcast.194, pred[2,256]{1,0:T(4,128)(4,1)S(1)} %copy-done.69, ...), kind=kLoop, calls=%fused_computation.347 | loop fusion | flops 49807360 | bytes 69348864 | tf_op jit(solution)/shard_map/convert_element_type | solution.py:135
  173.4 2.3 convolution_convert_fusion.1
  175.7 4.0 reshape.279
  179.7 2.8 copy.41
  182.5 9.5 %convolution_bitcast_fusion = f32[2,768,1,16,64]{1,4,3,0,2:T(8,128)} fusion(bf16[2,256,16,64]{1,3,2,0:T(8,128)(2,1)S(1)} %copy.41, bf16[2,16,256,768]{3,2,1,0:T(8,128)(2,1)} %fusion.6), kind=kOutput, calls=%fused_computation.31 | convolution fusion | flops 805306368 | bytes 19922944 | tf_op jit(solution)/shard_map/bhqk,bqhd->bkhd/dot_general | solution.py:144
  192.8 15.1 %multiply_convert_fusion = bf16[2,16,256,768]{3,2,1,0:T(8,128)(2,1)} fusion(f32[2,16,256]{2,1,0:T(8,128)S(1)} %bitcast.233, f32[2,16,256,768]{3,2,1,0:T(8,128)} %get-tuple-element.122, f32[2,16,256]{2,1,0:T(8,128)S(1)} %copy-done.53, bf16[2,256,16,64]{1,3,2,0:T(8,128)(2,1)S(1)} %copy.41, bf16[2,768,2,16,64]{1,4,3,0,2:T(8,128)(2,1)} %pad_maximum_fusion.2), kind=kOutput, calls=%fused_computation.1 | convolution fusion | flops 836763648 | bytes 42008576 | tf_op jit(solution)/shard_map/bqhd,bkhd->bhqk/dot_general | solution.py:147
  207.9 9.5 %convolution_bitcast_fusion.1 = f32[2,768,1,16,64]{1,4,3,0,2:T(8,128)} fusion(bf16[2,16,256,768]{3,2,1,0:T(8,128)(2,1)} %multiply_convert_fusion, bf16[2,256,1,16,64]{1,4,3,0,2:T(8,128)(2,1)S(1)} %copy-done.12), kind=kOutput, calls=%fused_computation.32 | convolution fusion | flops 805306368 | bytes 19922944 | tf_op jit(solution)/shard_map/bhqk,bqhd->bkhd/dot_general | solution.py:154
  217.5 8.2 %fusion.2 = bf16[2,768,2,16,64]{1,4,3,0,2:T(8,128)(2,1)} fusion(f32[2,768,1,16,64]{1,4,3,0,2:T(8,128)} %convolution_bitcast_fusion, f32[2,768,1,16,64]{1,4,3,0,2:T(8,128)} %convolution_bitcast_fusion.1), kind=kLoop, calls=%fused_computation.9 | loop fusion | flops 3145728 | bytes 18874368 | tf_op jit(solution)/shard_map/convert.1
  225.7 5.0 fusion.173
  231.9 6.8 %collective-permute-start.7 = (bf16[2,256,2,16,64]{1,4,3,0,2:T(8,128)(2,1)}, bf16[2,256,2,16,64]{1,4,3,0,2:T(8,128)(2,1)}, u32[]{:S(2)}, u32[]{:S(2)}) collective-permute-start(bf16[2,256,2,16,64]{1,4,3,0,2:T(8,128)(2,1)} %get-tuple-element.51), channel_id=1, source_target_pairs={{0,4},{4,8},{8,12},{12,16},{16,20},{20,24},{24,28},{28,32},{32,36}... | collective-permute-start | bytes 6291464 | tf_op jit(solution)/shard_map/ppermute | solution.py:45
  238.7 3.8 select_reduce_fusion.18
  242.5 2.7 stack.157
  245.5 4.5 fusion.184
  250.0 9.4 %fusion.101 = bf16[2,256,1,16,64]{1,4,3,0,2:T(8,128)(2,1)S(1)} fusion(bf16[2,16,256,768]{3,2,1,0:T(8,128)(2,1)} %multiply_convert_fusion, bf16[2,768,2,16,64]{1,4,3,0,2:T(8,128)(2,1)} %pad_maximum_fusion.2), kind=kOutput, calls=%fused_computation.186 | convolution fusion | flops 805830656 | bytes 16777216 | tf_op jit(solution)/shard_map/bhqk,bkhd->bqhd/dot_general | solution.py:151
  259.4 4.6 fusion.12
  264.3 3.3 copy.46
  268.9 3.5 fusion.183
  272.4 6.0 %pad_maximum_fusion = f32[1024,4096]{1,0:T(8,128)} fusion(f32[1024,1024]{1,0:T(8,128)S(1)} %copy-done.16, f32[1024,3072]{1,0:T(8,128)S(1)} %fusion.183), kind=kLoop, calls=%fused_computation.5 | loop fusion | flops 4194304 | bytes 33554432 | tf_op jit(solution)/shard_map/concatenate | solution.py:181
  280.3 1.7 add_convert_fusion
  282.0 125.4 %all-reduce.2.cloned.1.call-done = f32[31,1024]{1,0:T(8,128)} async-done(((f32[31,1024]{1,0:T(8,128)}), f32[31,1024]{1,0:T(8,128)}) %all-reduce.2.cloned.1.call-update) | async-done | bytes 126992 | tf_op jit(solution)/shard_map/psum | solution.py:196
  407.4 1.6 broadcast_multiply_fusion
  409.0 2.3 copy.44
  411.3 8.2 %fusion.30 = (f32[1024]{0:T(1024)S(1)}, f32[2,256]{1,0:T(2,128)S(1)}, f32[2,256]{1,0:T(2,128)S(1)}, f32[2,256,1024]{2,1,0:T(8,128)}) fusion(bf16[2,256,1024]{2,1,0:T(8,128)(2,1)S(1)} %copy-done.8, f32[2,256]{1,0:T(2,128)S(1)} %copy-done.55, f32[2,256]{1,0:T(2,128)S(1)} %copy-done.52, f32[1024]{0:T(1024)S(1)} %copy-done.79, ...), kind=kOutput, calls=%fused_computation.49 | convolution fusion | flops 3225942016 | bytes 12599296 | tf_op jit(solution)/shard_map/dot_general | solution.py:170
  419.5 63.2 %psum.15 = f32[1024]{0:T(1024)S(1)} all-reduce(f32[1024]{0:T(1024)S(1)} %get-tuple-element.37), channel_id=1, replica_groups=mesh['seq'=32,'dp'=4] {'seq','dp'}, use_global_device_ids=true, to_apply=%region_50.51 | all-reduce | flops 1024 | bytes 8192 | tf_op jit(solution)/shard_map/psum | solution.py:196
  483.4 4.1 fusion.29
  487.5 14.5 %reduce-scatter.5.cloned.1.call-done = f32[8,4096]{1,0:T(8,128)} async-done(((f32[32,4096]{1,0:T(8,128)}), f32[8,4096]{1,0:T(8,128)}) %reduce-scatter.5.cloned.1.call-update) | async-done | bytes 131088 | tf_op jit(solution)/shard_map/reduce_scatter | solution.py:29
  502.0 1.4 slice_multiply_fusion.32
  503.4 1.5 slice_multiply_fusion.31
  (236 shorter events, 23.0 us)
Async XLA Ops:
  8.0 98.1 %copy-start = (bf16[1024,1024]{1,0:T(8,128)(2,1)S(1)}, bf16[1024,1024]{1,0:T(8,128)(2,1)}, u32[]{:S(2)}) copy-start(bf16[1024,1024]{1,0:T(8,128)(2,1)} %param.11) | copy-start | bytes 6291460
  8.0 3.3 copy-start.7
  8.0 3.3 copy-start.78
  8.0 399.4 %all-reduce.2.cloned.1.call-start = ((), (), s32[]{:S(2)}) async-start(), calls=%async_computation.4 | async-start | bytes 262144 | tf_op jit(solution)/shard_map/psum | solution.py:196
  39.9 20.3 %collective-permute-start.1 = (bf16[2,256,2,16,64]{1,4,3,0,2:T(8,128)(2,1)}, bf16[2,256,2,16,64]{1,4,3,0,2:T(8,128)(2,1)}, u32[]{:S(2)}, u32[]{:S(2)}) collective-permute-start(bf16[2,256,2,16,64]{1,4,3,0,2:T(8,128)(2,1)} %copy.56), channel_id=1, source_target_pairs={{4,0},{8,4},{12,8},{16,12},{20,16},{24,20},{28,24},{32,28},{36,32}... | collective-permute-start | bytes 6291464 | tf_op jit(solution)/shard_map/ppermute | solution.py:45
  41.2 19.0 %collective-permute-start = (bf16[2,256,2,16,64]{1,4,3,0,2:T(8,128)(2,1)}, bf16[2,256,2,16,64]{1,4,3,0,2:T(8,128)(2,1)}, u32[]{:S(2)}, u32[]{:S(2)}) collective-permute-start(bf16[2,256,2,16,64]{1,4,3,0,2:T(8,128)(2,1)} %copy.56), channel_id=1, source_target_pairs={{0,4},{4,8},{8,12},{12,16},{16,20},{20,24},{24,28},{28,32},{32,36}... | collective-permute-start | bytes 6291464 | tf_op jit(solution)/shard_map/ppermute | solution.py:45
  45.8 3.4 copy-start.86
  49.2 9.3 %copy-start.19 = (f32[31,1024]{1,0:T(8,128)S(1)}, f32[31,1024]{1,0:T(8,128)}, u32[]{:S(2)}) copy-start(f32[31,1024]{1,0:T(8,128)} %param.12) | copy-start | bytes 380932
  106.1 13.7 %copy-start.9 = (bf16[2,16,64,256]{3,2,1,0:T(8,128)(2,1)}, bf16[2,16,64,256]{3,2,1,0:T(8,128)(2,1)S(1)}, u32[]{:S(2)}) copy-start(bf16[2,16,64,256]{3,2,1,0:T(8,128)(2,1)S(1)} %fusion.98) | copy-start | bytes 3145732
  107.4 15.7 %copy-start.13 = (bf16[2,256,1024]{2,1,0:T(8,128)(2,1)}, bf16[2,256,1024]{2,1,0:T(8,128)(2,1)S(1)}, u32[]{:S(2)}) copy-start(bf16[2,256,1024]{2,1,0:T(8,128)(2,1)S(1)} %fusion.58) | copy-start | bytes 3145732
  107.5 15.1 %collective-permute-start.2 = (bf16[2,15,1024]{2,1,0:T(8,128)(2,1)S(1)}, bf16[2,15,1024]{2,1,0:T(8,128)(2,1)S(1)}, u32[]{:S(2)}, u32[]{:S(2)}) collective-permute-start(bf16[2,15,1024]{2,1,0:T(8,128)(2,1)S(1)} %get-tuple-element.55), channel_id=1, source_target_pairs={{0,4},{4,8},{8,12},{12,16},{16,20},{20,24},{24,28},{28,32},{32,36}... | collective-permute-start | bytes 184328 | tf_op jit(solution)/shard_map/ppermute | solution.py:21
  118.0 5.1 %collective-permute-start.3 = (bf16[2,15,1024]{2,1,0:T(8,128)(2,1)S(1)}, bf16[2,15,1024]{2,1,0:T(8,128)(2,1)S(1)}, u32[]{:S(2)}, u32[]{:S(2)}) collective-permute-start(bf16[2,15,1024]{2,1,0:T(8,128)(2,1)S(1)} %get-tuple-element.56), channel_id=1, source_target_pairs={{4,0},{8,4},{12,8},{16,12},{20,16},{24,20},{28,24},{32,28},{36,32}... | collective-permute-start | bytes 184328 | tf_op jit(solution)/shard_map/ppermute | solution.py:22
  123.5 34.1 %copy-start.2 = (f32[2,286,1024]{2,1,0:T(8,128)}, f32[2,286,1024]{2,1,0:T(8,128)S(1)}, u32[]{:S(2)}) copy-start(f32[2,286,1024]{2,1,0:T(8,128)S(1)} %maximum_convert_fusion) | copy-start | bytes 7028740
  146.3 11.3 %copy-start.4 = (f32[2,256,1024]{2,1,0:T(8,128)}, f32[2,256,1024]{2,1,0:T(8,128)S(1)}, u32[]{:S(2)}) copy-start(f32[2,256,1024]{2,1,0:T(8,128)S(1)} %get-tuple-element.46) | copy-start | bytes 6291460
  146.4 11.3 %copy-start.68 = (pred[2,256]{1,0:T(4,128)(4,1)S(1)}, pred[2,256]{1,0:T(4,128)(4,1)}, u32[]{:S(2)}) copy-start(pred[2,256]{1,0:T(4,128)(4,1)} %get-tuple-element.88) | copy-start | bytes 1540
  146.4 11.3 %copy-start.69 = (pred[2,256]{1,0:T(4,128)(4,1)S(1)}, pred[2,256]{1,0:T(4,128)(4,1)}, u32[]{:S(2)}) copy-start(pred[2,256]{1,0:T(4,128)(4,1)} %get-tuple-element.89) | copy-start | bytes 1540
  146.4 11.3 %copy-start.70 = (pred[2,256]{1,0:T(4,128)(4,1)S(1)}, pred[2,256]{1,0:T(4,128)(4,1)}, u32[]{:S(2)}) copy-start(pred[2,256]{1,0:T(4,128)(4,1)} %get-tuple-element.90) | copy-start | bytes 1540
  146.4 11.3 %copy-start.71 = (pred[2,256]{1,0:T(4,128)(4,1)S(1)}, pred[2,256]{1,0:T(4,128)(4,1)}, u32[]{:S(2)}) copy-start(pred[2,256]{1,0:T(4,128)(4,1)} %get-tuple-element.91) | copy-start | bytes 1540
  151.3 8.0 %collective-permute-start.4 = (bf16[2,15,1024]{2,1,0:T(8,128)(2,1)S(1)}, bf16[2,15,1024]{2,1,0:T(8,128)(2,1)S(1)}, u32[]{:S(2)}, u32[]{:S(2)}) collective-permute-start(bf16[2,15,1024]{2,1,0:T(8,128)(2,1)S(1)} %get-tuple-element.53), channel_id=1, source_target_pairs={{0,4},{4,8},{8,12},{12,16},{16,20},{20,24},{24,28},{28,32},{32,36}... | collective-permute-start | bytes 184328 | tf_op jit(solution)/shard_map/ppermute | solution.py:21
  156.2 4.3 collective-permute-start.5
  159.1 1.7 copy-start.64
  159.1 1.7 copy-start.65
  159.1 1.7 copy-start.66
  159.1 1.7 copy-start.67
  159.2 1.7 copy-start.72
  159.2 1.7 copy-start.73
  159.2 1.7 copy-start.74
  159.2 1.7 copy-start.75
  159.2 1.7 copy-start.76
  159.2 1.7 copy-start.77
  159.2 1.7 copy-start.80
  159.2 1.7 copy-start.81
  182.5 9.5 %copy-start.10 = (bf16[2,16,64,256]{3,2,1,0:T(8,128)(2,1)S(1)}, bf16[2,16,64,256]{3,2,1,0:T(8,128)(2,1)}, u32[]{:S(2)}) copy-start(bf16[2,16,64,256]{3,2,1,0:T(8,128)(2,1)} %copy-done.9) | copy-start | bytes 3145732
  192.8 15.1 %copy-start.12 = (bf16[2,256,1,16,64]{1,4,3,0,2:T(8,128)(2,1)S(1)}, bf16[2,256,1,16,64]{1,4,3,0,2:T(8,128)(2,1)}, u32[]{:S(2)}) copy-start(bf16[2,256,1,16,64]{1,4,3,0,2:T(8,128)(2,1)} %copy.57) | copy-start | bytes 3145732
  225.7 13.0 %copy-start.3 = (f32[2,286,1024]{2,1,0:T(8,128)S(1)}, f32[2,286,1024]{2,1,0:T(8,128)}, u32[]{:S(2)}) copy-start(f32[2,286,1024]{2,1,0:T(8,128)} %copy-done.2) | copy-start | bytes 7028740
  225.7 13.0 %copy-start.5 = (f32[2,256,1024]{2,1,0:T(8,128)S(1)}, f32[2,256,1024]{2,1,0:T(8,128)}, u32[]{:S(2)}) copy-start(f32[2,256,1024]{2,1,0:T(8,128)} %copy-done.4) | copy-start | bytes 6291460
  230.6 28.8 %collective-permute-start.6 = (bf16[2,256,2,16,64]{1,4,3,0,2:T(8,128)(2,1)}, bf16[2,256,2,16,64]{1,4,3,0,2:T(8,128)(2,1)}, u32[]{:S(2)}, u32[]{:S(2)}) collective-permute-start(bf16[2,256,2,16,64]{1,4,3,0,2:T(8,128)(2,1)} %get-tuple-element.50), channel_id=1, source_target_pairs={{4,0},{8,4},{12,8},{16,12},{20,16},{24,20},{28,24},{32,28},{36,32}... | collective-permute-start | bytes 6291464 | tf_op jit(solution)/shard_map/ppermute | solution.py:45
  231.9 27.5 %collective-permute-start.7 = (bf16[2,256,2,16,64]{1,4,3,0,2:T(8,128)(2,1)}, bf16[2,256,2,16,64]{1,4,3,0,2:T(8,128)(2,1)}, u32[]{:S(2)}, u32[]{:S(2)}) collective-permute-start(bf16[2,256,2,16,64]{1,4,3,0,2:T(8,128)(2,1)} %get-tuple-element.51), channel_id=1, source_target_pairs={{0,4},{4,8},{8,12},{12,16},{16,20},{20,24},{24,28},{28,32},{32,36}... | collective-permute-start | bytes 6291464 | tf_op jit(solution)/shard_map/ppermute | solution.py:45
  245.2 237.6 %reduce-scatter.3.cloned.1.call-start = ((), (), s32[]{:S(2)}) async-start(), calls=%async_computation.2 | async-start | bytes 17301504 | tf_op jit(solution)/shard_map/reduce_scatter | solution.py:28
  264.3 3.3 copy-start.6
  268.9 3.5 copy-start.16
  278.4 1.9 copy-start.14
  278.5 223.6 %reduce-scatter.5.cloned.1.call-start = ((), (), s32[]{:S(2)}) async-start(), calls=%async_computation.3 | async-start | bytes 655360 | tf_op jit(solution)/shard_map/reduce_scatter | solution.py:29
  409.0 2.3 copy-start.8
  409.0 2.3 copy-start.52
  409.0 2.3 copy-start.55
  409.0 2.3 copy-start.79
  483.4 21.5 %copy-start.1 = (bf16[1024,1024]{1,0:T(8,128)(2,1)S(1)}, bf16[1024,1024]{1,0:T(8,128)(2,1)}, u32[]{:S(2)}) copy-start(bf16[1024,1024]{1,0:T(8,128)(2,1)} %param.11) | copy-start | bytes 6291460
  (50 other events, 66.7 us)
Sparse Core Ops, SparseCore 0:
  245.3 162.0 all-reduce.1
Sparse Core Ops, SparseCore 1:
  278.5 132.0 reduce-scatter.2
  482.9 19.1 reduce-scatter.4

commit v4 on v3

--- a/solution.py
+++ b/solution.py
@@ -22,6 +22,19 @@
         after = lax.ppermute(initial, axis, down)
         shard = jnp.concatenate([before, shard, after], axis=dim)
     return shard
+
+
+def exchange_sum(value, axes):
+    for axis in axes:
+        size = lax.axis_size(axis)
+        if size & (size - 1):
+            value = lax.psum(value, axis)
+            continue
+        bit = 1
+        while bit < size:
+            value = value + lax.ppermute(value, axis, [(i, i ^ bit) for i in range(size)])
+            bit *= 2
+    return value
 
 
 def staged_scatter(partial):
@@ -193,7 +206,10 @@
             axis=1,
         )
     )
-    small_sums = lax.psum((jnp.stack(kernel_rows), gain_sum), ("seq", "dp"))
+    small_sums = (
+        exchange_sum(jnp.stack(kernel_rows), ("seq", "dp")),
+        exchange_sum(gain_sum.reshape(8, -1), ("seq", "dp")).reshape(-1),
+    )
     return (
         output,
         grad_inputs.astype(jnp.bfloat16),

time: 518 us -> 445 us (0.86)
  blocking collectives: 63.2 us -> 0 us
  waiting for transfers between devices: 142 us -> 92.2 us
  starting transfers between devices: 33.1 us -> 79 us
    psum x1 -> x0, waiting for transfers between devices: 125 us -> none  [local(): small_sums = lax.psum((jnp.stack(kernel_rows), gain_sum), ('seq', 'dp'))]
    psum x1 -> x0, blocking collectives: 63.2 us -> none  [local(): small_sums = lax.psum((jnp.stack(kernel_rows), gain_sum), ('seq', 'dp'))]
    reduce_scatter x1, waiting for transfers between devices: 0.03 us -> 53.6 us  [staged_scatter(): partial = lax.psum_scatter(partial, 'seq', scatter_dimension=0, tiled=True)]
    ppermute x0 -> x14, starting transfers between devices: none -> 46.6 us  [exchange_sum(): lax.ppermute(value, axis, [(i, i ^ bit) for i in range(size)])]
    ppermute x0 -> x14, waiting for transfers between devices: none -> 21.5 us  [exchange_sum(): lax.ppermute(value, axis, [(i, i ^ bit) for i in range(size)])]
    unnamed x178 -> x200, local copies, waits for them, and re-layouts: 15.3 us -> 15.2 us
  transfers between devices with their start and end apart: 11 -> 24, of which waited for: 4 -> 12; matrix products, arithmetic and copies ran while one was open for 15% -> 12% of each run, Pallas kernels for 0% -> 0%
where the time goes in v4:
time: 445 us; the launch traced here: 440 us
  other arithmetic  103 us (23%)
  matrix products  98.8 us (22%)
  waiting for transfers between devices  92.2 us (21%)
  starting transfers between devices  79 us (18%)
  local copies, waits for them, and re-layouts  50.4 us (11%)
  between operations  16.1 us (4%)
    reduce_scatter x1, waiting for transfers between devices, staged_scatter(): partial = lax.psum_scatter(partial, 'seq', scatter_dimension=0, tiled=True)  53.6 us
    ppermute x14, starting transfers between devices, exchange_sum(): lax.ppermute(value, axis, [(i, i ^ bit) for i in range(size)])  46.6 us
    reduce_sum x4, other arithmetic, local(): jnp.sum(jnp.where(same_seg, grad_conv * padded[:, tap_index:tap_index + f...  33.8 us
    ppermute x14, waiting for transfers between devices, exchange_sum(): lax.ppermute(value, axis, [(i, i ^ bit) for i in range(size)])  21.5 us
    sub x1, matrix products, local(): exponent = jnp.where(allowed, jnp.exp(scores - row_max), 0.0)  17.3 us
    ppermute x2, starting transfers between devices, with_halo(): before = lax.ppermute(last, axis, up)  15.5 us
    unnamed x200, local copies, waits for them, and re-layouts  15.2 us
    dot_general x1, matrix products, local(): jnp.einsum('bqhd,bkhd->bhqk', grad_heads, head_values, preferred_element_...  15 us
  transfers between devices with their start and end apart: 24, of which 12 were waited for; matrix products, arithmetic and copies ran while one was open for 12% of the time, Pallas kernels for 0%

profile of v4, /device:TPU:0, one launch (start us, length us, event | category | flops | bytes accessed | tf_op | source)
XLA Modules:
  0.0 439.7 jit_solution(10186178893506809640)
XLA Ops:
  12.1 7.6 %convolution_convert_fusion = bf16[512,3072]{1,0:T(8,128)(2,1)} fusion(bf16[512,1024]{1,0:T(8,128)(2,1)S(1)} %bitcast.174, bf16[1024,3072]{1,0:T(8,128)(2,1)} %param.10), kind=kOutput, calls=%fused_computation.18 | convolution fusion | flops 3222798336 | bytes 10485760 | tf_op jit(solution)/shard_map/dot_general | solution.py:82
  19.7 8.6 %reshape.285 = bf16[2,256,3,16,64]{4,3,2,1,0:T(8,128)(2,1)} reshape(bf16[512,3072]{1,0:T(8,128)(2,1)} %convolution_convert_fusion) | data formatting | bytes 6291456 | tf_op jit(solution)/shard_map/reshape;reshape | solution.py:86
  28.3 4.9 %slice.686 = bf16[2,256,2,16,64]{4,3,2,1,0:T(8,128)(2,1)} slice(bf16[2,256,3,16,64]{4,3,2,1,0:T(8,128)(2,1)} %reshape.285), slice={[0:2], [0:256], [1:3], [0:16], [0:64]} | slice | bytes 4194304 | tf_op jit(solution)/shard_map/slice | solution.py:88
  33.2 5.8 %copy.56 = bf16[2,256,2,16,64]{1,4,3,0,2:T(8,128)(2,1)} copy(bf16[2,256,2,16,64]{4,3,2,1,0:T(8,128)(2,1)} %slice.686) | data formatting | bytes 4194304
  40.4 4.6 %collective-permute-start = (bf16[2,256,2,16,64]{1,4,3,0,2:T(8,128)(2,1)}, bf16[2,256,2,16,64]{1,4,3,0,2:T(8,128)(2,1)}, u32[]{:S(2)}, u32[]{:S(2)}) collective-permute-start(bf16[2,256,2,16,64]{1,4,3,0,2:T(8,128)(2,1)} %copy.56), channel_id=1, source_target_pairs={{0,4},{4,8},{8,12},{12,16},{16,20},{20,24},{24,28},{28,32},{32,36}... | collective-permute-start | bytes 6291464 | tf_op jit(solution)/shard_map/ppermute | solution.py:58
  45.0 3.3 slice.688
  49.2 3.6 copy.57
  59.3 5.9 %pad_maximum_fusion.2 = bf16[2,768,2,16,64]{1,4,3,0,2:T(8,128)(2,1)} fusion(bf16[2,256,2,16,64]{1,4,3,0,2:T(8,128)(2,1)} %collective-permute-done.1, bf16[2,256,2,16,64]{1,4,3,0,2:T(8,128)(2,1)} %copy.56, bf16[2,256,2,16,64]{1,4,3,0,2:T(8,128)(2,1)} %collective-permute-done), kind=kLoop, calls=%fused_computation.15 | loop fusion | flops 18874368 | bytes 12582912 | tf_op jit(solution)/shard_map/concatenate | solution.py:89
  65.2 17.3 %fusion.178 = (f32[2,16,256]{2,1,0:T(8,128)}, f32[2,16,256,768]{3,2,1,0:T(8,128)}) fusion(pred[2,256,768]{2,1,0:T(8,128)(4,1)S(1)} %broadcast_compare_fusion, bf16[2,768,2,16,64]{1,4,3,0,2:T(8,128)(2,1)} %pad_maximum_fusion.2, bf16[2,256,1,16,64]{1,4,3,0,2:T(8,128)(2,1)} %copy.57), kind=kOutput, calls=%fused_computation.354 | convolution fusion | flops 836764416 | bytes 30179328 | tf_op jit(solution)/shard_map/sub | solution.py:105
  82.6 13.3 %fusion.6 = bf16[2,16,256,768]{3,2,1,0:T(8,128)(2,1)} fusion(f32[2,16,256,768]{3,2,1,0:T(8,128)} %get-tuple-element.122, f32[2,16,256]{2,1,0:T(8,128)} %get-tuple-element.121), kind=kLoop, calls=%fused_computation.14 | loop fusion | flops 12582912 | bytes 37781504 | tf_op jit(solution)/shard_map/convert_element_type | solution.py:107
  95.9 9.4 %fusion.98 = bf16[2,16,64,256]{3,2,1,0:T(8,128)(2,1)S(1)} fusion(bf16[2,16,256,768]{3,2,1,0:T(8,128)(2,1)} %fusion.6, bf16[2,768,2,16,64]{1,4,3,0,2:T(8,128)(2,1)} %pad_maximum_fusion.2), kind=kOutput, calls=%fused_computation.185 | convolution fusion | flops 805830656 | bytes 16777216 | tf_op jit(solution)/shard_map/bhqk,bkhd->bqhd/dot_general | solution.py:108
  107.1 10.7 %collective-permute-start.2 = (bf16[2,15,1024]{2,1,0:T(8,128)(2,1)S(1)}, bf16[2,15,1024]{2,1,0:T(8,128)(2,1)S(1)}, u32[]{:S(2)}, u32[]{:S(2)}) collective-permute-start(bf16[2,15,1024]{2,1,0:T(8,128)(2,1)S(1)} %get-tuple-element.55), channel_id=1, source_target_pairs={{0,4},{4,8},{8,12},{12,16},{16,20},{20,24},{24,28},{28,32},{32,36}... | collective-permute-start | bytes 184328 | tf_op jit(solution)/shard_map/ppermute | solution.py:21
  119.4 3.5 collective-permute-done.3
  123.7 22.4 %select_reduce_fusion = (f32[1024]{0:T(1024)S(1)}, f32[1024]{0:T(1024)S(1)}, f32[1024]{0:T(1024)S(1)}, f32[1024]{0:T(1024)S(1)}, f32[1024]{0:T(1024)S(1)}, /*ind...) fusion(f32[2,286,1024]{2,1,0:T(8,128)S(1)} %maximum_convert_fus, ...), kind=kLoop, calls=%fused_computation.147 | loop fusion | flops 67099648 | bytes 70434304 | tf_op jit(solution)/shard_map/reduce_sum | solution.py:143
  146.1 4.8 %select_reduce_fusion.9 = (f32[1024]{0:T(1024)S(1)}, f32[1024]{0:T(1024)S(1)}, f32[1024]{0:T(1024)S(1)}, f32[1024]{0:T(1024)S(1)}, f32[1024]{0:T(1024)S(1)}, /*i...) fusion(f32[2,256,1024]{2,1,0:T(8,128)S(1)} %get-tuple-element.4, ...), kind=kLoop, calls=%fused_computation.156 | loop fusion | flops 14670848 | bytes 22061568 | tf_op jit(solution)/shard_map/reduce_sum | solution.py:143
  151.2 4.8 %collective-permute-start.4 = (bf16[2,15,1024]{2,1,0:T(8,128)(2,1)S(1)}, bf16[2,15,1024]{2,1,0:T(8,128)(2,1)S(1)}, u32[]{:S(2)}, u32[]{:S(2)}) collective-permute-start(bf16[2,15,1024]{2,1,0:T(8,128)(2,1)S(1)} %get-tuple-element.53), channel_id=1, source_target_pairs={{0,4},{4,8},{8,12},{12,16},{16,20},{20,24},{24,28},{28,32},{32,36}... | collective-permute-start | bytes 184328 | tf_op jit(solution)/shard_map/ppermute | solution.py:21
  159.8 12.5 %fusion.171 = (bf16[2,256,1024]{2,1,0:T(8,128)(2,1)S(1)}, f32[2,256,1024]{2,1,0:T(8,128)}) fusion(f32[2,286,1024]{2,1,0:T(8,128)S(1)} %maximum_convert_fusion.1, f32[1024]{0:T(1024)S(1)} %bitcast.198, pred[2,256]{1,0:T(4,128)(4,1)S(1)} %copy-done.76, f32[1024]{0:T(1024)S(1)} %bitcast.200, pred[2,256]{1,0:T(4,128)(4,1)S(1)} %copy-done.77, ...), kind=kLoop, calls=%fused_computation.348 | loop fusion | flops 49807360 | bytes 69348864 | tf_op jit(solution)/shard_map/convert_element_type | solution.py:148
  175.6 2.9 reshape.286
  180.2 9.5 %convolution_bitcast_fusion = f32[2,768,1,16,64]{1,4,3,0,2:T(8,128)} fusion(bf16[2,256,16,64]{1,3,2,0:T(8,128)(2,1)S(1)} %copy.41, bf16[2,16,256,768]{3,2,1,0:T(8,128)(2,1)} %fusion.6), kind=kOutput, calls=%fused_computation.31 | convolution fusion | flops 805306368 | bytes 19922944 | tf_op jit(solution)/shard_map/bhqk,bqhd->bkhd/dot_general | solution.py:157
  190.5 15.0 %multiply_convert_fusion = bf16[2,16,256,768]{3,2,1,0:T(8,128)(2,1)} fusion(f32[2,16,256]{2,1,0:T(8,128)S(1)} %bitcast.239, f32[2,16,256,768]{3,2,1,0:T(8,128)} %get-tuple-element.122, f32[2,16,256]{2,1,0:T(8,128)S(1)} %copy-done.57, bf16[2,256,16,64]{1,3,2,0:T(8,128)(2,1)S(1)} %copy.41, bf16[2,768,2,16,64]{1,4,3,0,2:T(8,128)(2,1)} %pad_maximum_fusion.2), kind=kOutput, calls=%fused_computation.1 | convolution fusion | flops 836763648 | bytes 42008576 | tf_op jit(solution)/shard_map/bqhd,bkhd->bhqk/dot_general | solution.py:160
  205.5 10.0 %convolution_bitcast_fusion.1 = f32[2,768,1,16,64]{1,4,3,0,2:T(8,128)} fusion(bf16[2,16,256,768]{3,2,1,0:T(8,128)(2,1)} %multiply_convert_fusion, bf16[2,256,1,16,64]{1,4,3,0,2:T(8,128)(2,1)} %copy.57), kind=kOutput, calls=%fused_computation.32 | convolution fusion | flops 805306368 | bytes 19922944 | tf_op jit(solution)/shard_map/bhqk,bqhd->bkhd/dot_general | solution.py:167
  215.5 6.5 %fusion.2 = bf16[2,768,2,16,64]{1,4,3,0,2:T(8,128)(2,1)} fusion(f32[2,768,1,16,64]{1,4,3,0,2:T(8,128)S(1)} %copy-done.4, f32[2,768,1,16,64]{1,4,3,0,2:T(8,128)} %convolution_bitcast_fusion.1), kind=kLoop, calls=%fused_computation.9 | loop fusion | flops 3145728 | bytes 18874368 | tf_op jit(solution)/shard_map/convert.1
  222.0 5.0 %fusion.173 = (bf16[2,256,2,16,64]{1,4,3,0,2:T(8,128)(2,1)}, bf16[2,256,2,16,64]{1,4,3,0,2:T(8,128)(2,1)}) fusion(bf16[2,768,2,16,64]{1,4,3,0,2:T(8,128)(2,1)} %fusion.2), kind=kLoop, calls=%fused_computation.349 | loop fusion | bytes 8388608 | tf_op jit(solution)/shard_map/slice | solution.py:173
  228.3 6.5 %collective-permute-start.7 = (bf16[2,256,2,16,64]{1,4,3,0,2:T(8,128)(2,1)}, bf16[2,256,2,16,64]{1,4,3,0,2:T(8,128)(2,1)}, u32[]{:S(2)}, u32[]{:S(2)}) collective-permute-start(bf16[2,256,2,16,64]{1,4,3,0,2:T(8,128)(2,1)} %get-tuple-element.51), channel_id=1, source_target_pairs={{0,4},{4,8},{8,12},{12,16},{16,20},{20,24},{24,28},{28,32},{32,36}... | collective-permute-start | bytes 6291464 | tf_op jit(solution)/shard_map/ppermute | solution.py:58
  236.1 3.3 fusion.184
  239.4 10.4 %fusion.101 = bf16[2,256,1,16,64]{1,4,3,0,2:T(8,128)(2,1)} fusion(bf16[2,16,256,768]{3,2,1,0:T(8,128)(2,1)} %multiply_convert_fusion, bf16[2,768,2,16,64]{1,4,3,0,2:T(8,128)(2,1)} %pad_maximum_fusion.2), kind=kOutput, calls=%fused_computation.186 | convolution fusion | flops 805830656 | bytes 16777216 | tf_op jit(solution)/shard_map/bhqk,bkhd->bqhd/dot_general | solution.py:164
  249.8 4.1 fusion.12
  254.3 3.3 copy.46
  258.8 3.7 fusion.183
  262.6 6.0 %pad_maximum_fusion = f32[1024,4096]{1,0:T(8,128)} fusion(f32[1024,1024]{1,0:T(8,128)S(1)} %copy-done.18, f32[1024,3072]{1,0:T(8,128)S(1)} %fusion.183), kind=kLoop, calls=%fused_computation.5 | loop fusion | flops 4194304 | bytes 33554432 | tf_op jit(solution)/shard_map/concatenate | solution.py:194
  270.3 2.7 select_reduce_fusion.27
  273.1 3.7 select_reduce_fusion.18
  277.1 8.5 %collective-permute-start.8 = (f32[31,1024]{1,0:T(8,128)S(1)}, f32[31,1024]{1,0:T(8,128)S(1)}, u32[]{:S(2)}, u32[]{:S(2)}) collective-permute-start(f32[31,1024]{1,0:T(8,128)S(1)} %stack.157), channel_id=1, source_target_pairs={{0,4},{4,0},{8,12},{12,8},{16,20},{20,16},{24,28},{28,24},{32,36},... | collective-permute-start | bytes 380936 | tf_op jit(solution)/shard_map/ppermute | solution.py:35
  286.5 2.8 collective-permute-start.9
  289.4 3.8 collective-permute-done.9
  293.2 12.5 %collective-permute-start.10 = (f32[31,1024]{1,0:T(8,128)S(1)}, f32[31,1024]{1,0:T(8,128)S(1)}, u32[]{:S(2)}, u32[]{:S(2)}) collective-permute-start(f32[31,1024]{1,0:T(8,128)S(1)} %add.421), channel_id=1, source_target_pairs={{0,16},{4,20},{8,24},{12,28},{16,0},{20,4},{24,8},{28,12},{32,48},... | collective-permute-start | bytes 380936 | tf_op jit(solution)/shard_map/ppermute | solution.py:35
  305.7 3.4 collective-permute-done.10
  309.1 5.3 %collective-permute-start.11 = (f32[31,1024]{1,0:T(8,128)S(1)}, f32[31,1024]{1,0:T(8,128)S(1)}, u32[]{:S(2)}, u32[]{:S(2)}) collective-permute-start(f32[31,1024]{1,0:T(8,128)S(1)} %add.422), channel_id=1, source_target_pairs={{0,32},{4,36},{8,40},{12,44},{16,48},{20,52},{24,56},{28,60},{32,0... | collective-permute-start | bytes 380936 | tf_op jit(solution)/shard_map/ppermute | solution.py:35
  314.5 2.9 collective-permute-done.11
  317.5 4.0 collective-permute-start.12
  324.0 8.9 %fusion.30 = (f32[1024]{0:T(1024)S(1)}, f32[2,256]{1,0:T(2,128)S(1)}, f32[2,256]{1,0:T(2,128)S(1)}, f32[2,256,1024]{2,1,0:T(8,128)}) fusion(bf16[2,256,1024]{2,1,0:T(8,128)(2,1)S(1)} %copy-done.9, f32[2,256]{1,0:T(2,128)S(1)} %copy-done.59, f32[2,256]{1,0:T(2,128)S(1)} %copy-done.56, f32[1024]{0:T(1024)S(1)} %copy-done.90, ...), kind=kOutput, calls=%fused_computation.49 | convolution fusion | flops 3225942016 | bytes 12599296 | tf_op jit(solution)/shard_map/dot_general | solution.py:183
  335.2 3.7 collective-permute-done.13
  339.0 3.9 collective-permute-start.14
  344.7 3.4 collective-permute-done.17
  352.4 53.6 %reduce-scatter.3.cloned.1.call-done = f32[32,4096]{1,0:T(8,128)} async-done(((f32[1024,4096]{1,0:T(8,128)}), f32[32,4096]{1,0:T(8,128)}) %reduce-scatter.3.cloned.1.call-update) | async-done | bytes 524304 | tf_op jit(solution)/shard_map/reduce_scatter | solution.py:41
  409.7 3.2 collective-permute-start.21
  412.9 4.1 fusion.29
  417.6 12.1 %reduce-scatter.5.cloned.1.call-done = f32[8,4096]{1,0:T(8,128)} async-done(((f32[32,4096]{1,0:T(8,128)}), f32[8,4096]{1,0:T(8,128)}) %reduce-scatter.5.cloned.1.call-update) | async-done | bytes 131088 | tf_op jit(solution)/shard_map/reduce_scatter | solution.py:42
  (294 shorter events, 51.4 us)
Async XLA Ops:
  7.2 98.1 %copy-start = (bf16[1024,1024]{1,0:T(8,128)(2,1)S(1)}, bf16[1024,1024]{1,0:T(8,128)(2,1)}, u32[]{:S(2)}) copy-start(bf16[1024,1024]{1,0:T(8,128)(2,1)} %param.11) | copy-start | bytes 6291460
  7.2 398.8 %reduce-scatter.3.cloned.1.call-start = ((), (), s32[]{:S(2)}) async-start(), calls=%async_computation.2 | async-start | bytes 17301504 | tf_op jit(solution)/shard_map/reduce_scatter | solution.py:41
  39.1 20.2 %collective-permute-start.1 = (bf16[2,256,2,16,64]{1,4,3,0,2:T(8,128)(2,1)}, bf16[2,256,2,16,64]{1,4,3,0,2:T(8,128)(2,1)}, u32[]{:S(2)}, u32[]{:S(2)}) collective-permute-start(bf16[2,256,2,16,64]{1,4,3,0,2:T(8,128)(2,1)} %copy.56), channel_id=1, source_target_pairs={{4,0},{8,4},{12,8},{16,12},{20,16},{24,20},{28,24},{32,28},{36,32}... | collective-permute-start | bytes 6291464 | tf_op jit(solution)/shard_map/ppermute | solution.py:58
  40.4 19.0 %collective-permute-start = (bf16[2,256,2,16,64]{1,4,3,0,2:T(8,128)(2,1)}, bf16[2,256,2,16,64]{1,4,3,0,2:T(8,128)(2,1)}, u32[]{:S(2)}, u32[]{:S(2)}) collective-permute-start(bf16[2,256,2,16,64]{1,4,3,0,2:T(8,128)(2,1)} %copy.56), channel_id=1, source_target_pairs={{0,4},{4,8},{8,12},{12,16},{16,20},{20,24},{24,28},{28,32},{32,36}... | collective-permute-start | bytes 6291464 | tf_op jit(solution)/shard_map/ppermute | solution.py:58
  106.6 16.6 %copy-start.14 = (bf16[2,256,1024]{2,1,0:T(8,128)(2,1)}, bf16[2,256,1024]{2,1,0:T(8,128)(2,1)S(1)}, u32[]{:S(2)}) copy-start(bf16[2,256,1024]{2,1,0:T(8,128)(2,1)S(1)} %fusion.58) | copy-start | bytes 3145732
  106.6 16.6 %copy-start.16 = (bf16[2,256,1024]{2,1,0:T(8,128)(2,1)S(1)}, bf16[2,256,1024]{2,1,0:T(8,128)(2,1)}, u32[]{:S(2)}) copy-start(bf16[2,256,1024]{2,1,0:T(8,128)(2,1)} %param.13) | copy-start | bytes 3145732
  106.6 16.6 %copy-start.24 = (f32[1,1024]{1,0:T(1,128)S(1)}, f32[1,1024]{1,0:T(1,128)}, u32[]{:S(2)}) copy-start(f32[1,1024]{1,0:T(1,128)} %get-tuple-element.76) | copy-start | bytes 12292
  106.7 16.6 %copy-start.25 = (f32[1,1024]{1,0:T(1,128)S(1)}, f32[1,1024]{1,0:T(1,128)}, u32[]{:S(2)}) copy-start(f32[1,1024]{1,0:T(1,128)} %get-tuple-element.77) | copy-start | bytes 12292
  106.7 16.6 %copy-start.26 = (f32[1,1024]{1,0:T(1,128)S(1)}, f32[1,1024]{1,0:T(1,128)}, u32[]{:S(2)}) copy-start(f32[1,1024]{1,0:T(1,128)} %get-tuple-element.78) | copy-start | bytes 12292
  106.7 16.6 %copy-start.27 = (f32[1,1024]{1,0:T(1,128)S(1)}, f32[1,1024]{1,0:T(1,128)}, u32[]{:S(2)}) copy-start(f32[1,1024]{1,0:T(1,128)} %get-tuple-element.79) | copy-start | bytes 12292
  106.7 16.6 %copy-start.28 = (f32[1,1024]{1,0:T(1,128)S(1)}, f32[1,1024]{1,0:T(1,128)}, u32[]{:S(2)}) copy-start(f32[1,1024]{1,0:T(1,128)} %get-tuple-element.80) | copy-start | bytes 12292
  106.7 16.6 %copy-start.29 = (f32[1,1024]{1,0:T(1,128)S(1)}, f32[1,1024]{1,0:T(1,128)}, u32[]{:S(2)}) copy-start(f32[1,1024]{1,0:T(1,128)} %get-tuple-element.81) | copy-start | bytes 12292
  106.7 16.6 %copy-start.30 = (f32[1,1024]{1,0:T(1,128)S(1)}, f32[1,1024]{1,0:T(1,128)}, u32[]{:S(2)}) copy-start(f32[1,1024]{1,0:T(1,128)} %get-tuple-element.82) | copy-start | bytes 12292
  106.7 16.6 %copy-start.31 = (f32[1,1024]{1,0:T(1,128)S(1)}, f32[1,1024]{1,0:T(1,128)}, u32[]{:S(2)}) copy-start(f32[1,1024]{1,0:T(1,128)} %get-tuple-element.83) | copy-start | bytes 12292
  106.7 16.6 %copy-start.32 = (f32[1,1024]{1,0:T(1,128)S(1)}, f32[1,1024]{1,0:T(1,128)}, u32[]{:S(2)}) copy-start(f32[1,1024]{1,0:T(1,128)} %get-tuple-element.84) | copy-start | bytes 12292
  106.7 16.6 %copy-start.33 = (f32[1,1024]{1,0:T(1,128)S(1)}, f32[1,1024]{1,0:T(1,128)}, u32[]{:S(2)}) copy-start(f32[1,1024]{1,0:T(1,128)} %get-tuple-element.85) | copy-start | bytes 12292
  106.7 16.6 %copy-start.34 = (f32[1,1024]{1,0:T(1,128)S(1)}, f32[1,1024]{1,0:T(1,128)}, u32[]{:S(2)}) copy-start(f32[1,1024]{1,0:T(1,128)} %get-tuple-element.86) | copy-start | bytes 12292
  106.8 16.6 %copy-start.35 = (f32[1,1024]{1,0:T(1,128)S(1)}, f32[1,1024]{1,0:T(1,128)}, u32[]{:S(2)}) copy-start(f32[1,1024]{1,0:T(1,128)} %get-tuple-element.87) | copy-start | bytes 12292
  106.8 16.6 %copy-start.36 = (f32[1,1024]{1,0:T(1,128)S(1)}, f32[1,1024]{1,0:T(1,128)}, u32[]{:S(2)}) copy-start(f32[1,1024]{1,0:T(1,128)} %get-tuple-element.57) | copy-start | bytes 12292
  106.8 16.6 %copy-start.37 = (f32[1,1024]{1,0:T(1,128)S(1)}, f32[1,1024]{1,0:T(1,128)}, u32[]{:S(2)}) copy-start(f32[1,1024]{1,0:T(1,128)} %get-tuple-element.58) | copy-start | bytes 12292
  106.8 16.6 %copy-start.38 = (f32[1,1024]{1,0:T(1,128)S(1)}, f32[1,1024]{1,0:T(1,128)}, u32[]{:S(2)}) copy-start(f32[1,1024]{1,0:T(1,128)} %get-tuple-element.59) | copy-start | bytes 12292
  106.8 16.6 %copy-start.39 = (f32[1,1024]{1,0:T(1,128)S(1)}, f32[1,1024]{1,0:T(1,128)}, u32[]{:S(2)}) copy-start(f32[1,1024]{1,0:T(1,128)} %get-tuple-element.60) | copy-start | bytes 12292
  106.8 16.6 %copy-start.40 = (f32[1,1024]{1,0:T(1,128)S(1)}, f32[1,1024]{1,0:T(1,128)}, u32[]{:S(2)}) copy-start(f32[1,1024]{1,0:T(1,128)} %get-tuple-element.61) | copy-start | bytes 12292
  107.1 12.3 %collective-permute-start.2 = (bf16[2,15,1024]{2,1,0:T(8,128)(2,1)S(1)}, bf16[2,15,1024]{2,1,0:T(8,128)(2,1)S(1)}, u32[]{:S(2)}, u32[]{:S(2)}) collective-permute-start(bf16[2,15,1024]{2,1,0:T(8,128)(2,1)S(1)} %get-tuple-element.55), channel_id=1, source_target_pairs={{0,4},{4,8},{8,12},{12,16},{16,20},{20,24},{24,28},{28,32},{32,36}... | collective-permute-start | bytes 184328 | tf_op jit(solution)/shard_map/ppermute | solution.py:21
  117.8 5.1 %collective-permute-start.3 = (bf16[2,15,1024]{2,1,0:T(8,128)(2,1)S(1)}, bf16[2,15,1024]{2,1,0:T(8,128)(2,1)S(1)}, u32[]{:S(2)}, u32[]{:S(2)}) collective-permute-start(bf16[2,15,1024]{2,1,0:T(8,128)(2,1)S(1)} %get-tuple-element.56), channel_id=1, source_target_pairs={{4,0},{8,4},{12,8},{16,12},{20,16},{24,20},{28,24},{32,28},{36,32}... | collective-permute-start | bytes 184328 | tf_op jit(solution)/shard_map/ppermute | solution.py:22
  123.2 22.9 %copy-start.2 = (f32[2,286,1024]{2,1,0:T(8,128)}, f32[2,286,1024]{2,1,0:T(8,128)S(1)}, u32[]{:S(2)}) copy-start(f32[2,286,1024]{2,1,0:T(8,128)S(1)} %maximum_convert_fusion) | copy-start | bytes 7028740
  151.2 6.6 %collective-permute-start.4 = (bf16[2,15,1024]{2,1,0:T(8,128)(2,1)S(1)}, bf16[2,15,1024]{2,1,0:T(8,128)(2,1)S(1)}, u32[]{:S(2)}, u32[]{:S(2)}) collective-permute-start(bf16[2,15,1024]{2,1,0:T(8,128)(2,1)S(1)} %get-tuple-element.53), channel_id=1, source_target_pairs={{0,4},{4,8},{8,12},{12,16},{16,20},{20,24},{24,28},{28,32},{32,36}... | collective-permute-start | bytes 184328 | tf_op jit(solution)/shard_map/ppermute | solution.py:21
  156.0 3.1 collective-permute-start.5
  227.0 22.8 %collective-permute-start.6 = (bf16[2,256,2,16,64]{1,4,3,0,2:T(8,128)(2,1)}, bf16[2,256,2,16,64]{1,4,3,0,2:T(8,128)(2,1)}, u32[]{:S(2)}, u32[]{:S(2)}) collective-permute-start(bf16[2,256,2,16,64]{1,4,3,0,2:T(8,128)(2,1)} %get-tuple-element.50), channel_id=1, source_target_pairs={{4,0},{8,4},{12,8},{16,12},{20,16},{24,20},{28,24},{32,28},{36,32}... | collective-permute-start | bytes 6291464 | tf_op jit(solution)/shard_map/ppermute | solution.py:58
  228.3 21.5 %collective-permute-start.7 = (bf16[2,256,2,16,64]{1,4,3,0,2:T(8,128)(2,1)}, bf16[2,256,2,16,64]{1,4,3,0,2:T(8,128)(2,1)}, u32[]{:S(2)}, u32[]{:S(2)}) collective-permute-start(bf16[2,256,2,16,64]{1,4,3,0,2:T(8,128)(2,1)} %get-tuple-element.51), channel_id=1, source_target_pairs={{0,4},{4,8},{8,12},{12,16},{16,20},{20,24},{24,28},{28,32},{32,36}... | collective-permute-start | bytes 6291464 | tf_op jit(solution)/shard_map/ppermute | solution.py:58
  268.7 161.0 %reduce-scatter.5.cloned.1.call-start = ((), (), s32[]{:S(2)}) async-start(), calls=%async_computation.3 | async-start | bytes 655360 | tf_op jit(solution)/shard_map/reduce_scatter | solution.py:42
  277.1 9.4 %collective-permute-start.8 = (f32[31,1024]{1,0:T(8,128)S(1)}, f32[31,1024]{1,0:T(8,128)S(1)}, u32[]{:S(2)}, u32[]{:S(2)}) collective-permute-start(f32[31,1024]{1,0:T(8,128)S(1)} %stack.157), channel_id=1, source_target_pairs={{0,4},{4,0},{8,12},{12,8},{16,20},{20,16},{24,28},{28,24},{32,36},... | collective-permute-start | bytes 380936 | tf_op jit(solution)/shard_map/ppermute | solution.py:35
  286.5 6.6 %collective-permute-start.9 = (f32[31,1024]{1,0:T(8,128)S(1)}, f32[31,1024]{1,0:T(8,128)S(1)}, u32[]{:S(2)}, u32[]{:S(2)}) collective-permute-start(f32[31,1024]{1,0:T(8,128)S(1)} %add.420), channel_id=1, source_target_pairs={{0,8},{4,12},{8,0},{12,4},{16,24},{20,28},{24,16},{28,20},{32,40},... | collective-permute-start | bytes 380936 | tf_op jit(solution)/shard_map/ppermute | solution.py:35
  293.2 15.9 %collective-permute-start.10 = (f32[31,1024]{1,0:T(8,128)S(1)}, f32[31,1024]{1,0:T(8,128)S(1)}, u32[]{:S(2)}, u32[]{:S(2)}) collective-permute-start(f32[31,1024]{1,0:T(8,128)S(1)} %add.421), channel_id=1, source_target_pairs={{0,16},{4,20},{8,24},{12,28},{16,0},{20,4},{24,8},{28,12},{32,48},... | collective-permute-start | bytes 380936 | tf_op jit(solution)/shard_map/ppermute | solution.py:35
  309.1 8.3 %collective-permute-start.11 = (f32[31,1024]{1,0:T(8,128)S(1)}, f32[31,1024]{1,0:T(8,128)S(1)}, u32[]{:S(2)}, u32[]{:S(2)}) collective-permute-start(f32[31,1024]{1,0:T(8,128)S(1)} %add.422), channel_id=1, source_target_pairs={{0,32},{4,36},{8,40},{12,44},{16,48},{20,52},{24,56},{28,60},{32,0... | collective-permute-start | bytes 380936 | tf_op jit(solution)/shard_map/ppermute | solution.py:35
  317.5 15.4 %collective-permute-start.12 = (f32[31,1024]{1,0:T(8,128)S(1)}, f32[31,1024]{1,0:T(8,128)S(1)}, u32[]{:S(2)}, u32[]{:S(2)}) collective-permute-start(f32[31,1024]{1,0:T(8,128)S(1)} %add.423), channel_id=1, source_target_pairs={{0,64},{4,68},{8,72},{12,76},{16,80},{20,84},{24,88},{28,92},{32,9... | collective-permute-start | bytes 380936 | tf_op jit(solution)/shard_map/ppermute | solution.py:35
  323.9 19.0 %copy-start.13 = (f32[2,256,1024]{2,1,0:T(8,128)S(1)}, f32[2,256,1024]{2,1,0:T(8,128)}, u32[]{:S(2)}) copy-start(f32[2,256,1024]{2,1,0:T(8,128)} %get-tuple-element.47) | copy-start | bytes 6291460
  323.9 19.0 %copy-start.15 = (bf16[2,256,1024]{2,1,0:T(8,128)(2,1)S(1)}, bf16[2,256,1024]{2,1,0:T(8,128)(2,1)}, u32[]{:S(2)}) copy-start(bf16[2,256,1024]{2,1,0:T(8,128)(2,1)} %copy-done.14) | copy-start | bytes 3145732
  332.9 1.9 collective-permute-start.15
  332.9 6.1 %collective-permute-start.13 = (f32[31,1024]{1,0:T(8,128)S(1)}, f32[31,1024]{1,0:T(8,128)S(1)}, u32[]{:S(2)}, u32[]{:S(2)}) collective-permute-start(f32[31,1024]{1,0:T(8,128)S(1)} %add.424), channel_id=1, source_target_pairs={{0,1},{1,0},{2,3},{3,2},{4,5},{5,4},{6,7},{7,6},{8,9},{9,8},{10,11... | collective-permute-start | bytes 380936 | tf_op jit(solution)/shard_map/ppermute | solution.py:35
  334.8 8.1 %collective-permute-start.16 = (f32[8,128]{1,0:T(8,128)S(1)}, f32[8,128]{1,0:T(8,128)S(1)}, u32[]{:S(2)}, u32[]{:S(2)}) collective-permute-start(f32[8,128]{1,0:T(8,128)S(1)} %bitcast_add_fusion), channel_id=1, source_target_pairs={{0,8},{4,12},{8,0},{12,4},{16,24},{20,28},{24,16},{28,20},{32,40},... | collective-permute-start | bytes 12296 | tf_op jit(solution)/shard_map/ppermute | solution.py:35
  339.0 11.0 %collective-permute-start.14 = (f32[31,1024]{1,0:T(8,128)S(1)}, f32[31,1024]{1,0:T(8,128)S(1)}, u32[]{:S(2)}, u32[]{:S(2)}) collective-permute-start(f32[31,1024]{1,0:T(8,128)S(1)} %add.425), channel_id=1, source_target_pairs={{0,2},{1,3},{2,0},{3,1},{4,6},{5,7},{6,4},{7,5},{8,10},{9,11},{10,... | collective-permute-start | bytes 380936 | tf_op jit(solution)/shard_map/ppermute | solution.py:35
  342.9 5.2 %collective-permute-start.17 = (f32[8,128]{1,0:T(8,128)S(1)}, f32[8,128]{1,0:T(8,128)S(1)}, u32[]{:S(2)}, u32[]{:S(2)}) collective-permute-start(f32[8,128]{1,0:T(8,128)S(1)} %fusion.201), channel_id=1, source_target_pairs={{0,16},{4,20},{8,24},{12,28},{16,0},{20,4},{24,8},{28,12},{32,48},... | collective-permute-start | bytes 12296 | tf_op jit(solution)/shard_map/ppermute | solution.py:35
  348.1 3.8 collective-permute-start.18
  351.9 54.1 %collective-permute-start.19 = (f32[8,128]{1,0:T(8,128)S(1)}, f32[8,128]{1,0:T(8,128)S(1)}, u32[]{:S(2)}, u32[]{:S(2)}) collective-permute-start(f32[8,128]{1,0:T(8,128)S(1)} %add.430), channel_id=1, source_target_pairs={{0,64},{4,68},{8,72},{12,76},{16,80},{20,84},{24,88},{28,92},{32,9... | collective-permute-start | bytes 12296 | tf_op jit(solution)/shard_map/ppermute | solution.py:35
  406.1 3.7 collective-permute-start.20
  409.7 7.3 %collective-permute-start.21 = (f32[8,128]{1,0:T(8,128)S(1)}, f32[8,128]{1,0:T(8,128)S(1)}, u32[]{:S(2)}, u32[]{:S(2)}) collective-permute-start(f32[8,128]{1,0:T(8,128)S(1)} %add.432), channel_id=1, source_target_pairs={{0,2},{1,3},{2,0},{3,1},{4,6},{5,7},{6,4},{7,5},{8,10},{9,11},{10,... | collective-permute-start | bytes 12296 | tf_op jit(solution)/shard_map/ppermute | solution.py:35
  412.9 19.7 %copy-start.1 = (bf16[1024,1024]{1,0:T(8,128)(2,1)S(1)}, bf16[1024,1024]{1,0:T(8,128)(2,1)}, u32[]{:S(2)}) copy-start(bf16[1024,1024]{1,0:T(8,128)(2,1)} %param.11) | copy-start | bytes 6291460
  (74 other events, 675.0 us)
Sparse Core Ops, SparseCore 0:
  268.7 137.2 reduce-scatter.2
  408.4 21.2 reduce-scatter.4

commit v5 on v4

--- a/solution.py
+++ b/solution.py
@@ -150,6 +150,14 @@
     grad_attended = jnp.dot(
         flat_grad_hidden, out_weight.T, preferred_element_type=jnp.float32
     ).astype(jnp.bfloat16)
+    out_partial = lax.dot_general(
+        flat_attended,
+        flat_grad_hidden,
+        (((0,), (0,)), ((), ())),
+        preferred_element_type=jnp.float32,
+    )
+    grad_attended, out_partial = lax.optimization_barrier((grad_attended, out_partial))
+    out_sum = staged_scatter(out_partial)
     grad_heads = grad_attended.reshape(batches, frames, HEADS, head_dim)
     row_delta = jnp.sum(
         grad_heads.astype(jnp.float32) * head_out.astype(jnp.float32), axis=-1
@@ -190,22 +198,11 @@
     )
     gain_sum = jnp.sum(grad_normed * unit_rows, axis=(0, 1))
     contract_rows = (((0,), (0,)), ((), ()))
-    summed = staged_scatter(
-        jnp.concatenate(
-            [
-                lax.dot_general(
-                    flat_normed, flat_grad_qkv, contract_rows, preferred_element_type=jnp.float32
-                ),
-                lax.dot_general(
-                    flat_attended,
-                    flat_grad_hidden,
-                    contract_rows,
-                    preferred_element_type=jnp.float32,
-                ),
-            ],
-            axis=1,
-        )
-    )
+    qkv_partial = lax.dot_general(
+        flat_normed, flat_grad_qkv, contract_rows, preferred_element_type=jnp.float32
+    )
+    qkv_partial, out_sum = lax.optimization_barrier((qkv_partial, out_sum))
+    qkv_sum = staged_scatter(qkv_partial)
     small_sums = (
         exchange_sum(jnp.stack(kernel_rows), ("seq", "dp")),
         exchange_sum(gain_sum.reshape(8, -1), ("seq", "dp")).reshape(-1),
@@ -213,8 +210,8 @@
     return (
         output,
         grad_inputs.astype(jnp.bfloat16),
-        summed[:, : 3 * model_width] * factor,
-        summed[:, 3 * model_width :] * factor,
+        qkv_sum * factor,
+        out_sum * factor,
         small_sums[0] * factor,
         small_sums[1] * factor,
     )

time: 445 us -> 471 us (1.058)
  waiting for transfers between devices: 92.2 us -> 149 us
  starting transfers between devices: 79 us -> 52.4 us
    reduce_scatter x1 -> x2, waiting for transfers between devices: 53.6 us -> 86.2 us  [staged_scatter(): partial = lax.psum_scatter(partial, 'seq', scatter_dimension=0, tiled=True)]
    ppermute x14, starting transfers between devices: 46.6 us -> 19.6 us  [exchange_sum(): lax.ppermute(value, axis, [(i, i ^ bit) for i in range(size)])]
    reduce_scatter x1 -> x2, waiting for transfers between devices: 12.1 us -> 32.5 us  [staged_scatter(): return lax.psum_scatter(partial, 'dp', scatter_dimension=0, tiled=True)]
    concatenate x1 -> x0, other arithmetic: 6.02 us -> none  [local(): jnp.concatenate([lax.dot_general(flat_normed, flat_grad_qkv, contract_row...]
    ppermute x14, waiting for transfers between devices: 21.5 us -> 26.9 us  [exchange_sum(): lax.ppermute(value, axis, [(i, i ^ bit) for i in range(size)])]
    unnamed x200 -> x198, local copies, waits for them, and re-layouts: 15.2 us -> 14.1 us
  transfers between devices with their start and end apart: 24 -> 26, of which waited for: 12 -> 15; matrix products, arithmetic and copies ran while one was open for 12% -> 23% of each run, Pallas kernels for 0% -> 0%
where the time goes in v5:
time: 471 us; the launch traced here: 466 us
  waiting for transfers between devices  149 us (32%)
  matrix products  102 us (22%)
  other arithmetic  98.9 us (21%)
  starting transfers between devices  52.4 us (11%)
  local copies, waits for them, and re-layouts  47.7 us (10%)
  between operations  15.6 us (3%)
    reduce_scatter x2, waiting for transfers between devices, staged_scatter(): partial = lax.psum_scatter(partial, 'seq', scatter_dimension=0, tiled=True)  86.2 us
    reduce_sum x4, other arithmetic, local(): jnp.sum(jnp.where(same_seg, grad_conv * padded[:, tap_index:tap_index + f...  33.8 us
    reduce_scatter x2, waiting for transfers between devices, staged_scatter(): return lax.psum_scatter(partial, 'dp', scatter_dimension=0, tiled=True)  32.5 us
    ppermute x14, waiting for transfers between devices, exchange_sum(): lax.ppermute(value, axis, [(i, i ^ bit) for i in range(size)])  26.9 us
    ppermute x14, starting transfers between devices, exchange_sum(): lax.ppermute(value, axis, [(i, i ^ bit) for i in range(size)])  19.6 us
    sub x1, matrix products, local(): exponent = jnp.where(allowed, jnp.exp(scores - row_max), 0.0)  17.3 us
    ppermute x2, starting transfers between devices, with_halo(): before = lax.ppermute(last, axis, up)  15.6 us
    dot_general x1, matrix products, local(): jnp.einsum('bqhd,bkhd->bhqk', grad_heads, head_values, preferred_element_...  15.1 us
  transfers between devices with their start and end apart: 26, of which 15 were waited for; matrix products, arithmetic and copies ran while one was open for 23% of the time, Pallas kernels for 0%

profile of v5, /device:TPU:0, one launch (start us, length us, event | category | flops | bytes accessed | tf_op | source)
XLA Modules:
  0.0 466.0 jit_solution(10684739541096360517)
XLA Ops:
  12.1 7.6 %convolution_convert_fusion = bf16[512,3072]{1,0:T(8,128)(2,1)} fusion(bf16[512,1024]{1,0:T(8,128)(2,1)S(1)} %bitcast.176, bf16[1024,3072]{1,0:T(8,128)(2,1)} %param.10), kind=kOutput, calls=%fused_computation.17 | convolution fusion | flops 3222798336 | bytes 10485760 | tf_op jit(solution)/shard_map/dot_general | solution.py:82
  19.7 8.6 %reshape.285 = bf16[2,256,3,16,64]{4,3,2,1,0:T(8,128)(2,1)} reshape(bf16[512,3072]{1,0:T(8,128)(2,1)} %convolution_convert_fusion) | data formatting | bytes 6291456 | tf_op jit(solution)/shard_map/reshape;reshape | solution.py:86
  28.3 4.9 %slice.678 = bf16[2,256,2,16,64]{4,3,2,1,0:T(8,128)(2,1)} slice(bf16[2,256,3,16,64]{4,3,2,1,0:T(8,128)(2,1)} %reshape.285), slice={[0:2], [0:256], [1:3], [0:16], [0:64]} | slice | bytes 4194304 | tf_op jit(solution)/shard_map/slice | solution.py:88
  33.2 5.8 %copy.52 = bf16[2,256,2,16,64]{1,4,3,0,2:T(8,128)(2,1)} copy(bf16[2,256,2,16,64]{4,3,2,1,0:T(8,128)(2,1)} %slice.678) | data formatting | bytes 4194304
  40.3 4.6 collective-permute-start
  44.9 3.3 slice.680
  49.1 3.6 copy.53
  59.2 5.9 %pad_maximum_fusion.1 = bf16[2,768,2,16,64]{1,4,3,0,2:T(8,128)(2,1)} fusion(bf16[2,256,2,16,64]{1,4,3,0,2:T(8,128)(2,1)} %collective-permute-done.1, bf16[2,256,2,16,64]{1,4,3,0,2:T(8,128)(2,1)} %copy.52, bf16[2,256,2,16,64]{1,4,3,0,2:T(8,128)(2,1)} %collective-permute-done), kind=kLoop, calls=%fused_computation.14 | loop fusion | flops 18874368 | bytes 12582912 | tf_op jit(solution)/shard_map/concatenate | solution.py:89
  65.1 17.3 %fusion.178 = (f32[2,16,256]{2,1,0:T(8,128)}, f32[2,16,256,768]{3,2,1,0:T(8,128)}) fusion(pred[2,256,768]{2,1,0:T(8,128)(4,1)S(1)} %broadcast_compare_fusion, bf16[2,768,2,16,64]{1,4,3,0,2:T(8,128)(2,1)} %pad_maximum_fusion.1, bf16[2,256,1,16,64]{1,4,3,0,2:T(8,128)(2,1)} %copy.53), kind=kOutput, calls=%fused_computation.353 | convolution fusion | flops 836764416 | bytes 30179328 | tf_op jit(solution)/shard_map/sub | solution.py:105
  82.5 13.3 %fusion.6 = bf16[2,16,256,768]{3,2,1,0:T(8,128)(2,1)} fusion(f32[2,16,256,768]{3,2,1,0:T(8,128)} %get-tuple-element.130, f32[2,16,256]{2,1,0:T(8,128)} %get-tuple-element.129), kind=kLoop, calls=%fused_computation.13 | loop fusion | flops 12582912 | bytes 37781504 | tf_op jit(solution)/shard_map/convert_element_type | solution.py:107
  95.8 9.4 %fusion.98 = bf16[2,16,64,256]{3,2,1,0:T(8,128)(2,1)S(1)} fusion(bf16[2,16,256,768]{3,2,1,0:T(8,128)(2,1)} %fusion.6, bf16[2,768,2,16,64]{1,4,3,0,2:T(8,128)(2,1)} %pad_maximum_fusion.1), kind=kOutput, calls=%fused_computation.184 | convolution fusion | flops 805830656 | bytes 16777216 | tf_op jit(solution)/shard_map/bhqk,bkhd->bqhd/dot_general | solution.py:108
  106.9 10.7 %collective-permute-start.2 = (bf16[2,15,1024]{2,1,0:T(8,128)(2,1)S(1)}, bf16[2,15,1024]{2,1,0:T(8,128)(2,1)S(1)}, u32[]{:S(2)}, u32[]{:S(2)}) collective-permute-start(bf16[2,15,1024]{2,1,0:T(8,128)(2,1)S(1)} %get-tuple-element.63), channel_id=1, source_target_pairs={{0,4},{4,8},{8,12},{12,16},{16,20},{20,24},{24,28},{28,32},{32,36}... | collective-permute-start | bytes 184328 | tf_op jit(solution)/shard_map/ppermute | solution.py:21
  119.3 3.5 collective-permute-done.3
  123.6 22.5 %select_reduce_fusion = (f32[1024]{0:T(1024)S(1)}, f32[1024]{0:T(1024)S(1)}, f32[1024]{0:T(1024)S(1)}, f32[1024]{0:T(1024)S(1)}, f32[1024]{0:T(1024)S(1)}, /*ind...) fusion(f32[2,286,1024]{2,1,0:T(8,128)S(1)} %maximum_convert_fus, ...), kind=kLoop, calls=%fused_computation.146 | loop fusion | flops 67099648 | bytes 70434304 | tf_op jit(solution)/shard_map/reduce_sum | solution.py:143
  146.0 4.8 %select_reduce_fusion.9 = (f32[1024]{0:T(1024)S(1)}, f32[1024]{0:T(1024)S(1)}, f32[1024]{0:T(1024)S(1)}, f32[1024]{0:T(1024)S(1)}, f32[1024]{0:T(1024)S(1)}, /*i...) fusion(f32[2,256,1024]{2,1,0:T(8,128)S(1)} %get-tuple-element.5, ...), kind=kLoop, calls=%fused_computation.155 | loop fusion | flops 14670848 | bytes 22061568 | tf_op jit(solution)/shard_map/reduce_sum | solution.py:143
  150.9 4.8 %collective-permute-start.4 = (bf16[2,15,1024]{2,1,0:T(8,128)(2,1)S(1)}, bf16[2,15,1024]{2,1,0:T(8,128)(2,1)S(1)}, u32[]{:S(2)}, u32[]{:S(2)}) collective-permute-start(bf16[2,15,1024]{2,1,0:T(8,128)(2,1)S(1)} %get-tuple-element.61), channel_id=1, source_target_pairs={{0,4},{4,8},{8,12},{12,16},{16,20},{20,24},{24,28},{28,32},{32,36}... | collective-permute-start | bytes 184328 | tf_op jit(solution)/shard_map/ppermute | solution.py:21
  159.7 12.5 %fusion.171 = (bf16[2,256,1024]{2,1,0:T(8,128)(2,1)S(1)}, f32[2,256,1024]{2,1,0:T(8,128)}) fusion(f32[2,286,1024]{2,1,0:T(8,128)S(1)} %maximum_convert_fusion.1, f32[1024]{0:T(1024)S(1)} %bitcast.200, pred[2,256]{1,0:T(4,128)(4,1)S(1)} %copy-done.73, f32[1024]{0:T(1024)S(1)} %bitcast.202, pred[2,256]{1,0:T(4,128)(4,1)S(1)} %copy-done.74, ...), kind=kLoop, calls=%fused_computation.347 | loop fusion | flops 49807360 | bytes 69348864 | tf_op jit(solution)/shard_map/convert_element_type | solution.py:148
  172.2 2.3 convolution_convert_fusion.1
  174.5 3.3 fusion.183
  180.8 9.5 %convolution_bitcast_fusion = f32[2,768,1,16,64]{1,4,3,0,2:T(8,128)} fusion(bf16[2,256,16,64]{1,3,2,0:T(8,128)(2,1)S(1)} %copy.40, bf16[2,16,256,768]{3,2,1,0:T(8,128)(2,1)} %fusion.6), kind=kOutput, calls=%fused_computation.30 | convolution fusion | flops 805306368 | bytes 19922944 | tf_op jit(solution)/shard_map/bhqk,bqhd->bkhd/dot_general | solution.py:165
  191.5 15.1 %multiply_convert_fusion = bf16[2,16,256,768]{3,2,1,0:T(8,128)(2,1)} fusion(f32[2,16,256]{2,1,0:T(8,128)S(1)} %bitcast.241, f32[2,16,256,768]{3,2,1,0:T(8,128)} %get-tuple-element.130, f32[2,16,256]{2,1,0:T(8,128)S(1)} %copy-done.54, bf16[2,256,16,64]{1,3,2,0:T(8,128)(2,1)S(1)} %copy.40, bf16[2,768,2,16,64]{1,4,3,0,2:T(8,128)(2,1)} %pad_maximum_fusion.1), kind=kOutput, calls=%fused_computation.1 | convolution fusion | flops 836763648 | bytes 42008576 | tf_op jit(solution)/shard_map/bqhd,bkhd->bhqk/dot_general | solution.py:168
  206.6 9.5 %convolution_bitcast_fusion.1 = f32[2,768,1,16,64]{1,4,3,0,2:T(8,128)} fusion(bf16[2,16,256,768]{3,2,1,0:T(8,128)(2,1)} %multiply_convert_fusion, bf16[2,256,1,16,64]{1,4,3,0,2:T(8,128)(2,1)S(1)} %copy-done.12), kind=kOutput, calls=%fused_computation.31 | convolution fusion | flops 805306368 | bytes 19922944 | tf_op jit(solution)/shard_map/bhqk,bqhd->bkhd/dot_general | solution.py:175
  216.2 8.5 %fusion.2 = bf16[2,768,2,16,64]{1,4,3,0,2:T(8,128)(2,1)} fusion(f32[2,768,1,16,64]{1,4,3,0,2:T(8,128)} %convolution_bitcast_fusion, f32[2,768,1,16,64]{1,4,3,0,2:T(8,128)} %convolution_bitcast_fusion.1), kind=kLoop, calls=%fused_computation.8 | loop fusion | flops 3145728 | bytes 18874368 | tf_op jit(solution)/shard_map/convert.1
  224.7 5.1 %fusion.173 = (bf16[2,256,2,16,64]{1,4,3,0,2:T(8,128)(2,1)}, bf16[2,256,2,16,64]{1,4,3,0,2:T(8,128)(2,1)}) fusion(bf16[2,768,2,16,64]{1,4,3,0,2:T(8,128)(2,1)} %fusion.2), kind=kLoop, calls=%fused_computation.348 | loop fusion | bytes 8388608 | tf_op jit(solution)/shard_map/slice | solution.py:181
  231.1 6.4 %collective-permute-start.7 = (bf16[2,256,2,16,64]{1,4,3,0,2:T(8,128)(2,1)}, bf16[2,256,2,16,64]{1,4,3,0,2:T(8,128)(2,1)}, u32[]{:S(2)}, u32[]{:S(2)}) collective-permute-start(bf16[2,256,2,16,64]{1,4,3,0,2:T(8,128)(2,1)} %get-tuple-element.59), channel_id=1, source_target_pairs={{0,4},{4,8},{8,12},{12,16},{16,20},{20,24},{24,28},{28,32},{32,36}... | collective-permute-start | bytes 6291464 | tf_op jit(solution)/shard_map/ppermute | solution.py:58
  237.5 10.4 %fusion.101 = bf16[2,256,1,16,64]{1,4,3,0,2:T(8,128)(2,1)} fusion(bf16[2,16,256,768]{3,2,1,0:T(8,128)(2,1)} %multiply_convert_fusion, bf16[2,768,2,16,64]{1,4,3,0,2:T(8,128)(2,1)} %pad_maximum_fusion.1), kind=kOutput, calls=%fused_computation.185 | convolution fusion | flops 805830656 | bytes 16777216 | tf_op jit(solution)/shard_map/bhqk,bkhd->bqhd/dot_general | solution.py:172
  248.0 4.5 fusion.12
  252.8 3.3 copy.45
  256.8 47.6 %reduce-scatter.5.cloned.1.call-done = f32[32,1024]{1,0:T(8,128)} async-done(((f32[1024,1024]{1,0:T(8,128)}), f32[32,1024]{1,0:T(8,128)}) %reduce-scatter.5.cloned.1.call-update) | async-done | bytes 131088 | tf_op jit(solution)/shard_map/reduce_scatter | solution.py:41
  304.7 7.7 %fusion.184 = f32[1024,3072]{1,0:T(8,128)} fusion(bf16[512,1024]{1,0:T(8,128)(2,1)} %bitcast.177, bf16[512,3072]{0,1:T(8,128)(2,1)S(1)} %bitcast.172), kind=kOutput, calls=%fused_computation.355 | convolution fusion | flops 3221225472 | bytes 16777216 | tf_op jit(solution)/shard_map/dot_general | solution.py:201
  312.3 14.8 %reduce-scatter.7.cloned.1.call-done = f32[8,1024]{1,0:T(8,128)} async-done(((f32[32,1024]{1,0:T(8,128)}), f32[8,1024]{1,0:T(8,128)}) %reduce-scatter.7.cloned.1.call-update) | async-done | bytes 32784 | tf_op jit(solution)/shard_map/reduce_scatter | solution.py:42
  328.7 2.7 select_reduce_fusion.27
  331.6 3.7 select_reduce_fusion.18
  338.6 4.1 collective-permute-done.9
  342.7 3.1 collective-permute-start.10
  345.7 3.5 collective-permute-done.10
  350.8 3.5 collective-permute-done.11
  354.4 3.1 collective-permute-start.12
  357.4 2.4 copy.43
  359.9 8.8 %fusion.30 = (f32[1024]{0:T(1024)S(1)}, f32[2,256]{1,0:T(2,128)S(1)}, f32[2,256]{1,0:T(2,128)S(1)}, f32[2,256,1024]{2,1,0:T(8,128)}) fusion(bf16[2,256,1024]{2,1,0:T(8,128)(2,1)S(1)} %copy-done.8, f32[2,256]{1,0:T(2,128)S(1)} %copy-done.56, f32[2,256]{1,0:T(2,128)S(1)} %copy-done.53, f32[1024]{0:T(1024)S(1)} %copy-done.87, ...), kind=kOutput, calls=%fused_computation.48 | convolution fusion | flops 3225942016 | bytes 12599296 | tf_op jit(solution)/shard_map/dot_general | solution.py:191
  371.3 3.4 collective-permute-done.13
  376.2 3.0 collective-permute-start.17
  385.5 4.7 %collective-permute-done.19 = f32[8,128]{1,0:T(8,128)S(1)} collective-permute-done((f32[8,128]{1,0:T(8,128)S(1)}, f32[8,128]{1,0:T(8,128)S(1)}, u32[]{:S(2)}, u32[]{:S(2)}) %collective-permute-start.19) | collective-permute-done | bytes 4128 | tf_op jit(solution)/shard_map/ppermute | solution.py:35
  390.4 3.5 collective-permute-done.20
  393.9 2.1 collective-permute-start.21
  396.0 38.6 %reduce-scatter.9.cloned.1.call-done = f32[32,3072]{1,0:T(8,128)} async-done(((f32[1024,3072]{1,0:T(8,128)}), f32[32,3072]{1,0:T(8,128)}) %reduce-scatter.9.cloned.1.call-update) | async-done | bytes 393232 | tf_op jit(solution)/shard_map/reduce_scatter | solution.py:41
  434.7 4.1 fusion.29
  440.0 17.8 %reduce-scatter.11.cloned.1.call-done = f32[8,3072]{1,0:T(8,128)} async-done(((f32[32,3072]{1,0:T(8,128)}), f32[8,3072]{1,0:T(8,128)}) %reduce-scatter.11.cloned.1.call-update) | async-done | bytes 98320 | tf_op jit(solution)/shard_map/reduce_scatter | solution.py:42
  (298 shorter events, 47.0 us)
Async XLA Ops:
  7.2 98.0 %copy-start = (bf16[1024,1024]{1,0:T(8,128)(2,1)S(1)}, bf16[1024,1024]{1,0:T(8,128)(2,1)}, u32[]{:S(2)}) copy-start(bf16[1024,1024]{1,0:T(8,128)(2,1)} %param.11) | copy-start | bytes 6291460
  7.2 297.2 %reduce-scatter.5.cloned.1.call-start = ((), (), s32[]{:S(2)}) async-start(), calls=%async_computation.4 | async-start | bytes 4325376 | tf_op jit(solution)/shard_map/reduce_scatter | solution.py:41
  39.0 20.2 %collective-permute-start.1 = (bf16[2,256,2,16,64]{1,4,3,0,2:T(8,128)(2,1)}, bf16[2,256,2,16,64]{1,4,3,0,2:T(8,128)(2,1)}, u32[]{:S(2)}, u32[]{:S(2)}) collective-permute-start(bf16[2,256,2,16,64]{1,4,3,0,2:T(8,128)(2,1)} %copy.52), channel_id=1, source_target_pairs={{4,0},{8,4},{12,8},{16,12},{20,16},{24,20},{28,24},{32,28},{36,32}... | collective-permute-start | bytes 6291464 | tf_op jit(solution)/shard_map/ppermute | solution.py:58
  40.3 18.9 %collective-permute-start = (bf16[2,256,2,16,64]{1,4,3,0,2:T(8,128)(2,1)}, bf16[2,256,2,16,64]{1,4,3,0,2:T(8,128)(2,1)}, u32[]{:S(2)}, u32[]{:S(2)}) collective-permute-start(bf16[2,256,2,16,64]{1,4,3,0,2:T(8,128)(2,1)} %copy.52), channel_id=1, source_target_pairs={{0,4},{4,8},{8,12},{12,16},{16,20},{20,24},{24,28},{28,32},{32,36}... | collective-permute-start | bytes 6291464 | tf_op jit(solution)/shard_map/ppermute | solution.py:58
  105.2 52.3 %copy-start.9 = (bf16[2,16,64,256]{3,2,1,0:T(8,128)(2,1)}, bf16[2,16,64,256]{3,2,1,0:T(8,128)(2,1)S(1)}, u32[]{:S(2)}) copy-start(bf16[2,16,64,256]{3,2,1,0:T(8,128)(2,1)S(1)} %fusion.98) | copy-start | bytes 3145732
  106.5 16.7 %copy-start.13 = (bf16[2,256,1024]{2,1,0:T(8,128)(2,1)}, bf16[2,256,1024]{2,1,0:T(8,128)(2,1)S(1)}, u32[]{:S(2)}) copy-start(bf16[2,256,1024]{2,1,0:T(8,128)(2,1)S(1)} %fusion.58) | copy-start | bytes 3145732
  106.5 16.7 %copy-start.15 = (bf16[2,256,1024]{2,1,0:T(8,128)(2,1)S(1)}, bf16[2,256,1024]{2,1,0:T(8,128)(2,1)}, u32[]{:S(2)}) copy-start(bf16[2,256,1024]{2,1,0:T(8,128)(2,1)} %param.13) | copy-start | bytes 3145732
  106.5 16.7 %copy-start.20 = (f32[1,1024]{1,0:T(1,128)S(1)}, f32[1,1024]{1,0:T(1,128)}, u32[]{:S(2)}) copy-start(f32[1,1024]{1,0:T(1,128)} %get-tuple-element.84) | copy-start | bytes 12292
  106.5 16.7 %copy-start.21 = (f32[1,1024]{1,0:T(1,128)S(1)}, f32[1,1024]{1,0:T(1,128)}, u32[]{:S(2)}) copy-start(f32[1,1024]{1,0:T(1,128)} %get-tuple-element.85) | copy-start | bytes 12292
  106.5 16.7 %copy-start.22 = (f32[1,1024]{1,0:T(1,128)S(1)}, f32[1,1024]{1,0:T(1,128)}, u32[]{:S(2)}) copy-start(f32[1,1024]{1,0:T(1,128)} %get-tuple-element.86) | copy-start | bytes 12292
  106.5 16.7 %copy-start.23 = (f32[1,1024]{1,0:T(1,128)S(1)}, f32[1,1024]{1,0:T(1,128)}, u32[]{:S(2)}) copy-start(f32[1,1024]{1,0:T(1,128)} %get-tuple-element.87) | copy-start | bytes 12292
  106.6 16.7 %copy-start.24 = (f32[1,1024]{1,0:T(1,128)S(1)}, f32[1,1024]{1,0:T(1,128)}, u32[]{:S(2)}) copy-start(f32[1,1024]{1,0:T(1,128)} %get-tuple-element.88) | copy-start | bytes 12292
  106.6 16.7 %copy-start.25 = (f32[1,1024]{1,0:T(1,128)S(1)}, f32[1,1024]{1,0:T(1,128)}, u32[]{:S(2)}) copy-start(f32[1,1024]{1,0:T(1,128)} %get-tuple-element.89) | copy-start | bytes 12292
  106.6 16.7 %copy-start.26 = (f32[1,1024]{1,0:T(1,128)S(1)}, f32[1,1024]{1,0:T(1,128)}, u32[]{:S(2)}) copy-start(f32[1,1024]{1,0:T(1,128)} %get-tuple-element.90) | copy-start | bytes 12292
  106.6 16.7 %copy-start.27 = (f32[1,1024]{1,0:T(1,128)S(1)}, f32[1,1024]{1,0:T(1,128)}, u32[]{:S(2)}) copy-start(f32[1,1024]{1,0:T(1,128)} %get-tuple-element.91) | copy-start | bytes 12292
  106.6 16.7 %copy-start.28 = (f32[1,1024]{1,0:T(1,128)S(1)}, f32[1,1024]{1,0:T(1,128)}, u32[]{:S(2)}) copy-start(f32[1,1024]{1,0:T(1,128)} %get-tuple-element.92) | copy-start | bytes 12292
  106.6 16.7 %copy-start.29 = (f32[1,1024]{1,0:T(1,128)S(1)}, f32[1,1024]{1,0:T(1,128)}, u32[]{:S(2)}) copy-start(f32[1,1024]{1,0:T(1,128)} %get-tuple-element.93) | copy-start | bytes 12292
  106.6 16.7 %copy-start.30 = (f32[1,1024]{1,0:T(1,128)S(1)}, f32[1,1024]{1,0:T(1,128)}, u32[]{:S(2)}) copy-start(f32[1,1024]{1,0:T(1,128)} %get-tuple-element.94) | copy-start | bytes 12292
  106.6 16.7 %copy-start.31 = (f32[1,1024]{1,0:T(1,128)S(1)}, f32[1,1024]{1,0:T(1,128)}, u32[]{:S(2)}) copy-start(f32[1,1024]{1,0:T(1,128)} %get-tuple-element.95) | copy-start | bytes 12292
  106.9 12.3 %collective-permute-start.2 = (bf16[2,15,1024]{2,1,0:T(8,128)(2,1)S(1)}, bf16[2,15,1024]{2,1,0:T(8,128)(2,1)S(1)}, u32[]{:S(2)}, u32[]{:S(2)}) collective-permute-start(bf16[2,15,1024]{2,1,0:T(8,128)(2,1)S(1)} %get-tuple-element.63), channel_id=1, source_target_pairs={{0,4},{4,8},{8,12},{12,16},{16,20},{20,24},{24,28},{28,32},{32,36}... | collective-permute-start | bytes 184328 | tf_op jit(solution)/shard_map/ppermute | solution.py:21
  117.7 5.1 %collective-permute-start.3 = (bf16[2,15,1024]{2,1,0:T(8,128)(2,1)S(1)}, bf16[2,15,1024]{2,1,0:T(8,128)(2,1)S(1)}, u32[]{:S(2)}, u32[]{:S(2)}) collective-permute-start(bf16[2,15,1024]{2,1,0:T(8,128)(2,1)S(1)} %get-tuple-element.64), channel_id=1, source_target_pairs={{4,0},{8,4},{12,8},{16,12},{20,16},{24,20},{28,24},{32,28},{36,32}... | collective-permute-start | bytes 184328 | tf_op jit(solution)/shard_map/ppermute | solution.py:22
  123.1 22.9 %copy-start.2 = (f32[2,286,1024]{2,1,0:T(8,128)}, f32[2,286,1024]{2,1,0:T(8,128)S(1)}, u32[]{:S(2)}) copy-start(f32[2,286,1024]{2,1,0:T(8,128)S(1)} %maximum_convert_fusion) | copy-start | bytes 7028740
  150.9 8.1 %collective-permute-start.4 = (bf16[2,15,1024]{2,1,0:T(8,128)(2,1)S(1)}, bf16[2,15,1024]{2,1,0:T(8,128)(2,1)S(1)}, u32[]{:S(2)}, u32[]{:S(2)}) collective-permute-start(bf16[2,15,1024]{2,1,0:T(8,128)(2,1)S(1)} %get-tuple-element.61), channel_id=1, source_target_pairs={{0,4},{4,8},{8,12},{12,16},{16,20},{20,24},{24,28},{28,32},{32,36}... | collective-permute-start | bytes 184328 | tf_op jit(solution)/shard_map/ppermute | solution.py:21
  155.8 3.3 collective-permute-start.5
  190.8 136.3 %reduce-scatter.7.cloned.1.call-start = ((), (), s32[]{:S(2)}) async-start(), calls=%async_computation.5 | async-start | bytes 163840 | tf_op jit(solution)/shard_map/reduce_scatter | solution.py:42
  224.7 23.2 %slice-start = ((s8[6291456]{0:T(1024)(128)(4,1)}), s8[4194304]{0:T(1024)(128)(4,1)S(1)}, s32[]{:S(2)}) async-start(s8[6291456]{0:T(1024)(128)(4,1)} %bitcast.166), calls=%async_computation.8 | async-start | bytes 8388608
  229.8 18.1 %collective-permute-start.6 = (bf16[2,256,2,16,64]{1,4,3,0,2:T(8,128)(2,1)}, bf16[2,256,2,16,64]{1,4,3,0,2:T(8,128)(2,1)}, u32[]{:S(2)}, u32[]{:S(2)}) collective-permute-start(bf16[2,256,2,16,64]{1,4,3,0,2:T(8,128)(2,1)} %get-tuple-element.58), channel_id=1, source_target_pairs={{4,0},{8,4},{12,8},{16,12},{20,16},{24,20},{28,24},{32,28},{36,32}... | collective-permute-start | bytes 6291464 | tf_op jit(solution)/shard_map/ppermute | solution.py:58
  231.1 16.9 %slice-start.1 = ((s8[6291456]{0:T(1024)(128)(4,1)}), s8[2097152]{0:T(1024)(128)(4,1)S(1)}, s32[]{:S(2)}) async-start(s8[6291456]{0:T(1024)(128)(4,1)} %bitcast.166), calls=%async_computation.9 | async-start | bytes 4194304
  231.1 16.8 %collective-permute-start.7 = (bf16[2,256,2,16,64]{1,4,3,0,2:T(8,128)(2,1)}, bf16[2,256,2,16,64]{1,4,3,0,2:T(8,128)(2,1)}, u32[]{:S(2)}, u32[]{:S(2)}) collective-permute-start(bf16[2,256,2,16,64]{1,4,3,0,2:T(8,128)(2,1)} %get-tuple-element.59), channel_id=1, source_target_pairs={{0,4},{4,8},{8,12},{12,16},{16,20},{20,24},{24,28},{28,32},{32,36}... | collective-permute-start | bytes 6291464 | tf_op jit(solution)/shard_map/ppermute | solution.py:58
  304.4 130.2 %reduce-scatter.9.cloned.1.call-start = ((), (), s32[]{:S(2)}) async-start(), calls=%async_computation.6 | async-start | bytes 12976128 | tf_op jit(solution)/shard_map/reduce_scatter | solution.py:41
  327.2 130.6 %reduce-scatter.11.cloned.1.call-start = ((), (), s32[]{:S(2)}) async-start(), calls=%async_computation.7 | async-start | bytes 491520 | tf_op jit(solution)/shard_map/reduce_scatter | solution.py:42
  335.6 1.4 collective-permute-start.8
  337.0 5.6 %collective-permute-start.9 = (f32[31,1024]{1,0:T(8,128)S(1)}, f32[31,1024]{1,0:T(8,128)S(1)}, u32[]{:S(2)}, u32[]{:S(2)}) collective-permute-start(f32[31,1024]{1,0:T(8,128)S(1)} %add.424), channel_id=1, source_target_pairs={{0,8},{4,12},{8,0},{12,4},{16,24},{20,28},{24,16},{28,20},{32,40},... | collective-permute-start | bytes 380936 | tf_op jit(solution)/shard_map/ppermute | solution.py:35
  342.7 6.6 %collective-permute-start.10 = (f32[31,1024]{1,0:T(8,128)S(1)}, f32[31,1024]{1,0:T(8,128)S(1)}, u32[]{:S(2)}, u32[]{:S(2)}) collective-permute-start(f32[31,1024]{1,0:T(8,128)S(1)} %add.425), channel_id=1, source_target_pairs={{0,16},{4,20},{8,24},{12,28},{16,0},{20,4},{24,8},{28,12},{32,48},... | collective-permute-start | bytes 380936 | tf_op jit(solution)/shard_map/ppermute | solution.py:35
  349.2 5.0 %collective-permute-start.11 = (f32[31,1024]{1,0:T(8,128)S(1)}, f32[31,1024]{1,0:T(8,128)S(1)}, u32[]{:S(2)}, u32[]{:S(2)}) collective-permute-start(f32[31,1024]{1,0:T(8,128)S(1)} %add.426), channel_id=1, source_target_pairs={{0,32},{4,36},{8,40},{12,44},{16,48},{20,52},{24,56},{28,60},{32,0... | collective-permute-start | bytes 380936 | tf_op jit(solution)/shard_map/ppermute | solution.py:35
  354.4 14.3 %collective-permute-start.12 = (f32[31,1024]{1,0:T(8,128)S(1)}, f32[31,1024]{1,0:T(8,128)S(1)}, u32[]{:S(2)}, u32[]{:S(2)}) collective-permute-start(f32[31,1024]{1,0:T(8,128)S(1)} %add.427), channel_id=1, source_target_pairs={{0,64},{4,68},{8,72},{12,76},{16,80},{20,84},{24,88},{28,92},{32,9... | collective-permute-start | bytes 380936 | tf_op jit(solution)/shard_map/ppermute | solution.py:35
  359.8 19.4 %copy-start.11 = (f32[2,256,1024]{2,1,0:T(8,128)S(1)}, f32[2,256,1024]{2,1,0:T(8,128)}, u32[]{:S(2)}) copy-start(f32[2,256,1024]{2,1,0:T(8,128)} %get-tuple-element.55) | copy-start | bytes 6291460
  359.8 19.4 %copy-start.14 = (bf16[2,256,1024]{2,1,0:T(8,128)(2,1)S(1)}, bf16[2,256,1024]{2,1,0:T(8,128)(2,1)}, u32[]{:S(2)}) copy-start(bf16[2,256,1024]{2,1,0:T(8,128)(2,1)} %copy-done.13) | copy-start | bytes 3145732
  368.7 1.2 collective-permute-start.15
  368.7 6.0 %collective-permute-start.13 = (f32[31,1024]{1,0:T(8,128)S(1)}, f32[31,1024]{1,0:T(8,128)S(1)}, u32[]{:S(2)}, u32[]{:S(2)}) collective-permute-start(f32[31,1024]{1,0:T(8,128)S(1)} %add.428), channel_id=1, source_target_pairs={{0,1},{1,0},{2,3},{3,2},{4,5},{5,4},{6,7},{7,6},{8,9},{9,8},{10,11... | collective-permute-start | bytes 380936 | tf_op jit(solution)/shard_map/ppermute | solution.py:35
  369.9 6.3 %collective-permute-start.16 = (f32[8,128]{1,0:T(8,128)S(1)}, f32[8,128]{1,0:T(8,128)S(1)}, u32[]{:S(2)}, u32[]{:S(2)}) collective-permute-start(f32[8,128]{1,0:T(8,128)S(1)} %bitcast_add_fusion), channel_id=1, source_target_pairs={{0,8},{4,12},{8,0},{12,4},{16,24},{20,28},{24,16},{28,20},{32,40},... | collective-permute-start | bytes 12296 | tf_op jit(solution)/shard_map/ppermute | solution.py:35
  374.7 8.1 %collective-permute-start.14 = (f32[31,1024]{1,0:T(8,128)S(1)}, f32[31,1024]{1,0:T(8,128)S(1)}, u32[]{:S(2)}, u32[]{:S(2)}) collective-permute-start(f32[31,1024]{1,0:T(8,128)S(1)} %add.429), channel_id=1, source_target_pairs={{0,2},{1,3},{2,0},{3,1},{4,6},{5,7},{6,4},{7,5},{8,10},{9,11},{10,... | collective-permute-start | bytes 380936 | tf_op jit(solution)/shard_map/ppermute | solution.py:35
  376.2 5.1 %collective-permute-start.17 = (f32[8,128]{1,0:T(8,128)S(1)}, f32[8,128]{1,0:T(8,128)S(1)}, u32[]{:S(2)}, u32[]{:S(2)}) collective-permute-start(f32[8,128]{1,0:T(8,128)S(1)} %fusion.201), channel_id=1, source_target_pairs={{0,16},{4,20},{8,24},{12,28},{16,0},{20,4},{24,8},{28,12},{32,48},... | collective-permute-start | bytes 12296 | tf_op jit(solution)/shard_map/ppermute | solution.py:35
  381.3 3.6 collective-permute-start.18
  384.9 5.3 %collective-permute-start.19 = (f32[8,128]{1,0:T(8,128)S(1)}, f32[8,128]{1,0:T(8,128)S(1)}, u32[]{:S(2)}, u32[]{:S(2)}) collective-permute-start(f32[8,128]{1,0:T(8,128)S(1)} %add.434), channel_id=1, source_target_pairs={{0,64},{4,68},{8,72},{12,76},{16,80},{20,84},{24,88},{28,92},{32,9... | collective-permute-start | bytes 12296 | tf_op jit(solution)/shard_map/ppermute | solution.py:35
  390.3 3.6 collective-permute-start.20
  393.9 44.9 %collective-permute-start.21 = (f32[8,128]{1,0:T(8,128)S(1)}, f32[8,128]{1,0:T(8,128)S(1)}, u32[]{:S(2)}, u32[]{:S(2)}) collective-permute-start(f32[8,128]{1,0:T(8,128)S(1)} %add.436), channel_id=1, source_target_pairs={{0,2},{1,3},{2,0},{3,1},{4,6},{5,7},{6,4},{7,5},{8,10},{9,11},{10,... | collective-permute-start | bytes 12296 | tf_op jit(solution)/shard_map/ppermute | solution.py:35
  434.6 24.6 %copy-start.1 = (bf16[1024,1024]{1,0:T(8,128)(2,1)S(1)}, bf16[1024,1024]{1,0:T(8,128)(2,1)}, u32[]{:S(2)}) copy-start(bf16[1024,1024]{1,0:T(8,128)(2,1)} %param.11) | copy-start | bytes 6291460
  (75 other events, 589.1 us)
Sparse Core Ops, SparseCore 0:
  190.9 113.3 reduce-scatter.4
  306.7 20.3 reduce-scatter.6
  330.9 103.6 reduce-scatter.8
  436.9 20.8 reduce-scatter.10

commit v6 on v4

--- a/solution.py
+++ b/solution.py
@@ -131,19 +131,11 @@
         grad_conv.dtype
     )
     grad_hidden = incoming
-    kernel_rows = []
     for tap_index in range(kernel.shape[0]):
         back_index = 2 * conv_reach - tap_index
         same_back = (segment_ext[:, back_index : back_index + frames] == segment_local)[..., None]
         grad_hidden = grad_hidden + jnp.where(
             same_back, kernel[tap_index] * grad_pad[:, back_index : back_index + frames], 0.0
-        )
-        same_seg = (segment_ext[:, tap_index : tap_index + frames] == segment_local)[..., None]
-        kernel_rows.append(
-            jnp.sum(
-                jnp.where(same_seg, grad_conv * padded[:, tap_index : tap_index + frames], 0.0),
-                axis=(0, 1),
-            )
         )
     grad_hidden_b = grad_hidden.astype(jnp.bfloat16)
     flat_grad_hidden = grad_hidden_b.reshape(-1, model_width)
@@ -190,8 +182,7 @@
     )
     gain_sum = jnp.sum(grad_normed * unit_rows, axis=(0, 1))
     contract_rows = (((0,), (0,)), ((), ()))
-    summed = staged_scatter(
-        jnp.concatenate(
+    weight_partial = jnp.concatenate(
             [
                 lax.dot_general(
                     flat_normed, flat_grad_qkv, contract_rows, preferred_element_type=jnp.float32
@@ -205,7 +196,19 @@
             ],
             axis=1,
         )
-    )
+    weight_partial, late_conv, late_padded = lax.optimization_barrier(
+        (weight_partial, grad_conv, padded)
+    )
+    summed = staged_scatter(weight_partial)
+    kernel_rows = []
+    for tap_index in range(kernel.shape[0]):
+        same_seg = (segment_ext[:, tap_index : tap_index + frames] == segment_local)[..., None]
+        kernel_rows.append(
+            jnp.sum(
+                jnp.where(same_seg, late_conv * late_padded[:, tap_index : tap_index + frames], 0.0),
+                axis=(0, 1),
+            )
+        )
     small_sums = (
         exchange_sum(jnp.stack(kernel_rows), ("seq", "dp")),
         exchange_sum(gain_sum.reshape(8, -1), ("seq", "dp")).reshape(-1),

time: 445 us -> 436 us (0.980)
    reduce_sum x4, other arithmetic: 33.8 us -> 12.9 us  [local(): jnp.sum(jnp.where(same_seg, late_conv * late_padded[:, tap_index:tap_inde...]
    convert_element_type x0 -> x1, other arithmetic: none -> 14.2 us  [local(): grad_conv.astype(jnp.bfloat16)]
    reduce_scatter x1, waiting for transfers between devices: 53.6 us -> 65.3 us  [staged_scatter(): partial = lax.psum_scatter(partial, 'seq', scatter_dimension=0, tiled=True)]
    ppermute x14, waiting for transfers between devices: 21.5 us -> 13.4 us  [exchange_sum(): lax.ppermute(value, axis, [(i, i ^ bit) for i in range(size)])]
    reduce_scatter x1, waiting for transfers between devices: 12.1 us -> 7.42 us  [staged_scatter(): return lax.psum_scatter(partial, 'dp', scatter_dimension=0, tiled=True)]
    unnamed x200 -> x186, local copies, waits for them, and re-layouts: 15.2 us -> 13.7 us
  transfers between devices with their start and end apart: 24 -> 24, of which waited for: 12 -> 10; matrix products, arithmetic and copies ran while one was open for 12% -> 14% of each run, Pallas kernels for 0% -> 0%
where the time goes in v6:
time: 436 us; the launch traced here: 431 us
  other arithmetic  100 us (23%)
  matrix products  97.1 us (22%)
  waiting for transfers between devices  91.3 us (21%)
  starting transfers between devices  75.8 us (17%)
  local copies, waits for them, and re-layouts  50.4 us (12%)
  between operations  16.1 us (4%)
    reduce_scatter x1, waiting for transfers between devices, staged_scatter(): partial = lax.psum_scatter(partial, 'seq', scatter_dimension=0, tiled=True)  65.3 us
    ppermute x14, starting transfers between devices, exchange_sum(): lax.ppermute(value, axis, [(i, i ^ bit) for i in range(size)])  43.6 us
    sub x1, matrix products, local(): exponent = jnp.where(allowed, jnp.exp(scores - row_max), 0.0)  17.3 us
    ppermute x2, starting transfers between devices, with_halo(): before = lax.ppermute(last, axis, up)  15.5 us
    dot_general x1, matrix products, local(): jnp.einsum('bqhd,bkhd->bhqk', grad_heads, head_values, preferred_element_...  15 us
    convert_element_type x1, other arithmetic, local(): grad_conv.astype(jnp.bfloat16)  14.2 us
    unnamed x186, local copies, waits for them, and re-layouts  13.7 us
    ppermute x4, starting transfers between devices, from_neighbour(): return lax.ppermute(shard, axis, pairs)  13.6 us
  transfers between devices with their start and end apart: 24, of which 10 were waited for; matrix products, arithmetic and copies ran while one was open for 14% of the time, Pallas kernels for 0%

profile of v6, /device:TPU:0, one launch (start us, length us, event | category | flops | bytes accessed | tf_op | source)
XLA Modules:
  0.0 431.0 jit_solution(4806677001353593269)
XLA Ops:
  12.1 7.6 %convolution_convert_fusion = bf16[512,3072]{1,0:T(8,128)(2,1)} fusion(bf16[512,1024]{1,0:T(8,128)(2,1)S(1)} %bitcast.174, bf16[1024,3072]{1,0:T(8,128)(2,1)} %param.10), kind=kOutput, calls=%fused_computation.18 | convolution fusion | flops 3222798336 | bytes 10485760 | tf_op jit(solution)/shard_map/dot_general | solution.py:82
  19.7 8.6 %reshape.285 = bf16[2,256,3,16,64]{4,3,2,1,0:T(8,128)(2,1)} reshape(bf16[512,3072]{1,0:T(8,128)(2,1)} %convolution_convert_fusion) | data formatting | bytes 6291456 | tf_op jit(solution)/shard_map/reshape;reshape | solution.py:86
  28.3 4.9 %slice.779 = bf16[2,256,2,16,64]{4,3,2,1,0:T(8,128)(2,1)} slice(bf16[2,256,3,16,64]{4,3,2,1,0:T(8,128)(2,1)} %reshape.285), slice={[0:2], [0:256], [1:3], [0:16], [0:64]} | slice | bytes 4194304 | tf_op jit(solution)/shard_map/slice | solution.py:88
  33.2 5.8 %copy.56 = bf16[2,256,2,16,64]{1,4,3,0,2:T(8,128)(2,1)} copy(bf16[2,256,2,16,64]{4,3,2,1,0:T(8,128)(2,1)} %slice.779) | data formatting | bytes 4194304
  40.3 4.6 %collective-permute-start = (bf16[2,256,2,16,64]{1,4,3,0,2:T(8,128)(2,1)}, bf16[2,256,2,16,64]{1,4,3,0,2:T(8,128)(2,1)}, u32[]{:S(2)}, u32[]{:S(2)}) collective-permute-start(bf16[2,256,2,16,64]{1,4,3,0,2:T(8,128)(2,1)} %copy.56), channel_id=1, source_target_pairs={{0,4},{4,8},{8,12},{12,16},{16,20},{20,24},{24,28},{28,32},{32,36}... | collective-permute-start | bytes 6291464 | tf_op jit(solution)/shard_map/ppermute | solution.py:58
  45.0 3.4 slice.781
  49.2 3.6 copy.57
  59.3 5.9 %pad_maximum_fusion.2 = bf16[2,768,2,16,64]{1,4,3,0,2:T(8,128)(2,1)} fusion(bf16[2,256,2,16,64]{1,4,3,0,2:T(8,128)(2,1)} %collective-permute-done.1, bf16[2,256,2,16,64]{1,4,3,0,2:T(8,128)(2,1)} %copy.56, bf16[2,256,2,16,64]{1,4,3,0,2:T(8,128)(2,1)} %collective-permute-done), kind=kLoop, calls=%fused_computation.15 | loop fusion | flops 18874368 | bytes 12582912 | tf_op jit(solution)/shard_map/concatenate | solution.py:89
  65.2 17.3 %fusion.241 = (f32[2,16,256]{2,1,0:T(8,128)}, f32[2,16,256,768]{3,2,1,0:T(8,128)}) fusion(pred[2,256,768]{2,1,0:T(8,128)(4,1)S(1)} %broadcast_compare_fusion, bf16[2,768,2,16,64]{1,4,3,0,2:T(8,128)(2,1)} %pad_maximum_fusion.2, bf16[2,256,1,16,64]{1,4,3,0,2:T(8,128)(2,1)} %copy.57), kind=kOutput, calls=%fused_computation.446 | convolution fusion | flops 836764416 | bytes 30179328 | tf_op jit(solution)/shard_map/sub | solution.py:105
  82.6 13.3 %fusion.6 = bf16[2,16,256,768]{3,2,1,0:T(8,128)(2,1)} fusion(f32[2,16,256,768]{3,2,1,0:T(8,128)} %get-tuple-element.128, f32[2,16,256]{2,1,0:T(8,128)} %get-tuple-element.127), kind=kLoop, calls=%fused_computation.14 | loop fusion | flops 12582912 | bytes 37781504 | tf_op jit(solution)/shard_map/convert_element_type | solution.py:107
  95.9 9.4 %fusion.159 = bf16[2,16,64,256]{3,2,1,0:T(8,128)(2,1)S(1)} fusion(bf16[2,16,256,768]{3,2,1,0:T(8,128)(2,1)} %fusion.6, bf16[2,768,2,16,64]{1,4,3,0,2:T(8,128)(2,1)} %pad_maximum_fusion.2), kind=kOutput, calls=%fused_computation.276 | convolution fusion | flops 805830656 | bytes 16777216 | tf_op jit(solution)/shard_map/bhqk,bkhd->bqhd/dot_general | solution.py:108
  107.1 10.7 %collective-permute-start.2 = (bf16[2,15,1024]{2,1,0:T(8,128)(2,1)S(1)}, bf16[2,15,1024]{2,1,0:T(8,128)(2,1)S(1)}, u32[]{:S(2)}, u32[]{:S(2)}) collective-permute-start(bf16[2,15,1024]{2,1,0:T(8,128)(2,1)S(1)} %get-tuple-element.61), channel_id=1, source_target_pairs={{0,4},{4,8},{8,12},{12,16},{16,20},{20,24},{24,28},{28,32},{32,36}... | collective-permute-start | bytes 184328 | tf_op jit(solution)/shard_map/ppermute | solution.py:21
  119.6 3.3 collective-permute-done.3
  123.6 14.2 %fusion.233 = (bf16[2,256,1024]{2,1,0:T(8,128)(2,1)S(1)}, f32[2,256,1024]{2,1,0:T(8,128)}, f32[2,256,1024]{2,1,0:T(8,128)}) fusion(bf16[2,256,1024]{2,1,0:T(8,128)(2,1)S(1)} %copy-done.10, f32[2,286,1024]{2,1,0:T(8,128)S(1)} %maximum_convert_fusion, f32[1024]{0:T(1024)S(1)} %bitcast.197, pred[2,256]{1,0:T(4,128)(4,1)S(1)} %get-tuple-element.123, ...), kind=kLoop, calls=%fused_computation.440 | loop fusion | flops 53477376 | bytes 71446016 | tf_op jit(solution)/shard_map/convert_element_type | solution.py:130
  138.1 4.8 %collective-permute-start.4 = (bf16[2,15,1024]{2,1,0:T(8,128)(2,1)S(1)}, bf16[2,15,1024]{2,1,0:T(8,128)(2,1)S(1)}, u32[]{:S(2)}, u32[]{:S(2)}) collective-permute-start(bf16[2,15,1024]{2,1,0:T(8,128)(2,1)S(1)} %get-tuple-element.59), channel_id=1, source_target_pairs={{0,4},{4,8},{8,12},{12,16},{16,20},{20,24},{24,28},{28,32},{32,36}... | collective-permute-start | bytes 184328 | tf_op jit(solution)/shard_map/ppermute | solution.py:21
  146.7 12.5 %fusion.231 = (bf16[2,256,1024]{2,1,0:T(8,128)(2,1)S(1)}, f32[2,256,1024]{2,1,0:T(8,128)}) fusion(f32[2,286,1024]{2,1,0:T(8,128)S(1)} %maximum_convert_fusion.1, f32[1024]{0:T(1024)S(1)} %bitcast.198, pred[2,256]{1,0:T(4,128)(4,1)S(1)} %copy-done.53, f32[1024]{0:T(1024)S(1)} %bitcast.200, pred[2,256]{1,0:T(4,128)(4,1)S(1)} %copy-done.54, ...), kind=kLoop, calls=%fused_computation.439 | loop fusion | flops 49807360 | bytes 69348864 | tf_op jit(solution)/shard_map/convert_element_type | solution.py:140
  160.2 2.3 convolution_convert_fusion.1
  162.4 4.0 reshape.286
  166.4 2.8 copy.41
  169.2 9.5 %convolution_bitcast_fusion = f32[2,768,1,16,64]{1,4,3,0,2:T(8,128)} fusion(bf16[2,256,16,64]{1,3,2,0:T(8,128)(2,1)S(1)} %copy.41, bf16[2,16,256,768]{3,2,1,0:T(8,128)(2,1)} %fusion.6), kind=kOutput, calls=%fused_computation.31 | convolution fusion | flops 805306368 | bytes 19922944 | tf_op jit(solution)/shard_map/bhqk,bqhd->bkhd/dot_general | solution.py:149
  179.5 15.0 %multiply_convert_fusion = bf16[2,16,256,768]{3,2,1,0:T(8,128)(2,1)} fusion(f32[2,16,256]{2,1,0:T(8,128)S(1)} %bitcast.239, f32[2,16,256,768]{3,2,1,0:T(8,128)} %get-tuple-element.128, f32[2,16,256]{2,1,0:T(8,128)S(1)} %copy-done.50, bf16[2,256,16,64]{1,3,2,0:T(8,128)(2,1)S(1)} %copy.41, bf16[2,768,2,16,64]{1,4,3,0,2:T(8,128)(2,1)} %pad_maximum_fusion.2), kind=kOutput, calls=%fused_computation.1 | convolution fusion | flops 836763648 | bytes 42008576 | tf_op jit(solution)/shard_map/bqhd,bkhd->bhqk/dot_general | solution.py:152
  194.6 9.9 %convolution_bitcast_fusion.1 = f32[2,768,1,16,64]{1,4,3,0,2:T(8,128)} fusion(bf16[2,16,256,768]{3,2,1,0:T(8,128)(2,1)} %multiply_convert_fusion, bf16[2,256,1,16,64]{1,4,3,0,2:T(8,128)(2,1)} %copy.57), kind=kOutput, calls=%fused_computation.32 | convolution fusion | flops 805306368 | bytes 19922944 | tf_op jit(solution)/shard_map/bhqk,bqhd->bkhd/dot_general | solution.py:159
  204.4 8.2 %fusion.2 = bf16[2,768,2,16,64]{1,4,3,0,2:T(8,128)(2,1)} fusion(f32[2,768,1,16,64]{1,4,3,0,2:T(8,128)} %convolution_bitcast_fusion, f32[2,768,1,16,64]{1,4,3,0,2:T(8,128)} %convolution_bitcast_fusion.1), kind=kLoop, calls=%fused_computation.9 | loop fusion | flops 3145728 | bytes 18874368 | tf_op jit(solution)/shard_map/convert.1
  212.6 4.8 %fusion.236 = (bf16[2,256,2,16,64]{1,4,3,0,2:T(8,128)(2,1)}, bf16[2,256,2,16,64]{1,4,3,0,2:T(8,128)(2,1)}) fusion(bf16[2,768,2,16,64]{1,4,3,0,2:T(8,128)(2,1)} %fusion.2), kind=kLoop, calls=%fused_computation.441 | loop fusion | bytes 8388608 | tf_op jit(solution)/shard_map/slice | solution.py:165
  218.7 6.4 %collective-permute-start.7 = (bf16[2,256,2,16,64]{1,4,3,0,2:T(8,128)(2,1)}, bf16[2,256,2,16,64]{1,4,3,0,2:T(8,128)(2,1)}, u32[]{:S(2)}, u32[]{:S(2)}) collective-permute-start(bf16[2,256,2,16,64]{1,4,3,0,2:T(8,128)(2,1)} %get-tuple-element.58), channel_id=1, source_target_pairs={{0,4},{4,8},{8,12},{12,16},{16,20},{20,24},{24,28},{28,32},{32,36}... | collective-permute-start | bytes 6291464 | tf_op jit(solution)/shard_map/ppermute | solution.py:58
  226.5 3.3 fusion.247
  229.8 9.4 %fusion.162 = bf16[2,256,1,16,64]{1,4,3,0,2:T(8,128)(2,1)S(1)} fusion(bf16[2,16,256,768]{3,2,1,0:T(8,128)(2,1)} %multiply_convert_fusion, bf16[2,768,2,16,64]{1,4,3,0,2:T(8,128)(2,1)} %pad_maximum_fusion.2), kind=kOutput, calls=%fused_computation.277 | convolution fusion | flops 805830656 | bytes 16777216 | tf_op jit(solution)/shard_map/bhqk,bkhd->bqhd/dot_general | solution.py:156
  239.2 4.0 fusion.12
  243.5 3.3 copy.46
  248.1 3.7 fusion.246
  251.8 6.0 %pad_maximum_fusion = f32[1024,4096]{1,0:T(8,128)} fusion(f32[1024,1024]{1,0:T(8,128)S(1)} %copy-done.11, f32[1024,3072]{1,0:T(8,128)S(1)} %fusion.246), kind=kLoop, calls=%fused_computation.5 | loop fusion | flops 4194304 | bytes 33554432 | tf_op jit(solution)/shard_map/concatenate | solution.py:185
  260.1 8.3 %fusion.30 = (f32[1024]{0:T(1024)S(1)}, f32[2,256]{1,0:T(2,128)S(1)}, f32[2,256]{1,0:T(2,128)S(1)}, f32[2,256,1024]{2,1,0:T(8,128)}) fusion(bf16[2,256,1024]{2,1,0:T(8,128)(2,1)S(1)} %copy-done.6, f32[2,256]{1,0:T(2,128)S(1)} %copy-done.52, f32[2,256]{1,0:T(2,128)S(1)} %copy-done.49, f32[1024]{0:T(1024)S(1)} %copy-done.89, ...), kind=kOutput, calls=%fused_computation.49 | convolution fusion | flops 3225942016 | bytes 12599296 | tf_op jit(solution)/shard_map/dot_general | solution.py:175
  268.4 9.5 %collective-permute-start.15 = (f32[8,128]{1,0:T(8,128)S(1)}, f32[8,128]{1,0:T(8,128)S(1)}, u32[]{:S(2)}, u32[]{:S(2)}) collective-permute-start(f32[8,128]{1,0:T(8,128)S(1)} %bitcast.244), channel_id=1, source_target_pairs={{0,4},{4,0},{8,12},{12,8},{16,20},{20,16},{24,28},{28,24},{32,36},... | collective-permute-start | bytes 12296 | tf_op jit(solution)/shard_map/ppermute | solution.py:35
  277.9 3.8 select_reduce_fusion.18
  281.8 3.8 select_reduce_fusion.9
  285.7 3.9 select_reduce_fusion
  291.3 2.8 collective-permute-start.16
  295.8 12.1 %collective-permute-start.17 = (f32[8,128]{1,0:T(8,128)S(1)}, f32[8,128]{1,0:T(8,128)S(1)}, u32[]{:S(2)}, u32[]{:S(2)}) collective-permute-start(f32[8,128]{1,0:T(8,128)S(1)} %fusion.264), channel_id=1, source_target_pairs={{0,16},{4,20},{8,24},{12,28},{16,0},{20,4},{24,8},{28,12},{32,48},... | collective-permute-start | bytes 12296 | tf_op jit(solution)/shard_map/ppermute | solution.py:35
  307.9 3.5 collective-permute-done.17
  311.4 4.4 %collective-permute-start.18 = (f32[8,128]{1,0:T(8,128)S(1)}, f32[8,128]{1,0:T(8,128)S(1)}, u32[]{:S(2)}, u32[]{:S(2)}) collective-permute-start(f32[8,128]{1,0:T(8,128)S(1)} %add.429), channel_id=1, source_target_pairs={{0,32},{4,36},{8,40},{12,44},{16,48},{20,52},{24,56},{28,60},{32,0... | collective-permute-start | bytes 12296 | tf_op jit(solution)/shard_map/ppermute | solution.py:35
  316.4 3.9 add_convert_fusion
  320.2 3.0 collective-permute-start.19
  328.8 2.4 collective-permute-start.12
  331.1 65.3 %reduce-scatter.3.cloned.1.call-done = f32[32,4096]{1,0:T(8,128)} async-done(((f32[1024,4096]{1,0:T(8,128)}), f32[32,4096]{1,0:T(8,128)}) %reduce-scatter.3.cloned.1.call-update) | async-done | bytes 524304 | tf_op jit(solution)/shard_map/reduce_scatter | solution.py:41
  396.5 3.2 collective-permute-start.21
  400.4 4.1 fusion.29
  407.1 5.7 %collective-permute-done.14 = f32[31,1024]{1,0:T(8,128)S(1)} collective-permute-done((f32[31,1024]{1,0:T(8,128)S(1)}, f32[31,1024]{1,0:T(8,128)S(1)}, u32[]{:S(2)}, u32[]{:S(2)}) %collective-permute-start.14) | collective-permute-done | bytes 127008 | tf_op jit(solution)/shard_map/ppermute | solution.py:35
  413.5 7.4 %reduce-scatter.5.cloned.1.call-done = f32[8,4096]{1,0:T(8,128)} async-done(((f32[32,4096]{1,0:T(8,128)}), f32[8,4096]{1,0:T(8,128)}) %reduce-scatter.5.cloned.1.call-update) | async-done | bytes 131088 | tf_op jit(solution)/shard_map/reduce_scatter | solution.py:42
  (281 shorter events, 45.1 us)
Async XLA Ops:
  7.2 98.1 %copy-start = (bf16[1024,1024]{1,0:T(8,128)(2,1)S(1)}, bf16[1024,1024]{1,0:T(8,128)(2,1)}, u32[]{:S(2)}) copy-start(bf16[1024,1024]{1,0:T(8,128)(2,1)} %param.11) | copy-start | bytes 6291460
  7.2 389.2 %reduce-scatter.3.cloned.1.call-start = ((), (), s32[]{:S(2)}) async-start(), calls=%async_computation.2 | async-start | bytes 17301504 | tf_op jit(solution)/shard_map/reduce_scatter | solution.py:41
  39.1 20.3 %collective-permute-start.1 = (bf16[2,256,2,16,64]{1,4,3,0,2:T(8,128)(2,1)}, bf16[2,256,2,16,64]{1,4,3,0,2:T(8,128)(2,1)}, u32[]{:S(2)}, u32[]{:S(2)}) collective-permute-start(bf16[2,256,2,16,64]{1,4,3,0,2:T(8,128)(2,1)} %copy.56), channel_id=1, source_target_pairs={{4,0},{8,4},{12,8},{16,12},{20,16},{24,20},{28,24},{32,28},{36,32}... | collective-permute-start | bytes 6291464 | tf_op jit(solution)/shard_map/ppermute | solution.py:58
  40.3 19.0 %collective-permute-start = (bf16[2,256,2,16,64]{1,4,3,0,2:T(8,128)(2,1)}, bf16[2,256,2,16,64]{1,4,3,0,2:T(8,128)(2,1)}, u32[]{:S(2)}, u32[]{:S(2)}) collective-permute-start(bf16[2,256,2,16,64]{1,4,3,0,2:T(8,128)(2,1)} %copy.56), channel_id=1, source_target_pairs={{0,4},{4,8},{8,12},{12,16},{16,20},{20,24},{24,28},{28,32},{32,36}... | collective-permute-start | bytes 6291464 | tf_op jit(solution)/shard_map/ppermute | solution.py:58
  106.6 31.3 %copy-start.9 = (bf16[2,256,1024]{2,1,0:T(8,128)(2,1)}, bf16[2,256,1024]{2,1,0:T(8,128)(2,1)S(1)}, u32[]{:S(2)}) copy-start(bf16[2,256,1024]{2,1,0:T(8,128)(2,1)S(1)} %fusion.58) | copy-start | bytes 3145732
  106.6 16.6 %copy-start.10 = (bf16[2,256,1024]{2,1,0:T(8,128)(2,1)S(1)}, bf16[2,256,1024]{2,1,0:T(8,128)(2,1)}, u32[]{:S(2)}) copy-start(bf16[2,256,1024]{2,1,0:T(8,128)(2,1)} %param.13) | copy-start | bytes 3145732
  106.6 16.6 %copy-start.17 = (f32[1,1024]{1,0:T(1,128)S(1)}, f32[1,1024]{1,0:T(1,128)}, u32[]{:S(2)}) copy-start(f32[1,1024]{1,0:T(1,128)} %get-tuple-element.82) | copy-start | bytes 12292
  106.7 16.6 %copy-start.18 = (f32[1,1024]{1,0:T(1,128)S(1)}, f32[1,1024]{1,0:T(1,128)}, u32[]{:S(2)}) copy-start(f32[1,1024]{1,0:T(1,128)} %get-tuple-element.83) | copy-start | bytes 12292
  106.7 16.6 %copy-start.19 = (f32[1,1024]{1,0:T(1,128)S(1)}, f32[1,1024]{1,0:T(1,128)}, u32[]{:S(2)}) copy-start(f32[1,1024]{1,0:T(1,128)} %get-tuple-element.84) | copy-start | bytes 12292
  106.7 16.6 %copy-start.20 = (f32[1,1024]{1,0:T(1,128)S(1)}, f32[1,1024]{1,0:T(1,128)}, u32[]{:S(2)}) copy-start(f32[1,1024]{1,0:T(1,128)} %get-tuple-element.85) | copy-start | bytes 12292
  106.7 16.6 %copy-start.21 = (f32[1,1024]{1,0:T(1,128)S(1)}, f32[1,1024]{1,0:T(1,128)}, u32[]{:S(2)}) copy-start(f32[1,1024]{1,0:T(1,128)} %get-tuple-element.86) | copy-start | bytes 12292
  106.7 16.6 %copy-start.22 = (f32[1,1024]{1,0:T(1,128)S(1)}, f32[1,1024]{1,0:T(1,128)}, u32[]{:S(2)}) copy-start(f32[1,1024]{1,0:T(1,128)} %get-tuple-element.87) | copy-start | bytes 12292
  106.7 16.6 %copy-start.23 = (f32[1,1024]{1,0:T(1,128)S(1)}, f32[1,1024]{1,0:T(1,128)}, u32[]{:S(2)}) copy-start(f32[1,1024]{1,0:T(1,128)} %get-tuple-element.88) | copy-start | bytes 12292
  106.7 16.6 %copy-start.24 = (f32[1,1024]{1,0:T(1,128)S(1)}, f32[1,1024]{1,0:T(1,128)}, u32[]{:S(2)}) copy-start(f32[1,1024]{1,0:T(1,128)} %get-tuple-element.89) | copy-start | bytes 12292
  106.7 16.6 %copy-start.25 = (f32[1,1024]{1,0:T(1,128)S(1)}, f32[1,1024]{1,0:T(1,128)}, u32[]{:S(2)}) copy-start(f32[1,1024]{1,0:T(1,128)} %get-tuple-element.90) | copy-start | bytes 12292
  106.7 16.6 %copy-start.26 = (f32[1,1024]{1,0:T(1,128)S(1)}, f32[1,1024]{1,0:T(1,128)}, u32[]{:S(2)}) copy-start(f32[1,1024]{1,0:T(1,128)} %get-tuple-element.91) | copy-start | bytes 12292
  106.7 16.6 %copy-start.27 = (f32[1,1024]{1,0:T(1,128)S(1)}, f32[1,1024]{1,0:T(1,128)}, u32[]{:S(2)}) copy-start(f32[1,1024]{1,0:T(1,128)} %get-tuple-element.92) | copy-start | bytes 12292
  106.8 16.6 %copy-start.28 = (f32[1,1024]{1,0:T(1,128)S(1)}, f32[1,1024]{1,0:T(1,128)}, u32[]{:S(2)}) copy-start(f32[1,1024]{1,0:T(1,128)} %get-tuple-element.93) | copy-start | bytes 12292
  106.8 16.6 %copy-start.29 = (f32[1,1024]{1,0:T(1,128)S(1)}, f32[1,1024]{1,0:T(1,128)}, u32[]{:S(2)}) copy-start(f32[1,1024]{1,0:T(1,128)} %get-tuple-element.63) | copy-start | bytes 12292
  106.8 16.6 %copy-start.30 = (f32[1,1024]{1,0:T(1,128)S(1)}, f32[1,1024]{1,0:T(1,128)}, u32[]{:S(2)}) copy-start(f32[1,1024]{1,0:T(1,128)} %get-tuple-element.64) | copy-start | bytes 12292
  106.8 16.6 %copy-start.31 = (f32[1,1024]{1,0:T(1,128)S(1)}, f32[1,1024]{1,0:T(1,128)}, u32[]{:S(2)}) copy-start(f32[1,1024]{1,0:T(1,128)} %get-tuple-element.65) | copy-start | bytes 12292
  107.1 12.5 %collective-permute-start.2 = (bf16[2,15,1024]{2,1,0:T(8,128)(2,1)S(1)}, bf16[2,15,1024]{2,1,0:T(8,128)(2,1)S(1)}, u32[]{:S(2)}, u32[]{:S(2)}) collective-permute-start(bf16[2,15,1024]{2,1,0:T(8,128)(2,1)S(1)} %get-tuple-element.61), channel_id=1, source_target_pairs={{0,4},{4,8},{8,12},{12,16},{16,20},{20,24},{24,28},{28,32},{32,36}... | collective-permute-start | bytes 184328 | tf_op jit(solution)/shard_map/ppermute | solution.py:21
  117.7 5.1 %collective-permute-start.3 = (bf16[2,15,1024]{2,1,0:T(8,128)(2,1)S(1)}, bf16[2,15,1024]{2,1,0:T(8,128)(2,1)S(1)}, u32[]{:S(2)}, u32[]{:S(2)}) collective-permute-start(bf16[2,15,1024]{2,1,0:T(8,128)(2,1)S(1)} %get-tuple-element.62), channel_id=1, source_target_pairs={{4,0},{8,4},{12,8},{16,12},{20,16},{24,20},{28,24},{32,28},{36,32}... | collective-permute-start | bytes 184328 | tf_op jit(solution)/shard_map/ppermute | solution.py:22
  119.5 26.9 %copy-start.82 = (pred[2,256]{1,0:T(4,128)(4,1)}, pred[2,256]{1,0:T(4,128)(4,1)S(1)}, u32[]{:S(2)}) copy-start(pred[2,256]{1,0:T(4,128)(4,1)S(1)} %get-tuple-element.122) | copy-start | bytes 1540
  119.5 26.9 %copy-start.84 = (pred[2,256]{1,0:T(4,128)(4,1)}, pred[2,256]{1,0:T(4,128)(4,1)S(1)}, u32[]{:S(2)}) copy-start(pred[2,256]{1,0:T(4,128)(4,1)S(1)} %get-tuple-element.123) | copy-start | bytes 1540
  119.6 26.9 %copy-start.86 = (pred[2,256]{1,0:T(4,128)(4,1)}, pred[2,256]{1,0:T(4,128)(4,1)S(1)}, u32[]{:S(2)}) copy-start(pred[2,256]{1,0:T(4,128)(4,1)S(1)} %get-tuple-element.124) | copy-start | bytes 1540
  138.1 6.2 %collective-permute-start.4 = (bf16[2,15,1024]{2,1,0:T(8,128)(2,1)S(1)}, bf16[2,15,1024]{2,1,0:T(8,128)(2,1)S(1)}, u32[]{:S(2)}, u32[]{:S(2)}) collective-permute-start(bf16[2,15,1024]{2,1,0:T(8,128)(2,1)S(1)} %get-tuple-element.59), channel_id=1, source_target_pairs={{0,4},{4,8},{8,12},{12,16},{16,20},{20,24},{24,28},{28,32},{32,36}... | collective-permute-start | bytes 184328 | tf_op jit(solution)/shard_map/ppermute | solution.py:21
  143.0 3.1 collective-permute-start.5
  217.4 21.8 %collective-permute-start.6 = (bf16[2,256,2,16,64]{1,4,3,0,2:T(8,128)(2,1)}, bf16[2,256,2,16,64]{1,4,3,0,2:T(8,128)(2,1)S(1)}, u32[]{:S(2)}, u32[]{:S(2)}) collective-permute-start(bf16[2,256,2,16,64]{1,4,3,0,2:T(8,128)(2,1)} %get-tuple-element.57), channel_id=1, source_target_pairs={{4,0},{8,4},{12,8},{16,12},{20,16},{24,20},{28,24},{32,28},{36,32}... | collective-permute-start | bytes 6291464 | tf_op jit(solution)/shard_map/ppermute | solution.py:58
  218.7 20.5 %collective-permute-start.7 = (bf16[2,256,2,16,64]{1,4,3,0,2:T(8,128)(2,1)}, bf16[2,256,2,16,64]{1,4,3,0,2:T(8,128)(2,1)}, u32[]{:S(2)}, u32[]{:S(2)}) collective-permute-start(bf16[2,256,2,16,64]{1,4,3,0,2:T(8,128)(2,1)} %get-tuple-element.58), channel_id=1, source_target_pairs={{0,4},{4,8},{8,12},{12,16},{16,20},{20,24},{24,28},{28,32},{32,36}... | collective-permute-start | bytes 6291464 | tf_op jit(solution)/shard_map/ppermute | solution.py:58
  257.9 163.0 %reduce-scatter.5.cloned.1.call-start = ((), (), s32[]{:S(2)}) async-start(), calls=%async_computation.3 | async-start | bytes 655360 | tf_op jit(solution)/shard_map/reduce_scatter | solution.py:42
  260.1 17.8 %copy-start.3 = (f32[2,286,1024]{2,1,0:T(8,128)S(1)}, f32[2,286,1024]{2,1,0:T(8,128)}, u32[]{:S(2)}) copy-start(f32[2,286,1024]{2,1,0:T(8,128)} %copy-done.2) | copy-start | bytes 7028740
  260.1 17.8 %copy-start.4 = (f32[2,256,1024]{2,1,0:T(8,128)S(1)}, f32[2,256,1024]{2,1,0:T(8,128)}, u32[]{:S(2)}) copy-start(f32[2,256,1024]{2,1,0:T(8,128)} %get-tuple-element.10) | copy-start | bytes 6291460
  268.4 22.9 %collective-permute-start.15 = (f32[8,128]{1,0:T(8,128)S(1)}, f32[8,128]{1,0:T(8,128)S(1)}, u32[]{:S(2)}, u32[]{:S(2)}) collective-permute-start(f32[8,128]{1,0:T(8,128)S(1)} %bitcast.244), channel_id=1, source_target_pairs={{0,4},{4,0},{8,12},{12,8},{16,20},{20,16},{24,28},{28,24},{32,36},... | collective-permute-start | bytes 12296 | tf_op jit(solution)/shard_map/ppermute | solution.py:35
  291.2 3.0 collective-permute-start.8
  291.3 4.4 %collective-permute-start.16 = (f32[8,128]{1,0:T(8,128)S(1)}, f32[8,128]{1,0:T(8,128)S(1)}, u32[]{:S(2)}, u32[]{:S(2)}) collective-permute-start(f32[8,128]{1,0:T(8,128)S(1)} %bitcast_add_fusion), channel_id=1, source_target_pairs={{0,8},{4,12},{8,0},{12,4},{16,24},{20,28},{24,16},{28,20},{32,40},... | collective-permute-start | bytes 12296 | tf_op jit(solution)/shard_map/ppermute | solution.py:35
  294.2 21.6 %collective-permute-start.9 = (f32[31,1024]{1,0:T(8,128)S(1)}, f32[31,1024]{1,0:T(8,128)S(1)}, u32[]{:S(2)}, u32[]{:S(2)}) collective-permute-start(f32[31,1024]{1,0:T(8,128)S(1)} %add.420), channel_id=1, source_target_pairs={{0,8},{4,12},{8,0},{12,4},{16,24},{20,28},{24,16},{28,20},{32,40},... | collective-permute-start | bytes 380936 | tf_op jit(solution)/shard_map/ppermute | solution.py:35
  295.8 15.6 %collective-permute-start.17 = (f32[8,128]{1,0:T(8,128)S(1)}, f32[8,128]{1,0:T(8,128)S(1)}, u32[]{:S(2)}, u32[]{:S(2)}) collective-permute-start(f32[8,128]{1,0:T(8,128)S(1)} %fusion.264), channel_id=1, source_target_pairs={{0,16},{4,20},{8,24},{12,28},{16,0},{20,4},{24,8},{28,12},{32,48},... | collective-permute-start | bytes 12296 | tf_op jit(solution)/shard_map/ppermute | solution.py:35
  311.4 8.8 %collective-permute-start.18 = (f32[8,128]{1,0:T(8,128)S(1)}, f32[8,128]{1,0:T(8,128)S(1)}, u32[]{:S(2)}, u32[]{:S(2)}) collective-permute-start(f32[8,128]{1,0:T(8,128)S(1)} %add.429), channel_id=1, source_target_pairs={{0,32},{4,36},{8,40},{12,44},{16,48},{20,52},{24,56},{28,60},{32,0... | collective-permute-start | bytes 12296 | tf_op jit(solution)/shard_map/ppermute | solution.py:35
  315.8 7.5 %collective-permute-start.10 = (f32[31,1024]{1,0:T(8,128)S(1)}, f32[31,1024]{1,0:T(8,128)S(1)}, u32[]{:S(2)}, u32[]{:S(2)}) collective-permute-start(f32[31,1024]{1,0:T(8,128)S(1)} %add.421), channel_id=1, source_target_pairs={{0,16},{4,20},{8,24},{12,28},{16,0},{20,4},{24,8},{28,12},{32,48},... | collective-permute-start | bytes 380936 | tf_op jit(solution)/shard_map/ppermute | solution.py:35
  320.2 5.1 %collective-permute-start.19 = (f32[8,128]{1,0:T(8,128)S(1)}, f32[8,128]{1,0:T(8,128)S(1)}, u32[]{:S(2)}, u32[]{:S(2)}) collective-permute-start(f32[8,128]{1,0:T(8,128)S(1)} %add.430), channel_id=1, source_target_pairs={{0,64},{4,68},{8,72},{12,76},{16,80},{20,84},{24,88},{28,92},{32,9... | collective-permute-start | bytes 12296 | tf_op jit(solution)/shard_map/ppermute | solution.py:35
  323.3 5.5 %collective-permute-start.11 = (f32[31,1024]{1,0:T(8,128)S(1)}, f32[31,1024]{1,0:T(8,128)S(1)}, u32[]{:S(2)}, u32[]{:S(2)}) collective-permute-start(f32[31,1024]{1,0:T(8,128)S(1)} %add.422), channel_id=1, source_target_pairs={{0,32},{4,36},{8,40},{12,44},{16,48},{20,52},{24,56},{28,60},{32,0... | collective-permute-start | bytes 380936 | tf_op jit(solution)/shard_map/ppermute | solution.py:35
  325.4 71.1 %collective-permute-start.20 = (f32[8,128]{1,0:T(8,128)S(1)}, f32[8,128]{1,0:T(8,128)S(1)}, u32[]{:S(2)}, u32[]{:S(2)}) collective-permute-start(f32[8,128]{1,0:T(8,128)S(1)} %add.431), channel_id=1, source_target_pairs={{0,1},{1,0},{2,3},{3,2},{4,5},{5,4},{6,7},{7,6},{8,9},{9,8},{10,11... | collective-permute-start | bytes 12296 | tf_op jit(solution)/shard_map/ppermute | solution.py:35
  328.8 70.9 %collective-permute-start.12 = (f32[31,1024]{1,0:T(8,128)S(1)}, f32[31,1024]{1,0:T(8,128)S(1)}, u32[]{:S(2)}, u32[]{:S(2)}) collective-permute-start(f32[31,1024]{1,0:T(8,128)S(1)} %add.423), channel_id=1, source_target_pairs={{0,64},{4,68},{8,72},{12,76},{16,80},{20,84},{24,88},{28,92},{32,9... | collective-permute-start | bytes 380936 | tf_op jit(solution)/shard_map/ppermute | solution.py:35
  396.5 10.0 %collective-permute-start.21 = (f32[8,128]{1,0:T(8,128)S(1)}, f32[8,128]{1,0:T(8,128)S(1)}, u32[]{:S(2)}, u32[]{:S(2)}) collective-permute-start(f32[8,128]{1,0:T(8,128)S(1)} %add.432), channel_id=1, source_target_pairs={{0,2},{1,3},{2,0},{3,1},{4,6},{5,7},{6,4},{7,5},{8,10},{9,11},{10,... | collective-permute-start | bytes 12296 | tf_op jit(solution)/shard_map/ppermute | solution.py:35
  399.7 5.2 %collective-permute-start.13 = (f32[31,1024]{1,0:T(8,128)S(1)}, f32[31,1024]{1,0:T(8,128)S(1)}, u32[]{:S(2)}, u32[]{:S(2)}) collective-permute-start(f32[31,1024]{1,0:T(8,128)S(1)} %add.424), channel_id=1, source_target_pairs={{0,1},{1,0},{2,3},{3,2},{4,5},{5,4},{6,7},{7,6},{8,9},{9,8},{10,11... | collective-permute-start | bytes 380936 | tf_op jit(solution)/shard_map/ppermute | solution.py:35
  400.4 23.4 %copy-start.1 = (bf16[1024,1024]{1,0:T(8,128)(2,1)S(1)}, bf16[1024,1024]{1,0:T(8,128)(2,1)}, u32[]{:S(2)}) copy-start(bf16[1024,1024]{1,0:T(8,128)(2,1)} %param.11) | copy-start | bytes 6291460
  404.9 8.0 %collective-permute-start.14 = (f32[31,1024]{1,0:T(8,128)S(1)}, f32[31,1024]{1,0:T(8,128)S(1)}, u32[]{:S(2)}, u32[]{:S(2)}) collective-permute-start(f32[31,1024]{1,0:T(8,128)S(1)} %add.425), channel_id=1, source_target_pairs={{0,2},{1,3},{2,0},{3,1},{4,6},{5,7},{6,4},{7,5},{8,10},{9,11},{10,... | collective-permute-start | bytes 380936 | tf_op jit(solution)/shard_map/ppermute | solution.py:35
  (67 other events, 651.9 us)
Sparse Core Ops, SparseCore 0:
  258.0 138.3 reduce-scatter.2
  398.8 22.1 reduce-scatter.4

commit v7 on v6

--- a/solution.py
+++ b/solution.py
@@ -124,7 +124,6 @@
             same_seg, kernel[tap_index] * padded[:, tap_index : tap_index + frames], 0.0
         )
     gated = jax.nn.sigmoid(conv_sum)
-    output = (hidden.astype(jnp.float32) + conv_sum * gated).astype(jnp.bfloat16)
     incoming = cotangent.astype(jnp.float32)
     grad_conv = incoming * gated * (1.0 + conv_sum * (1.0 - gated))
     grad_pad = with_halo(grad_conv.astype(jnp.bfloat16), (("seq", 1),), conv_reach).astype(
@@ -196,9 +195,12 @@
             ],
             axis=1,
         )
-    weight_partial, late_conv, late_padded = lax.optimization_barrier(
-        (weight_partial, grad_conv, padded)
-    )
+    weight_partial, late_conv, late_padded, late_hidden, late_sum = lax.optimization_barrier(
+        (weight_partial, grad_conv, padded, hidden, conv_sum)
+    )
+    output = (
+        late_hidden.astype(jnp.float32) + late_sum * jax.nn.sigmoid(late_sum)
+    ).astype(jnp.bfloat16)
     summed = staged_scatter(weight_partial)
     kernel_rows = []
     for tap_index in range(kernel.shape[0]):

time: 436 us -> 433 us (level)
  no operation moved by 1% of the time
where the time goes in v7:
time: 433 us; the launch traced here: 428 us
  other arithmetic  100 us (23%)
  matrix products  97.1 us (22%)
  waiting for transfers between devices  88.5 us (20%)
  starting transfers between devices  76 us (18%)
  local copies, waits for them, and re-layouts  50.4 us (12%)
  between operations  16.1 us (4%)
    reduce_scatter x1, waiting for transfers between devices, staged_scatter(): partial = lax.psum_scatter(partial, 'seq', scatter_dimension=0, tiled=True)  65.6 us
    ppermute x14, starting transfers between devices, exchange_sum(): lax.ppermute(value, axis, [(i, i ^ bit) for i in range(size)])  41.8 us
    ppermute x2, starting transfers between devices, with_halo(): before = lax.ppermute(last, axis, up)  19.2 us
    sub x1, matrix products, local(): exponent = jnp.where(allowed, jnp.exp(scores - row_max), 0.0)  17.3 us
    dot_general x1, matrix products, local(): jnp.einsum('bqhd,bkhd->bhqk', grad_heads, head_values, preferred_element_...  15 us
    convert_element_type x1, other arithmetic, local(): grad_conv.astype(jnp.bfloat16)  14.3 us
    unnamed x186, local copies, waits for them, and re-layouts  13.7 us
    convert_element_type x1, other arithmetic, local(): weights = attn_probs.astype(jnp.bfloat16)  13.3 us
  transfers between devices with their start and end apart: 24, of which 10 were waited for; matrix products, arithmetic and copies ran while one was open for 14% of the time, Pallas kernels for 0%

profile of v7, /device:TPU:0, one launch (start us, length us, event | category | flops | bytes accessed | tf_op | source)
XLA Modules:
  0.0 428.3 jit_solution(10855682895943374725)
XLA Ops:
  12.1 7.6 %convolution_convert_fusion = bf16[512,3072]{1,0:T(8,128)(2,1)} fusion(bf16[512,1024]{1,0:T(8,128)(2,1)S(1)} %bitcast.174, bf16[1024,3072]{1,0:T(8,128)(2,1)} %param.10), kind=kOutput, calls=%fused_computation.18 | convolution fusion | flops 3222798336 | bytes 10485760 | tf_op jit(solution)/shard_map/dot_general | solution.py:82
  19.7 8.6 %reshape.285 = bf16[2,256,3,16,64]{4,3,2,1,0:T(8,128)(2,1)} reshape(bf16[512,3072]{1,0:T(8,128)(2,1)} %convolution_convert_fusion) | data formatting | bytes 6291456 | tf_op jit(solution)/shard_map/reshape;reshape | solution.py:86
  28.3 4.9 %slice.779 = bf16[2,256,2,16,64]{4,3,2,1,0:T(8,128)(2,1)} slice(bf16[2,256,3,16,64]{4,3,2,1,0:T(8,128)(2,1)} %reshape.285), slice={[0:2], [0:256], [1:3], [0:16], [0:64]} | slice | bytes 4194304 | tf_op jit(solution)/shard_map/slice | solution.py:88
  33.2 5.8 %copy.56 = bf16[2,256,2,16,64]{1,4,3,0,2:T(8,128)(2,1)} copy(bf16[2,256,2,16,64]{4,3,2,1,0:T(8,128)(2,1)} %slice.779) | data formatting | bytes 4194304
  39.1 2.7 collective-permute-start
  43.2 3.4 slice.781
  47.2 3.6 copy.57
  57.6 5.9 %pad_maximum_fusion.2 = bf16[2,768,2,16,64]{1,4,3,0,2:T(8,128)(2,1)} fusion(bf16[2,256,2,16,64]{1,4,3,0,2:T(8,128)(2,1)} %collective-permute-done.1, bf16[2,256,2,16,64]{1,4,3,0,2:T(8,128)(2,1)} %copy.56, bf16[2,256,2,16,64]{1,4,3,0,2:T(8,128)(2,1)} %collective-permute-done), kind=kLoop, calls=%fused_computation.15 | loop fusion | flops 18874368 | bytes 12582912 | tf_op jit(solution)/shard_map/concatenate | solution.py:89
  63.5 17.3 %fusion.241 = (f32[2,16,256]{2,1,0:T(8,128)}, f32[2,16,256,768]{3,2,1,0:T(8,128)}) fusion(pred[2,256,768]{2,1,0:T(8,128)(4,1)S(1)} %broadcast_compare_fusion, bf16[2,768,2,16,64]{1,4,3,0,2:T(8,128)(2,1)} %pad_maximum_fusion.2, bf16[2,256,1,16,64]{1,4,3,0,2:T(8,128)(2,1)} %copy.57), kind=kOutput, calls=%fused_computation.445 | convolution fusion | flops 836764416 | bytes 30179328 | tf_op jit(solution)/shard_map/sub | solution.py:105
  80.8 13.3 %fusion.6 = bf16[2,16,256,768]{3,2,1,0:T(8,128)(2,1)} fusion(f32[2,16,256,768]{3,2,1,0:T(8,128)} %get-tuple-element.132, f32[2,16,256]{2,1,0:T(8,128)} %get-tuple-element.131), kind=kLoop, calls=%fused_computation.14 | loop fusion | flops 12582912 | bytes 37781504 | tf_op jit(solution)/shard_map/convert_element_type | solution.py:107
  94.2 9.4 %fusion.159 = bf16[2,16,64,256]{3,2,1,0:T(8,128)(2,1)S(1)} fusion(bf16[2,16,256,768]{3,2,1,0:T(8,128)(2,1)} %fusion.6, bf16[2,768,2,16,64]{1,4,3,0,2:T(8,128)(2,1)} %pad_maximum_fusion.2), kind=kOutput, calls=%fused_computation.275 | convolution fusion | flops 805830656 | bytes 16777216 | tf_op jit(solution)/shard_map/bhqk,bkhd->bqhd/dot_general | solution.py:108
  105.3 14.9 %collective-permute-start.2 = (bf16[2,15,1024]{2,1,0:T(8,128)(2,1)S(1)}, bf16[2,15,1024]{2,1,0:T(8,128)(2,1)S(1)}, u32[]{:S(2)}, u32[]{:S(2)}) collective-permute-start(bf16[2,15,1024]{2,1,0:T(8,128)(2,1)S(1)} %get-tuple-element.65), channel_id=1, source_target_pairs={{0,4},{4,8},{8,12},{12,16},{16,20},{20,24},{24,28},{28,32},{32,36}... | collective-permute-start | bytes 184328 | tf_op jit(solution)/shard_map/ppermute | solution.py:21
  124.1 14.3 %fusion.233 = (bf16[2,256,1024]{2,1,0:T(8,128)(2,1)S(1)}, f32[2,256,1024]{2,1,0:T(8,128)}, f32[2,256,1024]{2,1,0:T(8,128)}) fusion(bf16[2,256,1024]{2,1,0:T(8,128)(2,1)S(1)} %copy-done.10, f32[2,286,1024]{2,1,0:T(8,128)S(1)} %maximum_convert_fusion, f32[1024]{0:T(1024)S(1)} %bitcast.197, pred[2,256]{1,0:T(4,128)(4,1)S(1)} %copy-done.57, ...), kind=kLoop, calls=%fused_computation.439 | loop fusion | flops 53477376 | bytes 71446016 | tf_op jit(solution)/shard_map/convert_element_type | solution.py:129
  138.6 4.4 %collective-permute-start.4 = (bf16[2,15,1024]{2,1,0:T(8,128)(2,1)S(1)}, bf16[2,15,1024]{2,1,0:T(8,128)(2,1)S(1)}, u32[]{:S(2)}, u32[]{:S(2)}) collective-permute-start(bf16[2,15,1024]{2,1,0:T(8,128)(2,1)S(1)} %get-tuple-element.63), channel_id=1, source_target_pairs={{0,4},{4,8},{8,12},{12,16},{16,20},{20,24},{24,28},{28,32},{32,36}... | collective-permute-start | bytes 184328 | tf_op jit(solution)/shard_map/ppermute | solution.py:21
  146.7 12.5 %fusion.231 = (bf16[2,256,1024]{2,1,0:T(8,128)(2,1)S(1)}, f32[2,256,1024]{2,1,0:T(8,128)}) fusion(f32[2,286,1024]{2,1,0:T(8,128)S(1)} %maximum_convert_fusion.1, f32[1024]{0:T(1024)S(1)} %bitcast.198, pred[2,256]{1,0:T(4,128)(4,1)S(1)} %copy-done.53, f32[1024]{0:T(1024)S(1)} %bitcast.200, pred[2,256]{1,0:T(4,128)(4,1)S(1)} %copy-done.54, ...), kind=kLoop, calls=%fused_computation.438 | loop fusion | flops 49807360 | bytes 69348864 | tf_op jit(solution)/shard_map/convert_element_type | solution.py:139
  160.2 2.3 convolution_convert_fusion.1
  162.5 4.0 reshape.286
  166.5 2.8 copy.41
  169.3 9.5 %convolution_bitcast_fusion = f32[2,768,1,16,64]{1,4,3,0,2:T(8,128)} fusion(bf16[2,256,16,64]{1,3,2,0:T(8,128)(2,1)S(1)} %copy.41, bf16[2,16,256,768]{3,2,1,0:T(8,128)(2,1)} %fusion.6), kind=kOutput, calls=%fused_computation.31 | convolution fusion | flops 805306368 | bytes 19922944 | tf_op jit(solution)/shard_map/bhqk,bqhd->bkhd/dot_general | solution.py:148
  179.6 15.0 %multiply_convert_fusion = bf16[2,16,256,768]{3,2,1,0:T(8,128)(2,1)} fusion(f32[2,16,256]{2,1,0:T(8,128)S(1)} %bitcast.239, f32[2,16,256,768]{3,2,1,0:T(8,128)} %get-tuple-element.132, f32[2,16,256]{2,1,0:T(8,128)S(1)} %copy-done.50, bf16[2,256,16,64]{1,3,2,0:T(8,128)(2,1)S(1)} %copy.41, bf16[2,768,2,16,64]{1,4,3,0,2:T(8,128)(2,1)} %pad_maximum_fusion.2), kind=kOutput, calls=%fused_computation.1 | convolution fusion | flops 836763648 | bytes 42008576 | tf_op jit(solution)/shard_map/bqhd,bkhd->bhqk/dot_general | solution.py:151
  194.6 9.9 %convolution_bitcast_fusion.1 = f32[2,768,1,16,64]{1,4,3,0,2:T(8,128)} fusion(bf16[2,16,256,768]{3,2,1,0:T(8,128)(2,1)} %multiply_convert_fusion, bf16[2,256,1,16,64]{1,4,3,0,2:T(8,128)(2,1)} %copy.57), kind=kOutput, calls=%fused_computation.32 | convolution fusion | flops 805306368 | bytes 19922944 | tf_op jit(solution)/shard_map/bhqk,bqhd->bkhd/dot_general | solution.py:158
  204.5 8.2 %fusion.2 = bf16[2,768,2,16,64]{1,4,3,0,2:T(8,128)(2,1)} fusion(f32[2,768,1,16,64]{1,4,3,0,2:T(8,128)} %convolution_bitcast_fusion, f32[2,768,1,16,64]{1,4,3,0,2:T(8,128)} %convolution_bitcast_fusion.1), kind=kLoop, calls=%fused_computation.9 | loop fusion | flops 3145728 | bytes 18874368 | tf_op jit(solution)/shard_map/convert.1
  212.7 4.8 %fusion.236 = (bf16[2,256,2,16,64]{1,4,3,0,2:T(8,128)(2,1)}, bf16[2,256,2,16,64]{1,4,3,0,2:T(8,128)(2,1)}) fusion(bf16[2,768,2,16,64]{1,4,3,0,2:T(8,128)(2,1)} %fusion.2), kind=kLoop, calls=%fused_computation.440 | loop fusion | bytes 8388608 | tf_op jit(solution)/shard_map/slice | solution.py:164
  218.8 6.4 %collective-permute-start.7 = (bf16[2,256,2,16,64]{1,4,3,0,2:T(8,128)(2,1)}, bf16[2,256,2,16,64]{1,4,3,0,2:T(8,128)(2,1)}, u32[]{:S(2)}, u32[]{:S(2)}) collective-permute-start(bf16[2,256,2,16,64]{1,4,3,0,2:T(8,128)(2,1)} %get-tuple-element.62), channel_id=1, source_target_pairs={{0,4},{4,8},{8,12},{12,16},{16,20},{20,24},{24,28},{28,32},{32,36}... | collective-permute-start | bytes 6291464 | tf_op jit(solution)/shard_map/ppermute | solution.py:58
  226.5 3.3 fusion.247
  229.8 9.4 %fusion.162 = bf16[2,256,1,16,64]{1,4,3,0,2:T(8,128)(2,1)S(1)} fusion(bf16[2,16,256,768]{3,2,1,0:T(8,128)(2,1)} %multiply_convert_fusion, bf16[2,768,2,16,64]{1,4,3,0,2:T(8,128)(2,1)} %pad_maximum_fusion.2), kind=kOutput, calls=%fused_computation.276 | convolution fusion | flops 805830656 | bytes 16777216 | tf_op jit(solution)/shard_map/bhqk,bkhd->bqhd/dot_general | solution.py:155
  239.3 4.0 fusion.12
  243.6 3.3 copy.44
  248.1 3.7 fusion.246
  251.9 6.0 %pad_maximum_fusion = f32[1024,4096]{1,0:T(8,128)} fusion(f32[1024,1024]{1,0:T(8,128)S(1)} %copy-done.11, f32[1024,3072]{1,0:T(8,128)S(1)} %fusion.246), kind=kLoop, calls=%fused_computation.5 | loop fusion | flops 4194304 | bytes 33554432 | tf_op jit(solution)/shard_map/concatenate | solution.py:184
  258.0 2.1 copy.47
  260.1 8.3 %fusion.30 = (f32[1024]{0:T(1024)S(1)}, f32[2,256]{1,0:T(2,128)S(1)}, f32[2,256]{1,0:T(2,128)S(1)}, f32[2,256,1024]{2,1,0:T(8,128)}) fusion(bf16[2,256,1024]{2,1,0:T(8,128)(2,1)S(1)} %copy-done.6, f32[2,256]{1,0:T(2,128)S(1)} %copy-done.52, f32[2,256]{1,0:T(2,128)S(1)} %copy-done.49, f32[1024]{0:T(1024)S(1)} %copy-done.89, ...), kind=kOutput, calls=%fused_computation.49 | convolution fusion | flops 3225942016 | bytes 12599296 | tf_op jit(solution)/shard_map/dot_general | solution.py:174
  268.5 9.5 %collective-permute-start.15 = (f32[8,128]{1,0:T(8,128)S(1)}, f32[8,128]{1,0:T(8,128)S(1)}, u32[]{:S(2)}, u32[]{:S(2)}) collective-permute-start(f32[8,128]{1,0:T(8,128)S(1)} %bitcast.244), channel_id=1, source_target_pairs={{0,4},{4,0},{8,12},{12,8},{16,20},{20,16},{24,28},{28,24},{32,36},... | collective-permute-start | bytes 12296 | tf_op jit(solution)/shard_map/ppermute | solution.py:35
  278.0 3.9 select_reduce_fusion.18
  281.9 3.8 select_reduce_fusion.9
  285.7 3.9 select_reduce_fusion
  291.4 2.9 collective-permute-start.16
  295.9 9.6 %collective-permute-start.17 = (f32[8,128]{1,0:T(8,128)S(1)}, f32[8,128]{1,0:T(8,128)S(1)}, u32[]{:S(2)}, u32[]{:S(2)}) collective-permute-start(f32[8,128]{1,0:T(8,128)S(1)} %fusion.264), channel_id=1, source_target_pairs={{0,16},{4,20},{8,24},{12,28},{16,0},{20,4},{24,8},{28,12},{32,48},... | collective-permute-start | bytes 12296 | tf_op jit(solution)/shard_map/ppermute | solution.py:35
  305.5 3.5 collective-permute-done.17
  309.0 4.4 %collective-permute-start.18 = (f32[8,128]{1,0:T(8,128)S(1)}, f32[8,128]{1,0:T(8,128)S(1)}, u32[]{:S(2)}, u32[]{:S(2)}) collective-permute-start(f32[8,128]{1,0:T(8,128)S(1)} %add.433), channel_id=1, source_target_pairs={{0,32},{4,36},{8,40},{12,44},{16,48},{20,52},{24,56},{28,60},{32,0... | collective-permute-start | bytes 12296 | tf_op jit(solution)/shard_map/ppermute | solution.py:35
  314.0 3.9 add_convert_fusion
  317.9 2.7 collective-permute-start.19
  325.8 2.5 collective-permute-start.12
  328.4 65.6 %reduce-scatter.3.cloned.1.call-done = f32[32,4096]{1,0:T(8,128)} async-done(((f32[1024,4096]{1,0:T(8,128)}), f32[32,4096]{1,0:T(8,128)}) %reduce-scatter.3.cloned.1.call-update) | async-done | bytes 524304 | tf_op jit(solution)/shard_map/reduce_scatter | solution.py:41
  394.0 3.1 collective-permute-start.21
  398.0 4.1 fusion.29
  404.7 5.6 %collective-permute-done.14 = f32[31,1024]{1,0:T(8,128)S(1)} collective-permute-done((f32[31,1024]{1,0:T(8,128)S(1)}, f32[31,1024]{1,0:T(8,128)S(1)}, u32[]{:S(2)}, u32[]{:S(2)}) %collective-permute-start.14) | collective-permute-done | bytes 127008 | tf_op jit(solution)/shard_map/ppermute | solution.py:35
  410.9 7.4 %reduce-scatter.5.cloned.1.call-done = f32[8,4096]{1,0:T(8,128)} async-done(((f32[32,4096]{1,0:T(8,128)}), f32[8,4096]{1,0:T(8,128)}) %reduce-scatter.5.cloned.1.call-update) | async-done | bytes 131088 | tf_op jit(solution)/shard_map/reduce_scatter | solution.py:42
  (281 shorter events, 44.3 us)
Async XLA Ops:
  7.2 96.4 %copy-start = (bf16[1024,1024]{1,0:T(8,128)(2,1)S(1)}, bf16[1024,1024]{1,0:T(8,128)(2,1)}, u32[]{:S(2)}) copy-start(bf16[1024,1024]{1,0:T(8,128)(2,1)} %param.11) | copy-start | bytes 6291460
  7.2 386.8 %reduce-scatter.3.cloned.1.call-start = ((), (), s32[]{:S(2)}) async-start(), calls=%async_computation.2 | async-start | bytes 17301504 | tf_op jit(solution)/shard_map/reduce_scatter | solution.py:41
  39.1 18.5 %collective-permute-start = (bf16[2,256,2,16,64]{1,4,3,0,2:T(8,128)(2,1)}, bf16[2,256,2,16,64]{1,4,3,0,2:T(8,128)(2,1)}, u32[]{:S(2)}, u32[]{:S(2)}) collective-permute-start(bf16[2,256,2,16,64]{1,4,3,0,2:T(8,128)(2,1)} %copy.56), channel_id=1, source_target_pairs={{0,4},{4,8},{8,12},{12,16},{16,20},{20,24},{24,28},{28,32},{32,36}... | collective-permute-start | bytes 6291464 | tf_op jit(solution)/shard_map/ppermute | solution.py:58
  41.7 15.9 %collective-permute-start.1 = (bf16[2,256,2,16,64]{1,4,3,0,2:T(8,128)(2,1)}, bf16[2,256,2,16,64]{1,4,3,0,2:T(8,128)(2,1)}, u32[]{:S(2)}, u32[]{:S(2)}) collective-permute-start(bf16[2,256,2,16,64]{1,4,3,0,2:T(8,128)(2,1)} %copy.56), channel_id=1, source_target_pairs={{4,0},{8,4},{12,8},{16,12},{20,16},{24,20},{28,24},{32,28},{36,32}... | collective-permute-start | bytes 6291464 | tf_op jit(solution)/shard_map/ppermute | solution.py:58
  104.9 33.5 %copy-start.9 = (bf16[2,256,1024]{2,1,0:T(8,128)(2,1)}, bf16[2,256,1024]{2,1,0:T(8,128)(2,1)S(1)}, u32[]{:S(2)}) copy-start(bf16[2,256,1024]{2,1,0:T(8,128)(2,1)S(1)} %fusion.58) | copy-start | bytes 3145732
  104.9 18.8 %copy-start.10 = (bf16[2,256,1024]{2,1,0:T(8,128)(2,1)S(1)}, bf16[2,256,1024]{2,1,0:T(8,128)(2,1)}, u32[]{:S(2)}) copy-start(bf16[2,256,1024]{2,1,0:T(8,128)(2,1)} %param.13) | copy-start | bytes 3145732
  104.9 18.8 %copy-start.17 = (f32[1,1024]{1,0:T(1,128)S(1)}, f32[1,1024]{1,0:T(1,128)}, u32[]{:S(2)}) copy-start(f32[1,1024]{1,0:T(1,128)} %get-tuple-element.86) | copy-start | bytes 12292
  104.9 18.8 %copy-start.18 = (f32[1,1024]{1,0:T(1,128)S(1)}, f32[1,1024]{1,0:T(1,128)}, u32[]{:S(2)}) copy-start(f32[1,1024]{1,0:T(1,128)} %get-tuple-element.87) | copy-start | bytes 12292
  104.9 18.8 %copy-start.19 = (f32[1,1024]{1,0:T(1,128)S(1)}, f32[1,1024]{1,0:T(1,128)}, u32[]{:S(2)}) copy-start(f32[1,1024]{1,0:T(1,128)} %get-tuple-element.88) | copy-start | bytes 12292
  104.9 18.8 %copy-start.20 = (f32[1,1024]{1,0:T(1,128)S(1)}, f32[1,1024]{1,0:T(1,128)}, u32[]{:S(2)}) copy-start(f32[1,1024]{1,0:T(1,128)} %get-tuple-element.89) | copy-start | bytes 12292
  105.0 18.8 %copy-start.21 = (f32[1,1024]{1,0:T(1,128)S(1)}, f32[1,1024]{1,0:T(1,128)}, u32[]{:S(2)}) copy-start(f32[1,1024]{1,0:T(1,128)} %get-tuple-element.90) | copy-start | bytes 12292
  105.0 18.8 %copy-start.22 = (f32[1,1024]{1,0:T(1,128)S(1)}, f32[1,1024]{1,0:T(1,128)}, u32[]{:S(2)}) copy-start(f32[1,1024]{1,0:T(1,128)} %get-tuple-element.91) | copy-start | bytes 12292
  105.0 18.8 %copy-start.23 = (f32[1,1024]{1,0:T(1,128)S(1)}, f32[1,1024]{1,0:T(1,128)}, u32[]{:S(2)}) copy-start(f32[1,1024]{1,0:T(1,128)} %get-tuple-element.92) | copy-start | bytes 12292
  105.0 18.8 %copy-start.24 = (f32[1,1024]{1,0:T(1,128)S(1)}, f32[1,1024]{1,0:T(1,128)}, u32[]{:S(2)}) copy-start(f32[1,1024]{1,0:T(1,128)} %get-tuple-element.93) | copy-start | bytes 12292
  105.0 18.8 %copy-start.25 = (f32[1,1024]{1,0:T(1,128)S(1)}, f32[1,1024]{1,0:T(1,128)}, u32[]{:S(2)}) copy-start(f32[1,1024]{1,0:T(1,128)} %get-tuple-element.94) | copy-start | bytes 12292
  105.0 18.8 %copy-start.26 = (f32[1,1024]{1,0:T(1,128)S(1)}, f32[1,1024]{1,0:T(1,128)}, u32[]{:S(2)}) copy-start(f32[1,1024]{1,0:T(1,128)} %get-tuple-element.95) | copy-start | bytes 12292
  105.0 18.8 %copy-start.27 = (f32[1,1024]{1,0:T(1,128)S(1)}, f32[1,1024]{1,0:T(1,128)}, u32[]{:S(2)}) copy-start(f32[1,1024]{1,0:T(1,128)} %get-tuple-element.96) | copy-start | bytes 12292
  105.0 18.8 %copy-start.28 = (f32[1,1024]{1,0:T(1,128)S(1)}, f32[1,1024]{1,0:T(1,128)}, u32[]{:S(2)}) copy-start(f32[1,1024]{1,0:T(1,128)} %get-tuple-element.97) | copy-start | bytes 12292
  105.0 18.8 %copy-start.29 = (f32[1,1024]{1,0:T(1,128)S(1)}, f32[1,1024]{1,0:T(1,128)}, u32[]{:S(2)}) copy-start(f32[1,1024]{1,0:T(1,128)} %get-tuple-element.67) | copy-start | bytes 12292
  105.0 18.8 %copy-start.30 = (f32[1,1024]{1,0:T(1,128)S(1)}, f32[1,1024]{1,0:T(1,128)}, u32[]{:S(2)}) copy-start(f32[1,1024]{1,0:T(1,128)} %get-tuple-element.68) | copy-start | bytes 12292
  105.1 18.8 %copy-start.31 = (f32[1,1024]{1,0:T(1,128)S(1)}, f32[1,1024]{1,0:T(1,128)}, u32[]{:S(2)}) copy-start(f32[1,1024]{1,0:T(1,128)} %get-tuple-element.69) | copy-start | bytes 12292
  105.1 18.8 %copy-start.32 = (f32[1,1024]{1,0:T(1,128)S(1)}, f32[1,1024]{1,0:T(1,128)}, u32[]{:S(2)}) copy-start(f32[1,1024]{1,0:T(1,128)} %get-tuple-element.70) | copy-start | bytes 12292
  105.1 18.8 %copy-start.33 = (f32[1,1024]{1,0:T(1,128)S(1)}, f32[1,1024]{1,0:T(1,128)}, u32[]{:S(2)}) copy-start(f32[1,1024]{1,0:T(1,128)} %get-tuple-element.71) | copy-start | bytes 12292
  105.3 16.7 %collective-permute-start.2 = (bf16[2,15,1024]{2,1,0:T(8,128)(2,1)S(1)}, bf16[2,15,1024]{2,1,0:T(8,128)(2,1)S(1)}, u32[]{:S(2)}, u32[]{:S(2)}) collective-permute-start(bf16[2,15,1024]{2,1,0:T(8,128)(2,1)S(1)} %get-tuple-element.65), channel_id=1, source_target_pairs={{0,4},{4,8},{8,12},{12,16},{16,20},{20,24},{24,28},{28,32},{32,36}... | collective-permute-start | bytes 184328 | tf_op jit(solution)/shard_map/ppermute | solution.py:21
  120.2 3.1 collective-permute-start.3
  122.0 24.5 %copy-start.82 = (pred[2,256]{1,0:T(4,128)(4,1)}, pred[2,256]{1,0:T(4,128)(4,1)S(1)}, u32[]{:S(2)}) copy-start(pred[2,256]{1,0:T(4,128)(4,1)S(1)} %get-tuple-element.126) | copy-start | bytes 1540
  122.0 24.5 %copy-start.84 = (pred[2,256]{1,0:T(4,128)(4,1)}, pred[2,256]{1,0:T(4,128)(4,1)S(1)}, u32[]{:S(2)}) copy-start(pred[2,256]{1,0:T(4,128)(4,1)S(1)} %get-tuple-element.127) | copy-start | bytes 1540
  122.0 24.5 %copy-start.86 = (pred[2,256]{1,0:T(4,128)(4,1)}, pred[2,256]{1,0:T(4,128)(4,1)S(1)}, u32[]{:S(2)}) copy-start(pred[2,256]{1,0:T(4,128)(4,1)S(1)} %get-tuple-element.128) | copy-start | bytes 1540
  138.6 5.7 %collective-permute-start.4 = (bf16[2,15,1024]{2,1,0:T(8,128)(2,1)S(1)}, bf16[2,15,1024]{2,1,0:T(8,128)(2,1)S(1)}, u32[]{:S(2)}, u32[]{:S(2)}) collective-permute-start(bf16[2,15,1024]{2,1,0:T(8,128)(2,1)S(1)} %get-tuple-element.63), channel_id=1, source_target_pairs={{0,4},{4,8},{8,12},{12,16},{16,20},{20,24},{24,28},{28,32},{32,36}... | collective-permute-start | bytes 184328 | tf_op jit(solution)/shard_map/ppermute | solution.py:21
  143.0 3.1 collective-permute-start.5
  217.5 21.8 %collective-permute-start.6 = (bf16[2,256,2,16,64]{1,4,3,0,2:T(8,128)(2,1)}, bf16[2,256,2,16,64]{1,4,3,0,2:T(8,128)(2,1)S(1)}, u32[]{:S(2)}, u32[]{:S(2)}) collective-permute-start(bf16[2,256,2,16,64]{1,4,3,0,2:T(8,128)(2,1)} %get-tuple-element.61), channel_id=1, source_target_pairs={{4,0},{8,4},{12,8},{16,12},{20,16},{24,20},{28,24},{32,28},{36,32}... | collective-permute-start | bytes 6291464 | tf_op jit(solution)/shard_map/ppermute | solution.py:58
  218.8 20.5 %collective-permute-start.7 = (bf16[2,256,2,16,64]{1,4,3,0,2:T(8,128)(2,1)}, bf16[2,256,2,16,64]{1,4,3,0,2:T(8,128)(2,1)}, u32[]{:S(2)}, u32[]{:S(2)}) collective-permute-start(bf16[2,256,2,16,64]{1,4,3,0,2:T(8,128)(2,1)} %get-tuple-element.62), channel_id=1, source_target_pairs={{0,4},{4,8},{8,12},{12,16},{16,20},{20,24},{24,28},{28,32},{32,36}... | collective-permute-start | bytes 6291464 | tf_op jit(solution)/shard_map/ppermute | solution.py:58
  257.9 160.4 %reduce-scatter.5.cloned.1.call-start = ((), (), s32[]{:S(2)}) async-start(), calls=%async_computation.3 | async-start | bytes 655360 | tf_op jit(solution)/shard_map/reduce_scatter | solution.py:42
  268.5 22.9 %collective-permute-start.15 = (f32[8,128]{1,0:T(8,128)S(1)}, f32[8,128]{1,0:T(8,128)S(1)}, u32[]{:S(2)}, u32[]{:S(2)}) collective-permute-start(f32[8,128]{1,0:T(8,128)S(1)} %bitcast.244), channel_id=1, source_target_pairs={{0,4},{4,0},{8,12},{12,8},{16,20},{20,16},{24,28},{28,24},{32,36},... | collective-permute-start | bytes 12296 | tf_op jit(solution)/shard_map/ppermute | solution.py:35
  291.3 3.0 collective-permute-start.8
  291.4 4.5 %collective-permute-start.16 = (f32[8,128]{1,0:T(8,128)S(1)}, f32[8,128]{1,0:T(8,128)S(1)}, u32[]{:S(2)}, u32[]{:S(2)}) collective-permute-start(f32[8,128]{1,0:T(8,128)S(1)} %bitcast_add_fusion), channel_id=1, source_target_pairs={{0,8},{4,12},{8,0},{12,4},{16,24},{20,28},{24,16},{28,20},{32,40},... | collective-permute-start | bytes 12296 | tf_op jit(solution)/shard_map/ppermute | solution.py:35
  294.3 19.1 %collective-permute-start.9 = (f32[31,1024]{1,0:T(8,128)S(1)}, f32[31,1024]{1,0:T(8,128)S(1)}, u32[]{:S(2)}, u32[]{:S(2)}) collective-permute-start(f32[31,1024]{1,0:T(8,128)S(1)} %add.424), channel_id=1, source_target_pairs={{0,8},{4,12},{8,0},{12,4},{16,24},{20,28},{24,16},{28,20},{32,40},... | collective-permute-start | bytes 380936 | tf_op jit(solution)/shard_map/ppermute | solution.py:35
  295.9 13.1 %collective-permute-start.17 = (f32[8,128]{1,0:T(8,128)S(1)}, f32[8,128]{1,0:T(8,128)S(1)}, u32[]{:S(2)}, u32[]{:S(2)}) collective-permute-start(f32[8,128]{1,0:T(8,128)S(1)} %fusion.264), channel_id=1, source_target_pairs={{0,16},{4,20},{8,24},{12,28},{16,0},{20,4},{24,8},{28,12},{32,48},... | collective-permute-start | bytes 12296 | tf_op jit(solution)/shard_map/ppermute | solution.py:35
  309.0 8.8 %collective-permute-start.18 = (f32[8,128]{1,0:T(8,128)S(1)}, f32[8,128]{1,0:T(8,128)S(1)}, u32[]{:S(2)}, u32[]{:S(2)}) collective-permute-start(f32[8,128]{1,0:T(8,128)S(1)} %add.433), channel_id=1, source_target_pairs={{0,32},{4,36},{8,40},{12,44},{16,48},{20,52},{24,56},{28,60},{32,0... | collective-permute-start | bytes 12296 | tf_op jit(solution)/shard_map/ppermute | solution.py:35
  313.4 7.2 %collective-permute-start.10 = (f32[31,1024]{1,0:T(8,128)S(1)}, f32[31,1024]{1,0:T(8,128)S(1)}, u32[]{:S(2)}, u32[]{:S(2)}) collective-permute-start(f32[31,1024]{1,0:T(8,128)S(1)} %add.425), channel_id=1, source_target_pairs={{0,16},{4,20},{8,24},{12,28},{16,0},{20,4},{24,8},{28,12},{32,48},... | collective-permute-start | bytes 380936 | tf_op jit(solution)/shard_map/ppermute | solution.py:35
  317.9 5.1 %collective-permute-start.19 = (f32[8,128]{1,0:T(8,128)S(1)}, f32[8,128]{1,0:T(8,128)S(1)}, u32[]{:S(2)}, u32[]{:S(2)}) collective-permute-start(f32[8,128]{1,0:T(8,128)S(1)} %add.434), channel_id=1, source_target_pairs={{0,64},{4,68},{8,72},{12,76},{16,80},{20,84},{24,88},{28,92},{32,9... | collective-permute-start | bytes 12296 | tf_op jit(solution)/shard_map/ppermute | solution.py:35
  320.7 5.2 %collective-permute-start.11 = (f32[31,1024]{1,0:T(8,128)S(1)}, f32[31,1024]{1,0:T(8,128)S(1)}, u32[]{:S(2)}, u32[]{:S(2)}) collective-permute-start(f32[31,1024]{1,0:T(8,128)S(1)} %add.426), channel_id=1, source_target_pairs={{0,32},{4,36},{8,40},{12,44},{16,48},{20,52},{24,56},{28,60},{32,0... | collective-permute-start | bytes 380936 | tf_op jit(solution)/shard_map/ppermute | solution.py:35
  323.0 71.0 %collective-permute-start.20 = (f32[8,128]{1,0:T(8,128)S(1)}, f32[8,128]{1,0:T(8,128)S(1)}, u32[]{:S(2)}, u32[]{:S(2)}) collective-permute-start(f32[8,128]{1,0:T(8,128)S(1)} %add.435), channel_id=1, source_target_pairs={{0,1},{1,0},{2,3},{3,2},{4,5},{5,4},{6,7},{7,6},{8,9},{9,8},{10,11... | collective-permute-start | bytes 12296 | tf_op jit(solution)/shard_map/ppermute | solution.py:35
  325.8 71.3 %collective-permute-start.12 = (f32[31,1024]{1,0:T(8,128)S(1)}, f32[31,1024]{1,0:T(8,128)S(1)}, u32[]{:S(2)}, u32[]{:S(2)}) collective-permute-start(f32[31,1024]{1,0:T(8,128)S(1)} %add.427), channel_id=1, source_target_pairs={{0,64},{4,68},{8,72},{12,76},{16,80},{20,84},{24,88},{28,92},{32,9... | collective-permute-start | bytes 380936 | tf_op jit(solution)/shard_map/ppermute | solution.py:35
  394.0 10.1 %collective-permute-start.21 = (f32[8,128]{1,0:T(8,128)S(1)}, f32[8,128]{1,0:T(8,128)S(1)}, u32[]{:S(2)}, u32[]{:S(2)}) collective-permute-start(f32[8,128]{1,0:T(8,128)S(1)} %add.436), channel_id=1, source_target_pairs={{0,2},{1,3},{2,0},{3,1},{4,6},{5,7},{6,4},{7,5},{8,10},{9,11},{10,... | collective-permute-start | bytes 12296 | tf_op jit(solution)/shard_map/ppermute | solution.py:35
  397.2 5.1 %collective-permute-start.13 = (f32[31,1024]{1,0:T(8,128)S(1)}, f32[31,1024]{1,0:T(8,128)S(1)}, u32[]{:S(2)}, u32[]{:S(2)}) collective-permute-start(f32[31,1024]{1,0:T(8,128)S(1)} %add.428), channel_id=1, source_target_pairs={{0,1},{1,0},{2,3},{3,2},{4,5},{5,4},{6,7},{7,6},{8,9},{9,8},{10,11... | collective-permute-start | bytes 380936 | tf_op jit(solution)/shard_map/ppermute | solution.py:35
  398.0 23.2 %copy-start.1 = (bf16[1024,1024]{1,0:T(8,128)(2,1)S(1)}, bf16[1024,1024]{1,0:T(8,128)(2,1)}, u32[]{:S(2)}) copy-start(bf16[1024,1024]{1,0:T(8,128)(2,1)} %param.11) | copy-start | bytes 6291460
  402.3 8.0 %collective-permute-start.14 = (f32[31,1024]{1,0:T(8,128)S(1)}, f32[31,1024]{1,0:T(8,128)S(1)}, u32[]{:S(2)}, u32[]{:S(2)}) collective-permute-start(f32[31,1024]{1,0:T(8,128)S(1)} %add.429), channel_id=1, source_target_pairs={{0,2},{1,3},{2,0},{3,1},{4,6},{5,7},{6,4},{7,5},{8,10},{9,11},{10,... | collective-permute-start | bytes 380936 | tf_op jit(solution)/shard_map/ppermute | solution.py:35
  (67 other events, 693.5 us)
Sparse Core Ops, SparseCore 0:
  258.0 135.8 reduce-scatter.2
  396.3 21.9 reduce-scatter.4
